TPU v7x, 128 devices: a whole 4x4x4 slice. The times are simulated.
128 devices in a mesh: seq: 32 (over x, z, core), tp: 4 (over y).
Axes of the slice: x: 4, y: 4, z: 4, core: 2. Of those that a mesh axis runs over, the one named last changes fastest.
Arguments:
- x_long: bfloat16 [16384, 4096], P('seq', 'tp'), may hold values from -6 to 6
- bc_long: bfloat16 [16384, 2, 512], P('seq', None, 'tp'), may hold values from -6 to 6
- z_long: bfloat16 [16384, 4096], P('seq', 'tp'), may hold values from -6 to 6
- dt_long: bfloat16 [64, 16384], P('tp', 'seq'), may hold values from -2.5 to 13
- x_short: bfloat16 [64, 16, 4096], P('seq', None, 'tp'), may hold values from -6 to 6
- bc_short: bfloat16 [64, 16, 2, 512], P('seq', None, None, 'tp'), may hold values from -6 to 6
- z_short: bfloat16 [64, 16, 4096], P('seq', None, 'tp'), may hold values from -6 to 6
- dt_short: bfloat16 [64, 64, 16], P('tp', 'seq'), may hold values from -3 to 3
- lengths: int32 [64], P('seq'), may hold values from 1 to 16, as said below
- conv_x: float32 [4, 4096], P(None, 'tp'), may hold values from -3 to 3
- conv_bc: float32 [4, 2, 512], P(None, None, 'tp'), may hold values from -3 to 3
- conv_bias_x: float32 [4096], P('tp'), may hold values from -0.5 to 0.5
- conv_bias_bc: float32 [2, 512], P(None, 'tp'), may hold values from -0.5 to 0.5
- dt_bias: float32 [64], P('tp'), may hold values from -9.5 to -1.5
- a_log: float32 [64], P('tp'), may hold values from -1.2 to -0.5
- d_skip: float32 [64], P('tp'), may hold values from 0.5 to 1.5
- norm_gain: float32 [4096], P('tp'), may hold values from 0.1 to 1.9
- out_weight: bfloat16 [4096, 4096], P('tp'), may hold values from -0.09375 to 0.09375
- final_gain: float32 [4096], replicated, may hold values from 0.1 to 1.9
- head_weight: bfloat16 [131072, 4096], P(('seq', 'tp')), may hold values from -0.25 to 0.25
Outputs:
- hidden_long: bfloat16 [16384, 4096], P('seq', 'tp')
- hidden_short: bfloat16 [64, 16, 4096], P('seq', None, 'tp')
- block_states: float32 [32, 64, 64, 128], P('seq', 'tp')
- short_states: float32 [64, 64, 64, 128], P('seq', 'tp')
- tails_x: bfloat16 [64, 3, 4096], P('seq', None, 'tp')
- tails_bc: bfloat16 [64, 3, 2, 512], P('seq', None, None, 'tp')
- last_norm: bfloat16 [65, 4096], replicated
- top_logit: float32 [65], replicated
Inputs may be any that keep to these rules, and one draw needn't show every extreme that they name: Request r's real tokens are at positions 0 to lengths[r] - 1; some request has 16.
All inputs are finite; a program needn't handle non-finite values.
Results may differ from a plain program's by a relative error of at most 0.014.
Values may be sent and summed in bfloat16 or wider, within the bound.
No kernel may reach another device: no remote copies, remote signals or barrier semaphores. Data moves between devices by JAX's collectives and lax.ppermute only.
A program may use at most 128 MiB of HBM per device.

v0:
```python
import jax
import jax.numpy as jnp
from jax import lax
from jax.sharding import PartitionSpec as P

D = 4096
HEAD_SHARE = 64
HEADDIM = 64
GROUPS = 4
STATE = 128
KCONV = 4
BLOCK = 256
SLEN = 16


def passed_along(block, axis, distance):
    devices = range(lax.axis_size(axis))
    route = [(i - distance, i) for i in devices if i - distance in devices]
    return lax.ppermute(block, axis, route)


def conv_act(padded, weight, shift_bias, span_len):
    running_sum = shift_bias + 0.0 * padded[:span_len].astype(jnp.float32)
    for offset in range(weight.shape[0]):
        running_sum = running_sum + weight[offset] * padded[offset : offset + span_len].astype(
            jnp.float32
        )
    return jax.nn.silu(running_sum).astype(jnp.bfloat16)


def expand(portion):
    shaped = portion.reshape(portion.shape[:-1] + (portion.shape[-1] // STATE, STATE))
    return jnp.repeat(shaped, HEAD_SHARE // GROUPS, axis=-2)


def ssd_block(x_block, b_block, c_block, dt_block, decay_rate, state_in):
    step_log = dt_block * decay_rate[:, None]
    cumulative = jnp.cumsum(step_log, axis=1)
    span_len = x_block.shape[0]
    positions = jnp.arange(span_len)
    causal = (positions[:, None] >= positions[None, :])[None]
    log_gap = jnp.where(causal, cumulative[:, :, None] - cumulative[:, None, :], 0.0)
    decay_table = jnp.where(causal, jnp.exp(log_gap), 0.0)
    scores = jnp.einsum("thn,shn->hts", c_block, b_block, preferred_element_type=jnp.float32)
    weights = (scores * decay_table * dt_block[:, None, :]).astype(jnp.bfloat16)
    y_intra = jnp.einsum("hts,shp->thp", weights, x_block, preferred_element_type=jnp.float32)
    y_state = jnp.exp(cumulative).T[:, :, None] * jnp.einsum(
        "thn,hpn->thp", c_block.astype(jnp.float32), state_in, precision=lax.Precision.HIGHEST
    )
    to_end = jnp.exp(cumulative[:, -1:] - cumulative) * dt_block
    scaled = (x_block.astype(jnp.float32) * to_end.T[:, :, None]).astype(jnp.bfloat16)
    next_state = jnp.exp(cumulative[:, -1])[:, None, None] * state_in + jnp.einsum(
        "shp,shn->hpn", scaled, b_block, preferred_element_type=jnp.float32
    )
    return (y_intra + y_state, next_state)


def gate_norm(values, gating, scales):
    gated_rows = values * jax.nn.silu(gating.astype(jnp.float32))
    size_group = HEAD_SHARE // GROUPS * HEADDIM
    shaped = gated_rows.reshape(gated_rows.shape[0], -1, size_group)
    inv_rms = lax.rsqrt(jnp.mean(shaped * shaped, axis=-1, keepdims=True) + 1e-05)
    return ((shaped * inv_rms).reshape(gated_rows.shape) * scales).astype(jnp.bfloat16)


def local(
    x_long,
    bc_long,
    z_long,
    dt_long,
    x_short,
    bc_short,
    z_short,
    dt_short,
    lengths,
    conv_x,
    conv_bc,
    conv_bias_x,
    conv_bias_bc,
    dt_bias,
    a_log,
    d_skip,
    norm_gain,
    out_weight,
    final_gain,
    head_weight,
):
    tok_rows, inner_cols = x_long.shape
    head_count = dt_long.shape[0]
    req_count = lengths.shape[0]
    rim_rows = KCONV - 1
    decay_rate = -jnp.exp(a_log)
    rim_x, rim_bc = passed_along(
        (x_long[tok_rows - rim_rows :], bc_long[tok_rows - rim_rows :]), "seq", 1
    )
    x_act = conv_act(jnp.concatenate([rim_x, x_long], 0), conv_x, conv_bias_x, tok_rows)
    bc_act = conv_act(jnp.concatenate([rim_bc, bc_long], 0), conv_bc, conv_bias_bc, tok_rows)
    dt_full = jax.nn.softplus(dt_long.astype(jnp.float32) + dt_bias[:, None])
    block_count = tok_rows // BLOCK
    x_blocks = x_act.reshape(block_count, BLOCK, head_count, HEADDIM)
    b_blocks = expand(bc_act[:, 0]).reshape(block_count, BLOCK, head_count, STATE)
    c_all = expand(bc_act[:, 1])
    c_blocks = c_all.reshape(block_count, BLOCK, head_count, STATE)
    dt_blocks = dt_full.reshape(head_count, block_count, BLOCK).transpose(1, 0, 2)

    def advance(carry_state, inputs):
        y_block, next_state = ssd_block(
            inputs[0], inputs[1], inputs[2], inputs[3], decay_rate, carry_state
        )
        return (next_state, y_block)

    start_state = jnp.zeros((head_count, HEADDIM, STATE), jnp.float32)
    local_state, y_blocks = lax.scan(
        advance, start_state, (x_blocks, b_blocks, c_blocks, dt_blocks)
    )
    cum_device = jnp.cumsum(dt_full * decay_rate[:, None], axis=1)
    total_log = cum_device[:, -1]
    all_logs = lax.all_gather(total_log[None], "seq", axis=0, tiled=True)
    running = jnp.cumsum(all_logs, axis=0)
    my_index = lax.axis_index("seq")
    prior_log = lax.dynamic_index_in_dim(running, jnp.maximum(my_index - 1, 0), 0, keepdims=False)
    portion = lax.all_gather(
        local_state[None].astype(jnp.bfloat16), "seq", axis=0, tiled=True
    ).astype(jnp.float32)
    span_len = portion.shape[0]
    source_ids = jnp.arange(span_len)
    before_me = (source_ids < my_index)[:, None]
    factor = jnp.where(
        before_me, jnp.exp(jnp.where(before_me, prior_log[None] - running, 0.0)), 0.0
    )
    carry_in = jnp.zeros_like(local_state) + jnp.einsum(
        "ch,chpn->hpn", factor, portion, precision=lax.Precision.HIGHEST
    )
    carried = jnp.exp(cum_device).T[:, :, None] * jnp.einsum(
        "thn,hpn->thp", c_all.astype(jnp.float32), carry_in, precision=lax.Precision.HIGHEST
    )
    y_long = (
        y_blocks.reshape(tok_rows, head_count, HEADDIM)
        + carried
        + d_skip[None, :, None] * x_act.reshape(tok_rows, head_count, HEADDIM).astype(jnp.float32)
    )
    block_states = (jnp.exp(total_log)[:, None, None] * carry_in + local_state)[None]
    normed_long = gate_norm(y_long.reshape(tok_rows, inner_cols), z_long, norm_gain)
    is_valid = jnp.arange(SLEN)[None, :] < lengths[:, None]
    zero_x = jnp.zeros((req_count, rim_rows) + x_short.shape[2:], jnp.bfloat16)
    zero_bc = jnp.zeros((req_count, rim_rows) + bc_short.shape[2:], jnp.bfloat16)
    x_sact = jax.vmap(lambda item: conv_act(item, conv_x, conv_bias_x, SLEN))(
        jnp.concatenate([zero_x, x_short], 1)
    )
    bc_sact = jax.vmap(lambda item: conv_act(item, conv_bc, conv_bias_bc, SLEN))(
        jnp.concatenate([zero_bc, bc_short], 1)
    )
    dt_sfull = jax.nn.softplus(dt_short.astype(jnp.float32) + dt_bias[:, None, None]) * is_valid[
        None
    ].astype(jnp.float32)
    dt_sfull = dt_sfull.transpose(1, 0, 2)

    def per_request(x_req, bc_req, dt_req):
        return ssd_block(
            x_req.reshape(SLEN, head_count, HEADDIM),
            expand(bc_req[:, 0]),
            expand(bc_req[:, 1]),
            dt_req,
            decay_rate,
            start_state,
        )

    y_sblocks, short_states = jax.vmap(per_request)(x_sact, bc_sact, dt_sfull)
    y_short = y_sblocks + d_skip[None, None, :, None] * x_sact.reshape(
        req_count, SLEN, head_count, HEADDIM
    ).astype(jnp.float32)
    normed_short = gate_norm(
        y_short.reshape(req_count * SLEN, inner_cols),
        z_short.reshape(req_count * SLEN, inner_cols),
        norm_gain,
    )
    tail_pick = (
        jnp.arange(SLEN)[None, None, :]
        == (lengths[:, None] - rim_rows + jnp.arange(rim_rows)[None, :])[:, :, None]
    ).astype(jnp.float32)
    tails_x = jnp.einsum(
        "rks,rsc->rkc", tail_pick, x_short.astype(jnp.float32), precision=lax.Precision.HIGHEST
    ).astype(jnp.bfloat16)
    tails_bc = jnp.einsum(
        "rks,rsbc->rkbc", tail_pick, bc_short.astype(jnp.float32), precision=lax.Precision.HIGHEST
    ).astype(jnp.bfloat16)
    all_normed = jnp.concatenate([normed_long, normed_short], 0)
    out_terms = jnp.dot(all_normed, out_weight, preferred_element_type=jnp.float32)
    hidden = lax.psum_scatter(out_terms.astype(jnp.bfloat16), "tp", scatter_dimension=1, tiled=True)
    hidden_long = hidden[:tok_rows]
    hidden_short = hidden[tok_rows:].reshape(req_count, SLEN, -1) * is_valid[:, :, None].astype(
        jnp.bfloat16
    )
    last_pick = (jnp.arange(SLEN)[None, :] == lengths[:, None] - 1).astype(jnp.float32)
    short_rows = jnp.einsum(
        "rs,rsd->rd", last_pick, hidden_short.astype(jnp.float32), precision=lax.Precision.HIGHEST
    ).astype(jnp.bfloat16)
    packed = jnp.concatenate([short_rows, hidden_long[tok_rows - 1 :]], 0)
    seq_rows = lax.all_gather(packed, "seq", axis=0, tiled=True)
    full_rows = lax.all_gather(seq_rows, "tp", axis=1, tiled=True)
    seq_count = lax.axis_size("seq")
    shaped = full_rows.reshape(seq_count, req_count + 1, D)
    long_row = shaped[seq_count - 1, req_count][None]
    short_all = shaped[:, :req_count].reshape(seq_count * req_count, D)
    row_block = jnp.concatenate([long_row, short_all], 0).astype(jnp.float32)
    last_norm = (
        row_block
        * lax.rsqrt(jnp.mean(row_block * row_block, axis=-1, keepdims=True) + 1e-05)
        * final_gain
    ).astype(jnp.bfloat16)
    logits = lax.dot_general(
        last_norm, head_weight, (((1,), (1,)), ((), ())), preferred_element_type=jnp.float32
    )
    top_logit = lax.pmax(jnp.max(logits, axis=1), ("seq", "tp"))
    return (
        hidden_long,
        hidden_short,
        block_states,
        short_states,
        tails_x,
        tails_bc,
        last_norm,
        top_logit,
    )


def solution(mesh):
    in_specs = (
        P("seq", "tp"),
        P("seq", None, "tp"),
        P("seq", "tp"),
        P("tp", "seq"),
        P("seq", None, "tp"),
        P("seq", None, None, "tp"),
        P("seq", None, "tp"),
        P("tp", "seq", None),
        P("seq"),
        P(None, "tp"),
        P(None, None, "tp"),
        P("tp"),
        P(None, "tp"),
        P("tp"),
        P("tp"),
        P("tp"),
        P("tp"),
        P("tp", None),
        P(),
        P(("seq", "tp"), None),
    )
    out_specs = (
        P("seq", "tp"),
        P("seq", None, "tp"),
        P("seq", "tp", None, None),
        P("seq", "tp", None, None),
        P("seq", None, "tp"),
        P("seq", None, None, "tp"),
        P(),
        P(),
    )
    return jax.shard_map(local, mesh=mesh, in_specs=in_specs, out_specs=out_specs, check_vma=False)
```

profile of v0, /device:TPU:8, one launch (start us, length us, event | category | flops | bytes accessed | tf_op | source)
XLA Modules:
  0.0 368.2 jit_solution(5212772003908098945)
XLA Ops:
  10.8 4.1 %collective-permute-start = (bf16[3,1024]{1,0:T(4,128)(2,1)S(1)}, bf16[3,1024]{1,0:T(4,128)(2,1)S(1)}, u32[]{:S(2)}, u32[]{:S(2)}) collective-permute-start(bf16[3,1024]{1,0:T(4,128)(2,1)S(1)} %slice.135), channel_id=1, source_target_pairs={{0,4},{4,8},{8,12},{12,16},{16,20},{20,24},{24,28},{28,32},{32,36}... | collective-permute-start | bytes 18440 | tf_op jit(solution)/shard_map/ppermute | solution.py:19
  19.2 2.4 multiply_convert_fusion.4
  21.6 2.4 reshape.343
  24.0 2.8 copy.99
  26.8 1.8 broadcast_in_dim.83
  30.4 63.4 %while.13 = (s32[]{:T(128)}, f32[16,64,128]{2,1,0:T(8,128)S(1)}, f32[2,256,16,64]{1,0,3,2:T(2,128)}, f32[2,16,256]{2,0,1:T(2,128)S(1)}, f32[16]{0:T(128)S(1)}, /...) while((s32[]{:T(128)}, f32[16,64,128]{2,1,0:T(8,128)S(1)}, ...), condition=%wide.region_3.4_spmd.clone, body=%wide.region_0.3_spmd.clone.sunk | while | flops 881147968 | bytes 14636104 | solution.py:113
  31.5 3.3 fusion.139
  35.1 2.5 fusion.140
  38.6 21.9 %dynamic_update_slice.6 = f32[2,256,16,64]{1,0,3,2:T(2,128)} dynamic-update-slice(f32[2,256,16,64]{1,0,3,2:T(2,128)} %get-tuple-element.243, f32[1,256,16,64]{1,0,3,2:T(1,128)S(1)} %copy.180, s32[]{:T(128)} %get-tuple-element.241, s32[]{:T(128)} %constant.49.clone.1..sunk, s32[]{:T(128)} %constant.49.clone.1..sunk, s32[]{:T(128)} %constant.49.clone.1..sunk) | dynamic-update-slice | bytes 2097156 | tf_op jit(solution)/shard_map/while/body/jit(dynamic_update_index_in_dim)/dynamic_update_slice | solution.py:113
  63.1 3.3 fusion.139
  66.7 2.5 fusion.140
  70.3 21.9 %dynamic_update_slice.6 = f32[2,256,16,64]{1,0,3,2:T(2,128)} dynamic-update-slice(f32[2,256,16,64]{1,0,3,2:T(2,128)} %get-tuple-element.243, f32[1,256,16,64]{1,0,3,2:T(1,128)S(1)} %copy.180, s32[]{:T(128)} %get-tuple-element.241, s32[]{:T(128)} %constant.49.clone.1..sunk, s32[]{:T(128)} %constant.49.clone.1..sunk, s32[]{:T(128)} %constant.49.clone.1..sunk) | dynamic-update-slice | bytes 2097156 | tf_op jit(solution)/shard_map/while/body/jit(dynamic_update_index_in_dim)/dynamic_update_slice | solution.py:113
  98.2 65.9 %all-reduce.2 = f32[512]{0:T(512)S(1)} all-reduce(f32[512]{0:T(512)S(1)} %dynamic-update-slice), channel_id=2, replica_groups=mesh['seq'=32,'tp'=4] {'seq'}, use_global_device_ids=true, to_apply=%add.2 | all-reduce | flops 512 | bytes 4096
  169.6 2.9 reshape.311
  172.6 11.6 %fusion.31 = f32[16,1,64,128]{3,1,2,0:T(1,128)S(1)} fusion(f32[32,16,1,1]{0,2,3,1:T(1,128)S(1)} %copy.116, bf16[32,16,64,128]{3,2,1,0:T(8,128)(2,1)} %bitcast.202), kind=kOutput, calls=%fused_computation.40 | convolution fusion | flops 50331648 | bytes 8914944 | tf_op jit(solution)/shard_map/ch,chpn->hpn/dot_general | solution.py:131
  184.2 3.7 %fusion.43 = f32[512,16,64]{0,2,1:T(8,128)} fusion(f32[512,16,64]{0,2,1:T(8,128)S(1)} %reshape.311, f32[512,16,64]{0,2,1:T(8,128)S(1)} %bitcast.203, f32[16,64,128]{2,1,0:T(8,128)S(1)} %bitcast.205, f32[16]{0:T(128)S(1)} %copy-done.23, bf16[512,128]{1,0:T(8,128)(2,1)S(1)} %get-tuple-element.156, f32[512,16]{0,1:T(8,128)S(1)} %exponential_bitcast_fusion.1), kind=kOutput, calls=%fused_computation.58 | convolution fusion | flops 807403520 | bytes 6979648 | tf_op jit(solution)/shard_map/thn,hpn->thp/dot_general | solution.py:134
  188.0 1.9 copy.104
  189.9 2.0 multiply_reduce_fusion
  192.8 10.0 %convolution_convert_fusion = bf16[544,4096]{1,0:T(8,128)(2,1)} fusion(bf16[1024,4096]{1,0:T(8,128)(2,1)} %param.39, bf16[32,1024]{1,0:T(8,128)(2,1)S(1)} %copy-done.11, bf16[512,1024]{1,0:T(8,128)(2,1)S(1)} %multiply_convert_fusion.3), kind=kOutput, calls=%fused_computation.42 | convolution fusion | flops 4567859200 | bytes 13959168 | tf_op jit(solution)/shard_map/dot_general | solution.py:188
  207.9 39.2 %reduce-scatter.2.cloned.1.call-done = bf16[544,1024]{1,0:T(8,128)(2,1)} async-done(((bf16[544,4096]{1,0:T(8,128)(2,1)}), bf16[544,1024]{1,0:T(8,128)(2,1)}) %reduce-scatter.2.cloned.1.call-update) | async-done | bytes 1114128 | tf_op jit(solution)/shard_map/reduce_scatter | solution.py:189
  249.0 25.1 %all-gather.2 = bf16[32,3,1024]{2,1,0:T(4,128)(2,1)S(1)} all-gather(bf16[1,3,1024]{2,1,0:T(4,128)(2,1)S(1)} %maximum_bitcast_fusion), channel_id=1, replica_groups=mesh['seq'=32,'tp'=4] {'seq'}, dimensions={0}, use_global_device_ids=true | all-gather | bytes 202752 | tf_op jit(solution)/shard_map/all_gather | solution.py:199
  274.2 13.1 %all_gather.15 = bf16[96,4096]{1,0:T(8,128)(2,1)S(1)} all-gather(bf16[96,1024]{1,0:T(8,128)(2,1)S(1)} %reshape.332), channel_id=1, replica_groups=mesh['seq'=32,'tp'=4] {'tp'}, dimensions={1}, use_global_device_ids=true | all-gather | bytes 983040 | tf_op jit(solution)/shard_map/all_gather | solution.py:200
  289.1 6.4 %convolution_reduce_fusion = f32[65]{0:T(128)S(1)} fusion(bf16[65,4096]{1,0:T(8,128)(2,1)S(1)} %fusion.46, bf16[1024,4096]{1,0:T(8,128)(2,1)} %param.41), kind=kOutput, calls=%fused_computation.78 | convolution fusion | flops 545326016 | bytes 8921348 | tf_op jit(solution)/shard_map/dot_general | solution.py:211
  295.5 64.8 %pmax.7 = f32[65]{0:T(128)} all-reduce(f32[65]{0:T(128)S(1)} %convolution_reduce_fusion), channel_id=1, replica_groups=mesh['seq'=32,'tp'=4] {'seq','tp'}, use_global_device_ids=true, to_apply=%region_13.14 | all-reduce | flops 65 | bytes 520 | tf_op jit(solution)/shard_map/pmax | solution.py:214
  (172 shorter events, 37.3 us)
Async XLA Ops:
  7.2 12.0 %copy-start.6 = (bf16[512,1024]{1,0:T(8,128)(2,1)S(1)}, bf16[512,1024]{1,0:T(8,128)(2,1)}, u32[]{:S(2)}) copy-start(bf16[512,1024]{1,0:T(8,128)(2,1)} %param.22) | copy-start | bytes 3145732
  7.2 165.4 %all-gather.5.cloned.1.call-start = ((), (), s32[]{:S(2)}) async-start(), calls=%async_computation.2 | async-start | bytes 8650752 | tf_op jit(solution)/shard_map/all_gather | solution.py:122
  8.3 9.7 %collective-permute-start.1 = (bf16[3,2,128]{2,0,1:T(4,128)(2,1)S(1)}, bf16[3,2,128]{2,0,1:T(4,128)(2,1)S(1)}, u32[]{:S(2)}, u32[]{:S(2)}) collective-permute-start(bf16[3,2,128]{2,0,1:T(4,128)(2,1)S(1)} %slice.182), channel_id=1, source_target_pairs={{0,4},{4,8},{8,12},{12,16},{16,20},{20,24},{24,28},{28,32},{32,36}... | collective-permute-start | bytes 4616 | tf_op jit(solution)/shard_map/ppermute | solution.py:19
  10.8 8.4 %collective-permute-start = (bf16[3,1024]{1,0:T(4,128)(2,1)S(1)}, bf16[3,1024]{1,0:T(4,128)(2,1)S(1)}, u32[]{:S(2)}, u32[]{:S(2)}) collective-permute-start(bf16[3,1024]{1,0:T(4,128)(2,1)S(1)} %slice.135), channel_id=1, source_target_pairs={{0,4},{4,8},{8,12},{12,16},{16,20},{20,24},{24,28},{28,32},{32,36}... | collective-permute-start | bytes 18440 | tf_op jit(solution)/shard_map/ppermute | solution.py:19
  21.6 5.2 %copy-start = (bf16[512,1024]{1,0:T(8,128)(2,1)}, bf16[512,1024]{1,0:T(8,128)(2,1)S(1)}, u32[]{:S(2)}) copy-start(bf16[512,1024]{1,0:T(8,128)(2,1)S(1)} %multiply_convert_fusion.4) | copy-start | bytes 3145732
  30.4 65.7 %copy-start.26 = (u32[128]{0:T(128)S(1)}, u32[128]{0:T(128)}, u32[]{:S(2)}) copy-start(u32[128]{0:T(128)} %constant.102) | copy-start | bytes 1540
  30.4 134.1 %copy-start.10 = (bf16[2,16,1024]{2,1,0:T(8,128)(2,1)S(1)}, bf16[2,16,1024]{2,1,0:T(8,128)(2,1)}, u32[]{:S(2)}) copy-start(bf16[2,16,1024]{2,1,0:T(8,128)(2,1)} %param.26) | copy-start | bytes 196612
  30.4 134.1 %copy-start.14 = (f32[1024]{0:T(1024)S(1)}, f32[1024]{0:T(1024)}, u32[]{:S(2)}) copy-start(f32[1024]{0:T(1024)} %param.33) | copy-start | bytes 12292
  30.4 134.3 %copy-start.15 = (bf16[2,16,2,128]{3,2,1,0:T(2,128)(2,1)S(1)}, bf16[2,16,2,128]{3,2,1,0:T(2,128)(2,1)}, u32[]{:S(2)}) copy-start(bf16[2,16,2,128]{3,2,1,0:T(2,128)(2,1)} %param.27) | copy-start | bytes 49156
  30.4 134.4 %copy-start.24 = (s32[2]{0:T(128)S(1)}, s32[2]{0:T(128)}, u32[]{:S(2)}) copy-start(s32[2]{0:T(128)} %param.30) | copy-start | bytes 28
  30.4 134.9 %copy-start.9 = (bf16[16,2,16]{2,1,0:T(2,128)(2,1)S(1)}, bf16[16,2,16]{2,1,0:T(2,128)(2,1)}, u32[]{:S(2)}) copy-start(bf16[16,2,16]{2,1,0:T(2,128)(2,1)} %param.29) | copy-start | bytes 3076
  30.4 134.9 %copy-start.17 = (f32[16]{0:T(128)S(1)}, f32[16]{0:T(128)}, u32[]{:S(2)}) copy-start(f32[16]{0:T(128)} %param.35) | copy-start | bytes 196
  30.4 135.4 %copy-start.7 = (bf16[2,16,1024]{2,1,0:T(8,128)(2,1)S(1)}, bf16[2,16,1024]{2,1,0:T(8,128)(2,1)}, u32[]{:S(2)}) copy-start(bf16[2,16,1024]{2,1,0:T(8,128)(2,1)} %param.28) | copy-start | bytes 196612
  93.8 72.1 %copy-start.19 = (f32[2,128]{1,0:T(2,128)S(1)}, f32[2,128]{1,0:T(2,128)}, u32[]{:S(2)}) copy-start(f32[2,128]{1,0:T(2,128)} %param.34) | copy-start | bytes 3076
  93.8 72.7 %copy-start.22 = (f32[16]{0:T(128)S(1)}, f32[16]{0:T(128)}, u32[]{:S(2)}) copy-start(f32[16]{0:T(128)} %param.37) | copy-start | bytes 196
  94.6 152.5 %reduce-scatter.2.cloned.1.call-start = ((), (), s32[]{:S(2)}) async-start(), calls=%async_computation.1 | async-start | bytes 5570560 | tf_op jit(solution)/shard_map/reduce_scatter | solution.py:189
  172.6 11.6 %copy-start.2 = (f32[512,1024]{0,1:T(8,128)S(1)}, f32[512,1024]{0,1:T(8,128)}, u32[]{:S(2)}) copy-start(f32[512,1024]{0,1:T(8,128)} %copy.103) | copy-start | bytes 6291460
  172.6 11.6 %copy-start.23 = (f32[16]{0:T(128)S(1)}, f32[16]{0:T(128)}, u32[]{:S(2)}) copy-start(f32[16]{0:T(128)} %param.37) | copy-start | bytes 196
  202.8 2.6 copy-start.18
  202.8 4.2 %copy-start.20 = (f32[16]{0:T(128)S(1)}, f32[16]{0:T(128)}, u32[]{:S(2)}) copy-start(f32[16]{0:T(128)} %get-tuple-element.136) | copy-start | bytes 196
  203.5 44.5 %copy-start.21 = (bf16[2,16]{1,0:T(2,128)(2,1)S(1)}, bf16[2,16]{1,0:T(2,128)(2,1)}, u32[]{:S(2)}) copy-start(bf16[2,16]{1,0:T(2,128)(2,1)} %get-tuple-element.173) | copy-start | bytes 196
  248.1 40.2 %copy-start.8 = (bf16[2,16,1024]{2,1,0:T(8,128)(2,1)}, bf16[2,16,1024]{2,1,0:T(8,128)(2,1)S(1)}, u32[]{:S(2)}) copy-start(bf16[2,16,1024]{2,1,0:T(8,128)(2,1)S(1)} %broadcast_multiply_fusion.1) | copy-start | bytes 196612
  289.1 6.4 %copy-start.4 = (bf16[65,4096]{1,0:T(8,128)(2,1)}, bf16[65,4096]{1,0:T(8,128)(2,1)S(1)}, u32[]{:S(2)}) copy-start(bf16[65,4096]{1,0:T(8,128)(2,1)S(1)} %fusion.46) | copy-start | bytes 1597444
  289.1 71.2 %copy-start.5 = (bf16[544,1024]{1,0:T(8,128)(2,1)S(1)}, bf16[544,1024]{1,0:T(8,128)(2,1)}, u32[]{:S(2)}) copy-start(bf16[544,1024]{1,0:T(8,128)(2,1)} %reduce-scatter.2.cloned.1.call-done) | copy-start | bytes 3342340
  (7 other events, 10.1 us)
Sparse Core Ops, SparseCore 0:
  94.7 54.9 all-gather.4
  203.0 44.1 reduce-scatter.1
where the time goes:
time: 373 us; the launch traced here: 368 us
  blocking collectives  169 us (45%)
  local copies, waits for them, and re-layouts  73.8 us (20%)
  matrix products  49.3 us (13%)
  waiting for transfers between devices  39.3 us (11%)
  other arithmetic  15.5 us (4%)
  between operations  15.3 us (4%)
  starting transfers between devices  5.91 us (2%)
    unnamed x1, blocking collectives  65.9 us
    pmax x1, blocking collectives, local(): top_logit = lax.pmax(jnp.max(logits, axis=1), ('seq', 'tp'))  64.8 us
    dynamic_update_slice x4, local copies, waits for them, and re-layouts, local(): lax.scan(advance, start_state, (x_blocks, b_blocks, c_blocks, dt_blocks))  45.9 us
    reduce_scatter x1, waiting for transfers between devices, local(): lax.psum_scatter(out_terms.astype(jnp.bfloat16), 'tp', scatter_dimension=...  39.2 us
    all_gather x1, blocking collectives, local(): seq_rows = lax.all_gather(packed, 'seq', axis=0, tiled=True)  25.1 us
    all_gather x1, blocking collectives, local(): full_rows = lax.all_gather(seq_rows, 'tp', axis=1, tiled=True)  13.1 us
    dot_general x1, matrix products, local(): jnp.einsum('ch,chpn->hpn', factor, portion, precision=lax.Precision.HIGHEST)  11.6 us
    dot_general x1, matrix products, local(): jnp.dot(all_normed, out_weight, preferred_element_type=jnp.float32)  10 us
  transfers between devices with their start and end apart: 4, of which 1 were waited for; matrix products, arithmetic and copies ran while one was open for 6% of the time, Pallas kernels for 0%

commit v1 on v0

--- a/solution.py
+++ b/solution.py
@@ -17,6 +17,52 @@
     devices = range(lax.axis_size(axis))
     route = [(i - distance, i) for i in devices if i - distance in devices]
     return lax.ppermute(block, axis, route)
+
+
+def swapped(block, axis, distance):
+    devices = range(lax.axis_size(axis))
+    return lax.ppermute(block, axis, [(i, i ^ distance) for i in devices])
+
+
+def gather_all(block, axis, dim):
+    count = lax.axis_size(axis)
+    index = lax.axis_index(axis)
+    distance = 1
+    while distance < count:
+        other = swapped(block, axis, distance)
+        low = (index // distance) % 2 == 0
+        block = jnp.where(
+            low, jnp.concatenate([block, other], dim), jnp.concatenate([other, block], dim)
+        )
+        distance *= 2
+    return block
+
+
+def max_all(block, axis):
+    distance = 1
+    while distance < lax.axis_size(axis):
+        block = jnp.maximum(block, swapped(block, axis, distance))
+        distance *= 2
+    return block
+
+
+def carry_scan(total_log, local_state, axis):
+    sent = local_state.astype(jnp.bfloat16)
+    log_one, state_one = passed_along((total_log, sent), axis, 1)
+    log_two, state_two = passed_along((total_log, sent), axis, 2)
+    seg_log = log_one + log_two
+    seg_state = jnp.exp(log_one)[:, None, None] * state_two.astype(jnp.float32) + state_one.astype(
+        jnp.float32
+    )
+    distance = 2
+    while distance < lax.axis_size(axis):
+        got_log, got_state = passed_along(
+            (seg_log, seg_state.astype(jnp.bfloat16)), axis, distance
+        )
+        seg_state = jnp.exp(seg_log)[:, None, None] * got_state.astype(jnp.float32) + seg_state
+        seg_log = seg_log + got_log
+        distance *= 2
+    return seg_state
 
 
 def conv_act(padded, weight, shift_bias, span_len):
@@ -103,34 +149,18 @@
     c_blocks = c_all.reshape(block_count, BLOCK, head_count, STATE)
     dt_blocks = dt_full.reshape(head_count, block_count, BLOCK).transpose(1, 0, 2)
 
-    def advance(carry_state, inputs):
-        y_block, next_state = ssd_block(
-            inputs[0], inputs[1], inputs[2], inputs[3], decay_rate, carry_state
-        )
-        return (next_state, y_block)
-
     start_state = jnp.zeros((head_count, HEADDIM, STATE), jnp.float32)
-    local_state, y_blocks = lax.scan(
-        advance, start_state, (x_blocks, b_blocks, c_blocks, dt_blocks)
-    )
+    local_state = start_state
+    y_parts = []
+    for index in range(block_count):
+        y_block, local_state = ssd_block(
+            x_blocks[index], b_blocks[index], c_blocks[index], dt_blocks[index], decay_rate, local_state
+        )
+        y_parts.append(y_block)
+    y_blocks = jnp.stack(y_parts)
     cum_device = jnp.cumsum(dt_full * decay_rate[:, None], axis=1)
     total_log = cum_device[:, -1]
-    all_logs = lax.all_gather(total_log[None], "seq", axis=0, tiled=True)
-    running = jnp.cumsum(all_logs, axis=0)
-    my_index = lax.axis_index("seq")
-    prior_log = lax.dynamic_index_in_dim(running, jnp.maximum(my_index - 1, 0), 0, keepdims=False)
-    portion = lax.all_gather(
-        local_state[None].astype(jnp.bfloat16), "seq", axis=0, tiled=True
-    ).astype(jnp.float32)
-    span_len = portion.shape[0]
-    source_ids = jnp.arange(span_len)
-    before_me = (source_ids < my_index)[:, None]
-    factor = jnp.where(
-        before_me, jnp.exp(jnp.where(before_me, prior_log[None] - running, 0.0)), 0.0
-    )
-    carry_in = jnp.zeros_like(local_state) + jnp.einsum(
-        "ch,chpn->hpn", factor, portion, precision=lax.Precision.HIGHEST
-    )
+    carry_in = carry_scan(total_log, local_state, "seq")
     carried = jnp.exp(cum_device).T[:, :, None] * jnp.einsum(
         "thn,hpn->thp", c_all.astype(jnp.float32), carry_in, precision=lax.Precision.HIGHEST
     )
@@ -185,8 +215,22 @@
         "rks,rsbc->rkbc", tail_pick, bc_short.astype(jnp.float32), precision=lax.Precision.HIGHEST
     ).astype(jnp.bfloat16)
     all_normed = jnp.concatenate([normed_long, normed_short], 0)
-    out_terms = jnp.dot(all_normed, out_weight, preferred_element_type=jnp.float32)
-    hidden = lax.psum_scatter(out_terms.astype(jnp.bfloat16), "tp", scatter_dimension=1, tiled=True)
+    tp_count = lax.axis_size("tp")
+    tp_index = lax.axis_index("tp")
+    width = out_weight.shape[1] // tp_count
+    total = None
+    for step in (2, 1, 3, 0):
+        if step >= tp_count:
+            continue
+        target = (tp_index + step) % tp_count
+        piece = lax.dynamic_slice_in_dim(out_weight, target * width, width, 1)
+        term = jnp.dot(all_normed, piece, preferred_element_type=jnp.float32).astype(jnp.bfloat16)
+        if step:
+            term = lax.ppermute(
+                term, "tp", [(i, (i + step) % tp_count) for i in range(tp_count)]
+            )
+        total = term.astype(jnp.float32) if total is None else total + term.astype(jnp.float32)
+    hidden = total.astype(jnp.bfloat16)
     hidden_long = hidden[:tok_rows]
     hidden_short = hidden[tok_rows:].reshape(req_count, SLEN, -1) * is_valid[:, :, None].astype(
         jnp.bfloat16
@@ -196,8 +240,8 @@
         "rs,rsd->rd", last_pick, hidden_short.astype(jnp.float32), precision=lax.Precision.HIGHEST
     ).astype(jnp.bfloat16)
     packed = jnp.concatenate([short_rows, hidden_long[tok_rows - 1 :]], 0)
-    seq_rows = lax.all_gather(packed, "seq", axis=0, tiled=True)
-    full_rows = lax.all_gather(seq_rows, "tp", axis=1, tiled=True)
+    seq_rows = gather_all(packed, "seq", 0)
+    full_rows = gather_all(seq_rows, "tp", 1)
     seq_count = lax.axis_size("seq")
     shaped = full_rows.reshape(seq_count, req_count + 1, D)
     long_row = shaped[seq_count - 1, req_count][None]
@@ -211,7 +255,7 @@
     logits = lax.dot_general(
         last_norm, head_weight, (((1,), (1,)), ((), ())), preferred_element_type=jnp.float32
     )
-    top_logit = lax.pmax(jnp.max(logits, axis=1), ("seq", "tp"))
+    top_logit = max_all(max_all(jnp.max(logits, axis=1), "tp"), "seq")
     return (
         hidden_long,
         hidden_short,

time: 373 us -> 247 us (0.66)
  blocking collectives: 169 us -> 0 us
  starting transfers between devices: 5.91 us -> 79.6 us
  local copies, waits for them, and re-layouts: 73.8 us -> 15 us
  waiting for transfers between devices: 39.3 us -> 80.9 us
  between operations: 15.3 us -> 1.88 us
  other arithmetic: 15.5 us -> 25.3 us
  matrix products: 49.3 us -> 41.9 us
    ppermute x0 -> x17, waiting for transfers between devices: none -> 72.2 us  [the longest x3 37.1 us: local(): lax.ppermute(term, 'tp', [(i, (i + step) % tp_count) for i in range(tp_co...]
    unnamed x1 -> x0, blocking collectives: 65.9 us -> none
    pmax x1 -> x0, blocking collectives: 64.8 us -> none  [local(): top_logit = lax.pmax(jnp.max(logits, axis=1), ('seq', 'tp'))]
    dynamic_update_slice x4 -> x0, local copies, waits for them, and re-layouts: 45.9 us -> none  [local(): lax.scan(advance, start_state, (x_blocks, b_blocks, c_blocks, dt_blocks))]
    ppermute x2 -> x13, starting transfers between devices: 5.83 us -> 49.6 us  [passed_along(): return lax.ppermute(block, axis, route)]
    reduce_scatter x1 -> x0, waiting for transfers between devices: 39.2 us -> none  [local(): lax.psum_scatter(out_terms.astype(jnp.bfloat16), 'tp', scatter_dimension=...]
    all_gather x2 -> x0, blocking collectives: 38.2 us -> none  [the longest x1 25.1 us: local(): seq_rows = lax.all_gather(packed, 'seq', axis=0, tiled=True)]
    ppermute x0 -> x17, starting transfers between devices: none -> 30 us  [the longest x14 25.7 us: swapped(): return lax.ppermute(block, axis, [(i, i ^ distance) for i in devices])]
  transfers between devices with their start and end apart: 4 -> 30, of which waited for: 1 -> 18; matrix products, arithmetic and copies ran while one was open for 6% -> 20% of each run, Pallas kernels for 0% -> 0%
where the time goes in v1:
time: 247 us; the launch traced here: 245 us
  waiting for transfers between devices  80.9 us (33%)
  starting transfers between devices  79.6 us (32%)
  matrix products  41.9 us (17%)
  other arithmetic  25.3 us (10%)
  local copies, waits for them, and re-layouts  15 us (6%)
    ppermute x13, starting transfers between devices, passed_along(): return lax.ppermute(block, axis, route)  49.6 us
    ppermute x3, waiting for transfers between devices, local(): lax.ppermute(term, 'tp', [(i, (i + step) % tp_count) for i in range(tp_co...  37.1 us
    ppermute x14, waiting for transfers between devices, swapped(): return lax.ppermute(block, axis, [(i, i ^ distance) for i in devices])  35.2 us
    ppermute x14, starting transfers between devices, swapped(): return lax.ppermute(block, axis, [(i, i ^ distance) for i in devices])  25.7 us
    dot_general x4, matrix products, local(): jnp.dot(all_normed, piece, preferred_element_type=jnp.float32)  16.1 us
    ppermute x13, waiting for transfers between devices, passed_along(): return lax.ppermute(block, axis, route)  8.7 us
    dot_general x3, matrix products, ssd_block(): jnp.einsum('hts,shp->thp', weights, x_block, preferred_element_type=jnp.f...  7.76 us
    dot_general x1, matrix products, local(): lax.dot_general(last_norm, head_weight, (((1,), (1,)), ((), ())), preferr...  6.49 us
  transfers between devices with their start and end apart: 30, of which 18 were waited for; matrix products, arithmetic and copies ran while one was open for 20% of the time, Pallas kernels for 0%

profile of v1, /device:TPU:8, one launch (start us, length us, event | category | flops | bytes accessed | tf_op | source)
XLA Modules:
  0.0 244.7 jit_solution(9864444452899202734)
XLA Ops:
  5.6 4.0 %collective-permute-start.3 = (f32[16]{0:T(128)S(1)}, f32[16]{0:T(128)S(1)}, u32[]{:S(2)}, u32[]{:S(2)}) collective-permute-start(f32[16]{0:T(128)S(1)} %slice_reduce_fusion.5), channel_id=1, source_target_pairs={{0,8},{4,12},{8,16},{12,20},{16,24},{20,28},{24,32},{28,36},{32,40... | collective-permute-start | bytes 200 | tf_op jit(solution)/shard_map/ppermute | solution.py:19
  10.6 3.6 %collective-permute-start.1 = (bf16[3,2,128]{2,0,1:T(4,128)(2,1)S(1)}, bf16[3,2,128]{2,0,1:T(4,128)(2,1)S(1)}, u32[]{:S(2)}, u32[]{:S(2)}) collective-permute-start(bf16[3,2,128]{2,0,1:T(4,128)(2,1)S(1)} %slice.253), channel_id=1, source_target_pairs={{0,4},{4,8},{8,12},{12,16},{16,20},{20,24},{24,28},{28,32},{32,36}... | collective-permute-start | bytes 4616 | tf_op jit(solution)/shard_map/ppermute | solution.py:19
  45.4 5.4 %collective-permute-start.5 = (f32[16]{0:T(128)S(1)}, f32[16]{0:T(128)S(1)}, u32[]{:S(2)}, u32[]{:S(2)}) collective-permute-start(f32[16]{0:T(128)S(1)} %get-tuple-element.37), channel_id=1, source_target_pairs={{0,16},{4,20},{8,24},{12,28},{16,32},{20,36},{24,40},{28,44},{32,4... | collective-permute-start | bytes 200 | tf_op jit(solution)/shard_map/ppermute | solution.py:19
  52.6 4.5 %collective-permute-start.6 = (f32[16]{0:T(128)S(1)}, f32[16]{0:T(128)S(1)}, u32[]{:S(2)}, u32[]{:S(2)}) collective-permute-start(f32[16]{0:T(128)S(1)} %get-tuple-element.35), channel_id=1, source_target_pairs={{0,32},{4,36},{8,40},{12,44},{16,48},{20,52},{24,56},{28,60},{32,6... | collective-permute-start | bytes 200 | tf_op jit(solution)/shard_map/ppermute | solution.py:19
  57.3 3.8 %collective-permute-start.9 = (bf16[16,64,128]{2,1,0:T(8,128)(2,1)S(1)}, bf16[16,64,128]{2,1,0:T(8,128)(2,1)S(1)}, u32[]{:S(2)}, u32[]{:S(2)}) collective-permute-start(bf16[16,64,128]{2,1,0:T(8,128)(2,1)S(1)} %fusion.73), channel_id=1, source_target_pairs={{0,8},{4,12},{8,16},{12,20},{16,24},{20,28},{24,32},{28,36},{32,40... | collective-permute-start | bytes 786440 | tf_op jit(solution)/shard_map/ppermute | solution.py:19
  61.7 4.9 %collective-permute-done.9 = bf16[16,64,128]{2,1,0:T(8,128)(2,1)S(1)} collective-permute-done((bf16[16,64,128]{2,1,0:T(8,128)(2,1)S(1)}, bf16[16,64,128]{2,1,0:T(8,128)(2,1)S(1)}, u32[]{:S(2)}, u32[]{:S(2)}) %collective-permute-start.9) | collective-permute-done | bytes 262176 | tf_op jit(solution)/shard_map/ppermute | solution.py:19
  67.6 4.8 %collective-permute-start.10 = (bf16[16,64,128]{2,1,0:T(8,128)(2,1)S(1)}, bf16[16,64,128]{2,1,0:T(8,128)(2,1)S(1)}, u32[]{:S(2)}, u32[]{:S(2)}) collective-permute-start(bf16[16,64,128]{2,1,0:T(8,128)(2,1)S(1)} %fusion.137), channel_id=1, source_target_pairs={{0,16},{4,20},{8,24},{12,28},{16,32},{20,36},{24,40},{28,44},{32,4... | collective-permute-start | bytes 786440 | tf_op jit(solution)/shard_map/ppermute | solution.py:19
  72.4 3.7 %fusion.33 = f32[256,16,64]{0,2,1:T(8,128)} fusion(bf16[256,16,64]{0,2,1:T(8,128)(2,1)S(1)} %bitcast.184, f32[16,256]{1,0:T(8,128)} %get-tuple-element.75, f32[16,256]{1,0:T(8,128)} %copy-done.30, pred[256,256]{1,0:T(8,128)(4,1)} %iota_compare_fusion, bf16[256,128]{1,0:T(8,128)(2,1)} %copy-done.22, bf16[256,128]{1,0:T(8,128)(2,1)} %get-tuple-element.44), kind=kOutput, calls=%fused_computation.41 | convolution fusion | flops 408944640 | bytes 1802240 | tf_op jit(solution)/shard_map/hts,shp->thp/dot_general | solution.py:92
  78.4 8.1 %collective-permute-start.11 = (bf16[16,64,128]{2,1,0:T(8,128)(2,1)}, bf16[16,64,128]{2,1,0:T(8,128)(2,1)}, u32[]{:S(2)}, u32[]{:S(2)}) collective-permute-start(bf16[16,64,128]{2,1,0:T(8,128)(2,1)} %fusion.74), channel_id=1, source_target_pairs={{0,32},{4,36},{8,40},{12,44},{16,48},{20,52},{24,56},{28,60},{32,6... | collective-permute-start | bytes 786440 | tf_op jit(solution)/shard_map/ppermute | solution.py:19
  86.5 3.7 %fusion.34 = f32[256,16,64]{0,2,1:T(8,128)} fusion(bf16[256,16,64]{0,2,1:T(8,128)(2,1)S(1)} %bitcast.186, f32[16,256]{1,0:T(8,128)} %get-tuple-element.76, f32[16,256]{1,0:T(8,128)} %copy-done.29, pred[256,256]{1,0:T(8,128)(4,1)} %iota_compare_fusion, bf16[256,128]{1,0:T(8,128)(2,1)} %copy-done.28, bf16[256,128]{1,0:T(8,128)(2,1)} %get-tuple-element.42), kind=kOutput, calls=%fused_computation.42 | convolution fusion | flops 408944640 | bytes 1802240 | tf_op jit(solution)/shard_map/hts,shp->thp/dot_general | solution.py:92
  101.4 3.8 %fusion.10 = f32[512,16,64]{0,2,1:T(8,128)} fusion(f32[512,16,64]{0,2,1:T(8,128)S(1)} %bitcast.181, f32[512,16,64]{0,2,1:T(8,128)S(1)} %bitcast.180, f32[16]{0:T(128)S(1)} %copy-done.55, bf16[512,128]{1,0:T(8,128)(2,1)S(1)} %slice_bitcast_fusion, f32[512,16]{0,1:T(8,128)S(1)} %copy-done.23, f32[16,64,128]{2,1,0:T(8,128)S(1)} %get-tuple-element.33, ...), kind=kOutput, calls=%fused_computation.19 | convolution fusion | flops 807796736 | bytes 7241856 | tf_op jit(solution)/shard_map/thn,hpn->thp/dot_general | solution.py:164
  108.8 4.3 %fusion.19 = bf16[544,1024]{1,0:T(8,128)(2,1)} fusion(bf16[1024,4096]{1,0:T(8,128)(2,1)} %param.37, s32[]{:T(128)S(6)} %select_n.180, bf16[32,1024]{1,0:T(8,128)(2,1)S(1)} %copy-done.27, bf16[512,1024]{1,0:T(8,128)(2,1)S(1)} %multiply_convert_fusion.2), kind=kOutput, calls=%fused_computation.31 | convolution fusion | flops 1143635968 | bytes 4325380 | tf_op jit(solution)/shard_map/dot_general | solution.py:227
  115.4 3.9 %fusion.22 = bf16[544,1024]{1,0:T(8,128)(2,1)} fusion(bf16[1024,4096]{1,0:T(8,128)(2,1)} %param.37, s32[]{:T(128)S(6)} %select_n.182, bf16[32,1024]{1,0:T(8,128)(2,1)S(1)} %copy-done.27, bf16[512,1024]{1,0:T(8,128)(2,1)S(1)} %multiply_convert_fusion.2), kind=kOutput, calls=%fused_computation.32 | convolution fusion | flops 1143635968 | bytes 4325380 | tf_op jit(solution)/shard_map/dot_general | solution.py:227
  119.3 4.0 %fusion.25 = bf16[544,1024]{1,0:T(8,128)(2,1)} fusion(bf16[1024,4096]{1,0:T(8,128)(2,1)} %param.37, s32[]{:T(128)S(6)} %select_n.184, bf16[32,1024]{1,0:T(8,128)(2,1)S(1)} %copy-done.27, bf16[512,1024]{1,0:T(8,128)(2,1)S(1)} %multiply_convert_fusion.2), kind=kOutput, calls=%fused_computation.33 | convolution fusion | flops 1143635968 | bytes 4325380 | tf_op jit(solution)/shard_map/dot_general | solution.py:227
  125.4 16.9 %collective-permute-done.13 = bf16[544,1024]{1,0:T(8,128)(2,1)S(1)} collective-permute-done((bf16[544,1024]{1,0:T(8,128)(2,1)}, bf16[544,1024]{1,0:T(8,128)(2,1)S(1)}, u32[]{:S(2)}, u32[]{:S(2)}) %collective-permute-start.13) | collective-permute-done | bytes 1114144 | tf_op jit(solution)/shard_map/ppermute | solution.py:229
  142.3 20.2 %collective-permute-done.14 = bf16[544,1024]{1,0:T(8,128)(2,1)S(1)} collective-permute-done((bf16[544,1024]{1,0:T(8,128)(2,1)}, bf16[544,1024]{1,0:T(8,128)(2,1)S(1)}, u32[]{:S(2)}, u32[]{:S(2)}) %collective-permute-start.14) | collective-permute-done | bytes 1114144 | tf_op jit(solution)/shard_map/ppermute | solution.py:229
  163.4 3.9 %add_convert_fusion = bf16[544,1024]{1,0:T(8,128)(2,1)S(1)} fusion(bf16[544,1024]{1,0:T(8,128)(2,1)} %collective-permute-done.15, bf16[544,1024]{1,0:T(8,128)(2,1)} %copy-done.56, bf16[544,1024]{1,0:T(8,128)(2,1)S(1)} %collective-permute-done.13, bf16[1024,4096]{1,0:T(8,128)(2,1)} %param.37, s32[]{:T(128)S(6)} %select_n.186, ...), kind=kOutput, calls=%fused_computation.6 | convolution fusion | flops 1148092416 | bytes 7667716 | tf_op jit(solution)/shard_map/dot_general | solution.py:227
  175.7 3.8 %collective-permute-done.18 = bf16[12,1024]{1,0:T(8,128)(2,1)S(1)} collective-permute-done((bf16[12,1024]{1,0:T(8,128)(2,1)S(1)}, bf16[12,1024]{1,0:T(8,128)(2,1)S(1)}, u32[]{:S(2)}, u32[]{:S(2)}) %collective-permute-start.18) | collective-permute-done | bytes 24608 | tf_op jit(solution)/shard_map/ppermute | solution.py:24
  179.6 4.0 %collective-permute-done.19 = bf16[24,1024]{1,0:T(8,128)(2,1)S(1)} collective-permute-done((bf16[24,1024]{1,0:T(8,128)(2,1)S(1)}, bf16[24,1024]{1,0:T(8,128)(2,1)S(1)}, u32[]{:S(2)}, u32[]{:S(2)}) %collective-permute-start.19) | collective-permute-done | bytes 49184 | tf_op jit(solution)/shard_map/ppermute | solution.py:24
  183.7 4.1 %collective-permute-start.20 = (bf16[48,1024]{1,0:T(8,128)(2,1)S(1)}, bf16[48,1024]{1,0:T(8,128)(2,1)S(1)}, u32[]{:S(2)}, u32[]{:S(2)}) collective-permute-start(bf16[48,1024]{1,0:T(8,128)(2,1)S(1)} %maximum_select_fusion.4), channel_id=1, source_target_pairs={{0,64},{4,68},{8,72},{12,76},{16,80},{20,84},{24,88},{28,92},{32,9... | collective-permute-start | bytes 294920 | tf_op jit(solution)/shard_map/ppermute | solution.py:24
  190.8 5.6 %collective-permute-done.21 = bf16[96,1024]{1,0:T(8,128)(2,1)S(1)} collective-permute-done((bf16[96,1024]{1,0:T(8,128)(2,1)S(1)}, bf16[96,1024]{1,0:T(8,128)(2,1)S(1)}, u32[]{:S(2)}, u32[]{:S(2)}) %collective-permute-start.21) | collective-permute-done | bytes 196640 | tf_op jit(solution)/shard_map/ppermute | solution.py:24
  200.4 5.7 %collective-permute-done.22 = bf16[96,2048]{1,0:T(8,128)(2,1)S(1)} collective-permute-done((bf16[96,2048]{1,0:T(8,128)(2,1)S(1)}, bf16[96,2048]{1,0:T(8,128)(2,1)S(1)}, u32[]{:S(2)}, u32[]{:S(2)}) %collective-permute-start.22) | collective-permute-done | bytes 393248 | tf_op jit(solution)/shard_map/ppermute | solution.py:24
  208.6 6.5 %convolution_reduce_fusion = f32[65]{0:T(128)S(1)} fusion(bf16[65,4096]{1,0:T(8,128)(2,1)S(1)} %fusion.43, bf16[1024,4096]{1,0:T(8,128)(2,1)} %param.39), kind=kOutput, calls=%fused_computation.65 | convolution fusion | flops 545326016 | bytes 8921348 | tf_op jit(solution)/shard_map/dot_general | solution.py:255
  237.8 4.3 %collective-permute-start.29 = (f32[65]{0:T(128)S(1)}, f32[65]{0:T(128)S(1)}, u32[]{:S(2)}, u32[]{:S(2)}) collective-permute-start(f32[65]{0:T(128)S(1)} %max.46), channel_id=1, source_target_pairs={{0,64},{4,68},{8,72},{12,76},{16,80},{20,84},{24,88},{28,92},{32,9... | collective-permute-start | bytes 788 | tf_op jit(solution)/shard_map/ppermute | solution.py:24
  (282 shorter events, 105.2 us)
Async XLA Ops:
  3.9 26.9 %collective-permute-start.2 = (f32[16]{0:T(128)S(1)}, f32[16]{0:T(128)S(1)}, u32[]{:S(2)}, u32[]{:S(2)}) collective-permute-start(f32[16]{0:T(128)S(1)} %slice_reduce_fusion.5), channel_id=1, source_target_pairs={{0,4},{4,8},{8,12},{12,16},{16,20},{20,24},{24,28},{28,32},{32,36}... | collective-permute-start | bytes 200 | tf_op jit(solution)/shard_map/ppermute | solution.py:19
  5.6 25.2 %collective-permute-start.3 = (f32[16]{0:T(128)S(1)}, f32[16]{0:T(128)S(1)}, u32[]{:S(2)}, u32[]{:S(2)}) collective-permute-start(f32[16]{0:T(128)S(1)} %slice_reduce_fusion.5), channel_id=1, source_target_pairs={{0,8},{4,12},{8,16},{12,20},{16,24},{20,28},{24,32},{28,36},{32,40... | collective-permute-start | bytes 200 | tf_op jit(solution)/shard_map/ppermute | solution.py:19
  10.6 24.3 %collective-permute-start.1 = (bf16[3,2,128]{2,0,1:T(4,128)(2,1)S(1)}, bf16[3,2,128]{2,0,1:T(4,128)(2,1)S(1)}, u32[]{:S(2)}, u32[]{:S(2)}) collective-permute-start(bf16[3,2,128]{2,0,1:T(4,128)(2,1)S(1)} %slice.253), channel_id=1, source_target_pairs={{0,4},{4,8},{8,12},{12,16},{16,20},{20,24},{24,28},{28,32},{32,36}... | collective-permute-start | bytes 4616 | tf_op jit(solution)/shard_map/ppermute | solution.py:19
  15.0 21.0 %collective-permute-start = (bf16[3,1024]{1,0:T(4,128)(2,1)S(1)}, bf16[3,1024]{1,0:T(4,128)(2,1)S(1)}, u32[]{:S(2)}, u32[]{:S(2)}) collective-permute-start(bf16[3,1024]{1,0:T(4,128)(2,1)S(1)} %slice.193), channel_id=1, source_target_pairs={{0,4},{4,8},{8,12},{12,16},{16,20},{20,24},{24,28},{28,32},{32,36}... | collective-permute-start | bytes 18440 | tf_op jit(solution)/shard_map/ppermute | solution.py:19
  31.4 13.5 %collective-permute-start.4 = (f32[16]{0:T(128)S(1)}, f32[16]{0:T(128)S(1)}, u32[]{:S(2)}, u32[]{:S(2)}) collective-permute-start(f32[16]{0:T(128)S(1)} %get-tuple-element.39), channel_id=1, source_target_pairs={{0,8},{4,12},{8,16},{12,20},{16,24},{20,28},{24,32},{28,36},{32,40... | collective-permute-start | bytes 200 | tf_op jit(solution)/shard_map/ppermute | solution.py:19
  39.7 17.5 %collective-permute-start.7 = (bf16[16,64,128]{2,1,0:T(8,128)(2,1)S(1)}, bf16[16,64,128]{2,1,0:T(8,128)(2,1)S(1)}, u32[]{:S(2)}, u32[]{:S(2)}) collective-permute-start(bf16[16,64,128]{2,1,0:T(8,128)(2,1)S(1)} %get-tuple-element.73), channel_id=1, source_target_pairs={{0,8},{4,12},{8,16},{12,20},{16,24},{20,28},{24,32},{28,36},{32,40... | collective-permute-start | bytes 786440 | tf_op jit(solution)/shard_map/ppermute | solution.py:19
  41.7 15.4 %collective-permute-start.8 = (bf16[16,64,128]{2,1,0:T(8,128)(2,1)S(1)}, bf16[16,64,128]{2,1,0:T(8,128)(2,1)S(1)}, u32[]{:S(2)}, u32[]{:S(2)}) collective-permute-start(bf16[16,64,128]{2,1,0:T(8,128)(2,1)S(1)} %get-tuple-element.73), channel_id=1, source_target_pairs={{0,4},{4,8},{8,12},{12,16},{16,20},{20,24},{24,28},{28,32},{32,36}... | collective-permute-start | bytes 786440 | tf_op jit(solution)/shard_map/ppermute | solution.py:19
  45.4 6.7 %collective-permute-start.5 = (f32[16]{0:T(128)S(1)}, f32[16]{0:T(128)S(1)}, u32[]{:S(2)}, u32[]{:S(2)}) collective-permute-start(f32[16]{0:T(128)S(1)} %get-tuple-element.37), channel_id=1, source_target_pairs={{0,16},{4,20},{8,24},{12,28},{16,32},{20,36},{24,40},{28,44},{32,4... | collective-permute-start | bytes 200 | tf_op jit(solution)/shard_map/ppermute | solution.py:19
  52.6 8.5 %collective-permute-start.6 = (f32[16]{0:T(128)S(1)}, f32[16]{0:T(128)S(1)}, u32[]{:S(2)}, u32[]{:S(2)}) collective-permute-start(f32[16]{0:T(128)S(1)} %get-tuple-element.35), channel_id=1, source_target_pairs={{0,32},{4,36},{8,40},{12,44},{16,48},{20,52},{24,56},{28,60},{32,6... | collective-permute-start | bytes 200 | tf_op jit(solution)/shard_map/ppermute | solution.py:19
  57.3 9.3 %collective-permute-start.9 = (bf16[16,64,128]{2,1,0:T(8,128)(2,1)S(1)}, bf16[16,64,128]{2,1,0:T(8,128)(2,1)S(1)}, u32[]{:S(2)}, u32[]{:S(2)}) collective-permute-start(bf16[16,64,128]{2,1,0:T(8,128)(2,1)S(1)} %fusion.73), channel_id=1, source_target_pairs={{0,8},{4,12},{8,16},{12,20},{16,24},{20,28},{24,32},{28,36},{32,40... | collective-permute-start | bytes 786440 | tf_op jit(solution)/shard_map/ppermute | solution.py:19
  67.6 9.1 %collective-permute-start.10 = (bf16[16,64,128]{2,1,0:T(8,128)(2,1)S(1)}, bf16[16,64,128]{2,1,0:T(8,128)(2,1)S(1)}, u32[]{:S(2)}, u32[]{:S(2)}) collective-permute-start(bf16[16,64,128]{2,1,0:T(8,128)(2,1)S(1)} %fusion.137), channel_id=1, source_target_pairs={{0,16},{4,20},{8,24},{12,28},{16,32},{20,36},{24,40},{28,44},{32,4... | collective-permute-start | bytes 786440 | tf_op jit(solution)/shard_map/ppermute | solution.py:19
  78.4 15.2 %collective-permute-start.11 = (bf16[16,64,128]{2,1,0:T(8,128)(2,1)}, bf16[16,64,128]{2,1,0:T(8,128)(2,1)}, u32[]{:S(2)}, u32[]{:S(2)}) collective-permute-start(bf16[16,64,128]{2,1,0:T(8,128)(2,1)} %fusion.74), channel_id=1, source_target_pairs={{0,32},{4,36},{8,40},{12,44},{16,48},{20,52},{24,56},{28,60},{32,6... | collective-permute-start | bytes 786440 | tf_op jit(solution)/shard_map/ppermute | solution.py:19
  95.0 6.3 %collective-permute-start.12 = (bf16[16,64,128]{2,1,0:T(8,128)(2,1)S(1)}, bf16[16,64,128]{2,1,0:T(8,128)(2,1)S(1)}, u32[]{:S(2)}, u32[]{:S(2)}) collective-permute-start(bf16[16,64,128]{2,1,0:T(8,128)(2,1)S(1)} %get-tuple-element.32), channel_id=1, source_target_pairs={{0,64},{4,68},{8,72},{12,76},{16,80},{20,84},{24,88},{28,92},{32,9... | collective-permute-start | bytes 786440 | tf_op jit(solution)/shard_map/ppermute | solution.py:19
  113.1 29.2 %collective-permute-start.13 = (bf16[544,1024]{1,0:T(8,128)(2,1)}, bf16[544,1024]{1,0:T(8,128)(2,1)S(1)}, u32[]{:S(2)}, u32[]{:S(2)}) collective-permute-start(bf16[544,1024]{1,0:T(8,128)(2,1)} %fusion.19), channel_id=1, source_target_pairs={{0,2},{1,3},{2,0},{3,1},{4,6},{5,7},{6,4},{7,5},{8,10},{9,11},{10,... | collective-permute-start | bytes 3342344 | tf_op jit(solution)/shard_map/ppermute | solution.py:229
  119.3 43.1 %collective-permute-start.14 = (bf16[544,1024]{1,0:T(8,128)(2,1)}, bf16[544,1024]{1,0:T(8,128)(2,1)S(1)}, u32[]{:S(2)}, u32[]{:S(2)}) collective-permute-start(bf16[544,1024]{1,0:T(8,128)(2,1)} %fusion.22), channel_id=1, source_target_pairs={{0,1},{1,2},{2,3},{3,0},{4,5},{5,6},{6,7},{7,4},{8,9},{9,10},{10,1... | collective-permute-start | bytes 3342344 | tf_op jit(solution)/shard_map/ppermute | solution.py:229
  123.3 40.2 %collective-permute-start.15 = (bf16[544,1024]{1,0:T(8,128)(2,1)}, bf16[544,1024]{1,0:T(8,128)(2,1)}, u32[]{:S(2)}, u32[]{:S(2)}) collective-permute-start(bf16[544,1024]{1,0:T(8,128)(2,1)} %fusion.25), channel_id=1, source_target_pairs={{0,3},{1,0},{2,1},{3,2},{4,7},{5,4},{6,5},{7,6},{8,11},{9,8},{10,9... | collective-permute-start | bytes 3342344 | tf_op jit(solution)/shard_map/ppermute | solution.py:229
  168.9 5.0 %collective-permute-start.17 = (bf16[6,1024]{1,0:T(8,128)(2,1)S(1)}, bf16[6,1024]{1,0:T(8,128)(2,1)S(1)}, u32[]{:S(2)}, u32[]{:S(2)}) collective-permute-start(bf16[6,1024]{1,0:T(8,128)(2,1)S(1)} %maximum_select_fusion.7), channel_id=1, source_target_pairs={{0,8},{4,12},{8,0},{12,4},{16,24},{20,28},{24,16},{28,20},{32,40},... | collective-permute-start | bytes 36872 | tf_op jit(solution)/shard_map/ppermute | solution.py:24
  174.0 5.5 %collective-permute-start.18 = (bf16[12,1024]{1,0:T(8,128)(2,1)S(1)}, bf16[12,1024]{1,0:T(8,128)(2,1)S(1)}, u32[]{:S(2)}, u32[]{:S(2)}) collective-permute-start(bf16[12,1024]{1,0:T(8,128)(2,1)S(1)} %maximum_select_fusion.6), channel_id=1, source_target_pairs={{0,16},{4,20},{8,24},{12,28},{16,0},{20,4},{24,8},{28,12},{32,48},... | collective-permute-start | bytes 73736 | tf_op jit(solution)/shard_map/ppermute | solution.py:24
  183.7 6.7 %collective-permute-start.20 = (bf16[48,1024]{1,0:T(8,128)(2,1)S(1)}, bf16[48,1024]{1,0:T(8,128)(2,1)S(1)}, u32[]{:S(2)}, u32[]{:S(2)}) collective-permute-start(bf16[48,1024]{1,0:T(8,128)(2,1)S(1)} %maximum_select_fusion.4), channel_id=1, source_target_pairs={{0,64},{4,68},{8,72},{12,76},{16,80},{20,84},{24,88},{28,92},{32,9... | collective-permute-start | bytes 294920 | tf_op jit(solution)/shard_map/ppermute | solution.py:24
  190.4 6.0 %collective-permute-start.21 = (bf16[96,1024]{1,0:T(8,128)(2,1)S(1)}, bf16[96,1024]{1,0:T(8,128)(2,1)S(1)}, u32[]{:S(2)}, u32[]{:S(2)}) collective-permute-start(bf16[96,1024]{1,0:T(8,128)(2,1)S(1)} %maximum_select_fusion.3), channel_id=1, source_target_pairs={{0,1},{1,0},{2,3},{3,2},{4,5},{5,4},{6,7},{7,6},{8,9},{9,8},{10,11... | collective-permute-start | bytes 589832 | tf_op jit(solution)/shard_map/ppermute | solution.py:24
  196.5 9.6 %collective-permute-start.22 = (bf16[96,2048]{1,0:T(8,128)(2,1)S(1)}, bf16[96,2048]{1,0:T(8,128)(2,1)S(1)}, u32[]{:S(2)}, u32[]{:S(2)}) collective-permute-start(bf16[96,2048]{1,0:T(8,128)(2,1)S(1)} %maximum_select_fusion.2), channel_id=1, source_target_pairs={{0,2},{1,3},{2,0},{3,1},{4,6},{5,7},{6,4},{7,5},{8,10},{9,11},{10,... | collective-permute-start | bytes 1179656 | tf_op jit(solution)/shard_map/ppermute | solution.py:24
  218.8 5.1 %collective-permute-start.24 = (f32[65]{0:T(128)S(1)}, f32[65]{0:T(128)S(1)}, u32[]{:S(2)}, u32[]{:S(2)}) collective-permute-start(f32[65]{0:T(128)S(1)} %max.41), channel_id=1, source_target_pairs={{0,2},{1,3},{2,0},{3,1},{4,6},{5,7},{6,4},{7,5},{8,10},{9,11},{10,... | collective-permute-start | bytes 788 | tf_op jit(solution)/shard_map/ppermute | solution.py:24
  229.1 5.1 %collective-permute-start.27 = (f32[65]{0:T(128)S(1)}, f32[65]{0:T(128)S(1)}, u32[]{:S(2)}, u32[]{:S(2)}) collective-permute-start(f32[65]{0:T(128)S(1)} %max.44), channel_id=1, source_target_pairs={{0,16},{4,20},{8,24},{12,28},{16,0},{20,4},{24,8},{28,12},{32,48},... | collective-permute-start | bytes 788 | tf_op jit(solution)/shard_map/ppermute | solution.py:24
  237.8 6.4 %collective-permute-start.29 = (f32[65]{0:T(128)S(1)}, f32[65]{0:T(128)S(1)}, u32[]{:S(2)}, u32[]{:S(2)}) collective-permute-start(f32[65]{0:T(128)S(1)} %max.46), channel_id=1, source_target_pairs={{0,64},{4,68},{8,72},{12,76},{16,80},{20,84},{24,88},{28,92},{32,9... | collective-permute-start | bytes 788 | tf_op jit(solution)/shard_map/ppermute | solution.py:24
  (63 other events, 689.9 us)

commit v2 on v1

--- a/solution.py
+++ b/solution.py
@@ -43,6 +43,50 @@
     while distance < lax.axis_size(axis):
         block = jnp.maximum(block, swapped(block, axis, distance))
         distance *= 2
+    return block
+
+
+def digit_route(count, distance, step, radix):
+    route = []
+    for i in range(count):
+        digit = (i // distance) % radix
+        route.append((i, i + ((digit + step) % radix - digit) * distance))
+    return route
+
+
+def gather_fast(block, axis, dim):
+    count = lax.axis_size(axis)
+    index = lax.axis_index(axis)
+    distance = 1
+    while distance < count:
+        radix = min(4, count // distance)
+        digit = (index // distance) % radix
+        got = [block] + [
+            lax.ppermute(block, axis, digit_route(count, distance, step, radix))
+            for step in range(1, radix)
+        ]
+        stacked = jnp.stack(got)
+        parts = [
+            lax.dynamic_index_in_dim(stacked, (digit - part) % radix, 0, keepdims=False)
+            for part in range(radix)
+        ]
+        block = jnp.concatenate(parts, dim)
+        distance *= radix
+    return block
+
+
+def max_fast(block, axis):
+    count = lax.axis_size(axis)
+    distance = 1
+    while distance < count:
+        radix = min(4, count // distance)
+        got = [
+            lax.ppermute(block, axis, digit_route(count, distance, step, radix))
+            for step in range(1, radix)
+        ]
+        for other in got:
+            block = jnp.maximum(block, other)
+        distance *= radix
     return block
 
 
@@ -240,8 +284,8 @@
         "rs,rsd->rd", last_pick, hidden_short.astype(jnp.float32), precision=lax.Precision.HIGHEST
     ).astype(jnp.bfloat16)
     packed = jnp.concatenate([short_rows, hidden_long[tok_rows - 1 :]], 0)
-    seq_rows = gather_all(packed, "seq", 0)
-    full_rows = gather_all(seq_rows, "tp", 1)
+    seq_rows = gather_fast(packed, "seq", 0)
+    full_rows = gather_fast(seq_rows, "tp", 1)
     seq_count = lax.axis_size("seq")
     shaped = full_rows.reshape(seq_count, req_count + 1, D)
     long_row = shaped[seq_count - 1, req_count][None]
@@ -255,7 +299,7 @@
     logits = lax.dot_general(
         last_norm, head_weight, (((1,), (1,)), ((), ())), preferred_element_type=jnp.float32
     )
-    top_logit = max_all(max_all(jnp.max(logits, axis=1), "tp"), "seq")
+    top_logit = max_fast(max_fast(jnp.max(logits, axis=1), "tp"), "seq")
     return (
         hidden_long,
         hidden_short,

time: 247 us -> 236 us (0.955)
  waiting for transfers between devices: 80.9 us -> 61.6 us
  starting transfers between devices: 79.6 us -> 89.6 us
    ppermute x14 -> x20, waiting for transfers between devices: 35.2 us -> 16.8 us  [the longest x10 11.7 us: gather_fast(): lax.ppermute(block, axis, digit_route(count, distance, step, radix))]
    ppermute x14 -> x20, starting transfers between devices: 25.7 us -> 35.6 us  [the longest x10 18.1 us: gather_fast(): lax.ppermute(block, axis, digit_route(count, distance, step, radix))]
  transfers between devices with their start and end apart: 30 -> 36, of which waited for: 18 -> 18; matrix products, arithmetic and copies ran while one was open for 20% -> 20% of each run, Pallas kernels for 0% -> 0%
where the time goes in v2:
time: 236 us; the launch traced here: 233 us
  starting transfers between devices  89.6 us (38%)
  waiting for transfers between devices  61.6 us (26%)
  matrix products  41.8 us (18%)
  other arithmetic  22.9 us (10%)
  local copies, waits for them, and re-layouts  15.2 us (6%)
    ppermute x13, starting transfers between devices, passed_along(): return lax.ppermute(block, axis, route)  49.6 us
    ppermute x3, waiting for transfers between devices, local(): lax.ppermute(term, 'tp', [(i, (i + step) % tp_count) for i in range(tp_co...  36.8 us
    ppermute x10, starting transfers between devices, gather_fast(): lax.ppermute(block, axis, digit_route(count, distance, step, radix))  18.1 us
    ppermute x10, starting transfers between devices, max_fast(): lax.ppermute(block, axis, digit_route(count, distance, step, radix))  17.5 us
    dot_general x4, matrix products, local(): jnp.dot(all_normed, piece, preferred_element_type=jnp.float32)  16.1 us
    ppermute x10, waiting for transfers between devices, gather_fast(): lax.ppermute(block, axis, digit_route(count, distance, step, radix))  11.7 us
    ppermute x13, waiting for transfers between devices, passed_along(): return lax.ppermute(block, axis, route)  8.04 us
    dot_general x3, matrix products, ssd_block(): jnp.einsum('hts,shp->thp', weights, x_block, preferred_element_type=jnp.f...  7.72 us
  transfers between devices with their start and end apart: 36, of which 18 were waited for; matrix products, arithmetic and copies ran while one was open for 20% of the time, Pallas kernels for 0%

profile of v2, /device:TPU:8, one launch (start us, length us, event | category | flops | bytes accessed | tf_op | source)
XLA Modules:
  0.0 233.0 jit_solution(13568472238115317132)
XLA Ops:
  5.6 4.0 %collective-permute-start.3 = (f32[16]{0:T(128)S(1)}, f32[16]{0:T(128)S(1)}, u32[]{:S(2)}, u32[]{:S(2)}) collective-permute-start(f32[16]{0:T(128)S(1)} %slice_reduce_fusion.5), channel_id=1, source_target_pairs={{0,8},{4,12},{8,16},{12,20},{16,24},{20,28},{24,32},{28,36},{32,40... | collective-permute-start | bytes 200 | tf_op jit(solution)/shard_map/ppermute | solution.py:19
  10.6 3.6 %collective-permute-start.1 = (bf16[3,2,128]{2,0,1:T(4,128)(2,1)S(1)}, bf16[3,2,128]{2,0,1:T(4,128)(2,1)S(1)}, u32[]{:S(2)}, u32[]{:S(2)}) collective-permute-start(bf16[3,2,128]{2,0,1:T(4,128)(2,1)S(1)} %slice.253), channel_id=1, source_target_pairs={{0,4},{4,8},{8,12},{12,16},{16,20},{20,24},{24,28},{28,32},{32,36}... | collective-permute-start | bytes 4616 | tf_op jit(solution)/shard_map/ppermute | solution.py:19
  30.2 3.5 %collective-permute-start.4 = (f32[16]{0:T(128)S(1)}, f32[16]{0:T(128)S(1)}, u32[]{:S(2)}, u32[]{:S(2)}) collective-permute-start(f32[16]{0:T(128)S(1)} %get-tuple-element.39), channel_id=1, source_target_pairs={{0,8},{4,12},{8,16},{12,20},{16,24},{20,28},{24,32},{28,36},{32,40... | collective-permute-start | bytes 200 | tf_op jit(solution)/shard_map/ppermute | solution.py:19
  44.2 5.5 %collective-permute-start.5 = (f32[16]{0:T(128)S(1)}, f32[16]{0:T(128)S(1)}, u32[]{:S(2)}, u32[]{:S(2)}) collective-permute-start(f32[16]{0:T(128)S(1)} %get-tuple-element.37), channel_id=1, source_target_pairs={{0,16},{4,20},{8,24},{12,28},{16,32},{20,36},{24,40},{28,44},{32,4... | collective-permute-start | bytes 200 | tf_op jit(solution)/shard_map/ppermute | solution.py:19
  51.4 4.5 %collective-permute-start.6 = (f32[16]{0:T(128)S(1)}, f32[16]{0:T(128)S(1)}, u32[]{:S(2)}, u32[]{:S(2)}) collective-permute-start(f32[16]{0:T(128)S(1)} %get-tuple-element.35), channel_id=1, source_target_pairs={{0,32},{4,36},{8,40},{12,44},{16,48},{20,52},{24,56},{28,60},{32,6... | collective-permute-start | bytes 200 | tf_op jit(solution)/shard_map/ppermute | solution.py:19
  56.1 3.8 %collective-permute-start.9 = (bf16[16,64,128]{2,1,0:T(8,128)(2,1)S(1)}, bf16[16,64,128]{2,1,0:T(8,128)(2,1)S(1)}, u32[]{:S(2)}, u32[]{:S(2)}) collective-permute-start(bf16[16,64,128]{2,1,0:T(8,128)(2,1)S(1)} %fusion.73), channel_id=1, source_target_pairs={{0,8},{4,12},{8,16},{12,20},{16,24},{20,28},{24,32},{28,36},{32,40... | collective-permute-start | bytes 786440 | tf_op jit(solution)/shard_map/ppermute | solution.py:19
  61.2 4.3 %collective-permute-done.9 = bf16[16,64,128]{2,1,0:T(8,128)(2,1)S(1)} collective-permute-done((bf16[16,64,128]{2,1,0:T(8,128)(2,1)S(1)}, bf16[16,64,128]{2,1,0:T(8,128)(2,1)S(1)}, u32[]{:S(2)}, u32[]{:S(2)}) %collective-permute-start.9) | collective-permute-done | bytes 262176 | tf_op jit(solution)/shard_map/ppermute | solution.py:19
  66.4 4.8 %collective-permute-start.10 = (bf16[16,64,128]{2,1,0:T(8,128)(2,1)S(1)}, bf16[16,64,128]{2,1,0:T(8,128)(2,1)S(1)}, u32[]{:S(2)}, u32[]{:S(2)}) collective-permute-start(bf16[16,64,128]{2,1,0:T(8,128)(2,1)S(1)} %fusion.144), channel_id=1, source_target_pairs={{0,16},{4,20},{8,24},{12,28},{16,32},{20,36},{24,40},{28,44},{32,4... | collective-permute-start | bytes 786440 | tf_op jit(solution)/shard_map/ppermute | solution.py:19
  71.2 3.7 %fusion.33 = f32[256,16,64]{0,2,1:T(8,128)} fusion(bf16[256,16,64]{0,2,1:T(8,128)(2,1)S(1)} %bitcast.222, f32[16,256]{1,0:T(8,128)} %get-tuple-element.95, f32[16,256]{1,0:T(8,128)} %copy-done.28, pred[256,256]{1,0:T(8,128)(4,1)} %iota_compare_fusion, bf16[256,128]{1,0:T(8,128)(2,1)} %copy-done.22, bf16[256,128]{1,0:T(8,128)(2,1)} %get-tuple-element.48), kind=kOutput, calls=%fused_computation.41 | convolution fusion | flops 408944640 | bytes 1802240 | tf_op jit(solution)/shard_map/hts,shp->thp/dot_general | solution.py:136
  77.2 8.1 %collective-permute-start.11 = (bf16[16,64,128]{2,1,0:T(8,128)(2,1)}, bf16[16,64,128]{2,1,0:T(8,128)(2,1)}, u32[]{:S(2)}, u32[]{:S(2)}) collective-permute-start(bf16[16,64,128]{2,1,0:T(8,128)(2,1)} %fusion.74), channel_id=1, source_target_pairs={{0,32},{4,36},{8,40},{12,44},{16,48},{20,52},{24,56},{28,60},{32,6... | collective-permute-start | bytes 786440 | tf_op jit(solution)/shard_map/ppermute | solution.py:19
  85.3 3.7 %fusion.34 = f32[256,16,64]{0,2,1:T(8,128)} fusion(bf16[256,16,64]{0,2,1:T(8,128)(2,1)S(1)} %bitcast.224, f32[16,256]{1,0:T(8,128)} %get-tuple-element.96, f32[16,256]{1,0:T(8,128)} %copy-done.27, pred[256,256]{1,0:T(8,128)(4,1)} %iota_compare_fusion, bf16[256,128]{1,0:T(8,128)(2,1)} %copy-done.26, bf16[256,128]{1,0:T(8,128)(2,1)S(1)} %get-tuple-element.46), kind=kOutput, calls=%fused_computation.42 | convolution fusion | flops 408944640 | bytes 1802240 | tf_op jit(solution)/shard_map/hts,shp->thp/dot_general | solution.py:136
  100.2 3.8 %fusion.10 = f32[512,16,64]{0,2,1:T(8,128)} fusion(f32[512,16,64]{0,2,1:T(8,128)S(1)} %bitcast.219, f32[512,16,64]{0,2,1:T(8,128)S(1)} %bitcast.218, f32[16]{0:T(128)S(1)} %copy-done.52, bf16[512,128]{1,0:T(8,128)(2,1)S(1)} %copy-done.17, f32[512,16]{0,1:T(8,128)S(1)} %exponential_bitcast_fusion, f32[16,64,128]{2,1,0:T(8,128)S(1)} %get-tuple-element.33, ...), kind=kOutput, calls=%fused_computation.19 | convolution fusion | flops 807796736 | bytes 7241856 | tf_op jit(solution)/shard_map/thn,hpn->thp/dot_general | solution.py:208
  107.5 4.3 %fusion.19 = bf16[544,1024]{1,0:T(8,128)(2,1)} fusion(bf16[1024,4096]{1,0:T(8,128)(2,1)} %param.37, s32[]{:T(128)S(6)} %select_n.193, bf16[32,1024]{1,0:T(8,128)(2,1)S(1)} %copy-done.25, bf16[512,1024]{1,0:T(8,128)(2,1)S(1)} %multiply_convert_fusion.2), kind=kOutput, calls=%fused_computation.31 | convolution fusion | flops 1143635968 | bytes 4325380 | tf_op jit(solution)/shard_map/dot_general | solution.py:271
  114.1 3.9 %fusion.22 = bf16[544,1024]{1,0:T(8,128)(2,1)} fusion(bf16[1024,4096]{1,0:T(8,128)(2,1)} %param.37, s32[]{:T(128)S(6)} %select_n.195, bf16[32,1024]{1,0:T(8,128)(2,1)S(1)} %copy-done.25, bf16[512,1024]{1,0:T(8,128)(2,1)S(1)} %multiply_convert_fusion.2), kind=kOutput, calls=%fused_computation.32 | convolution fusion | flops 1143635968 | bytes 4325380 | tf_op jit(solution)/shard_map/dot_general | solution.py:271
  118.1 4.0 %fusion.25 = bf16[544,1024]{1,0:T(8,128)(2,1)} fusion(bf16[1024,4096]{1,0:T(8,128)(2,1)} %param.37, s32[]{:T(128)S(6)} %select_n.197, bf16[32,1024]{1,0:T(8,128)(2,1)S(1)} %copy-done.25, bf16[512,1024]{1,0:T(8,128)(2,1)S(1)} %multiply_convert_fusion.2), kind=kOutput, calls=%fused_computation.33 | convolution fusion | flops 1143635968 | bytes 4325380 | tf_op jit(solution)/shard_map/dot_general | solution.py:271
  124.5 16.5 %collective-permute-done.13 = bf16[544,1024]{1,0:T(8,128)(2,1)S(1)} collective-permute-done((bf16[544,1024]{1,0:T(8,128)(2,1)}, bf16[544,1024]{1,0:T(8,128)(2,1)S(1)}, u32[]{:S(2)}, u32[]{:S(2)}) %collective-permute-start.13) | collective-permute-done | bytes 1114144 | tf_op jit(solution)/shard_map/ppermute | solution.py:273
  141.0 20.2 %collective-permute-done.14 = bf16[544,1024]{1,0:T(8,128)(2,1)} collective-permute-done((bf16[544,1024]{1,0:T(8,128)(2,1)}, bf16[544,1024]{1,0:T(8,128)(2,1)}, u32[]{:S(2)}, u32[]{:S(2)}) %collective-permute-start.14) | collective-permute-done | bytes 1114144 | tf_op jit(solution)/shard_map/ppermute | solution.py:273
  161.3 3.9 %add_convert_fusion = bf16[544,1024]{1,0:T(8,128)(2,1)S(1)} fusion(bf16[544,1024]{1,0:T(8,128)(2,1)} %collective-permute-done.15, bf16[544,1024]{1,0:T(8,128)(2,1)} %collective-permute-done.14, bf16[544,1024]{1,0:T(8,128)(2,1)S(1)} %collective-permute-done.13, bf16[1024,4096]{1,0:T(8,128)(2,1)} %param.37, s32[]{:T(128)S(6)} %select_n.199, ...), kind=kOutput, calls=%fused_computation.6 | convolution fusion | flops 1148092416 | bytes 7667716 | tf_op jit(solution)/shard_map/dot_general | solution.py:271
  165.5 3.3 %collective-permute-start.17 = (bf16[3,1024]{1,0:T(4,128)(2,1)S(1)}, bf16[3,1024]{1,0:T(4,128)(2,1)S(1)}, u32[]{:S(2)}, u32[]{:S(2)}) collective-permute-start(bf16[3,1024]{1,0:T(4,128)(2,1)S(1)} %get-tuple-element.79), channel_id=1, source_target_pairs={{0,8},{4,12},{8,0},{12,4},{16,24},{20,28},{24,16},{28,20},{32,40},... | collective-permute-start | bytes 18440 | tf_op jit(solution)/shard_map/ppermute | solution.py:65
  172.4 3.8 %collective-permute-start.21 = (bf16[12,1024]{1,0:T(8,128)(2,1)S(1)}, bf16[12,1024]{1,0:T(8,128)(2,1)S(1)}, u32[]{:S(2)}, u32[]{:S(2)}) collective-permute-start(bf16[12,1024]{1,0:T(8,128)(2,1)S(1)} %get-tuple-element.59), channel_id=1, source_target_pairs={{0,48},{4,52},{8,56},{12,60},{16,0},{20,4},{24,8},{28,12},{32,16},... | collective-permute-start | bytes 73736 | tf_op jit(solution)/shard_map/ppermute | solution.py:65
  178.7 4.1 %collective-permute-start.22 = (bf16[48,1024]{1,0:T(8,128)(2,1)S(1)}, bf16[48,1024]{1,0:T(8,128)(2,1)S(1)}, u32[]{:S(2)}, u32[]{:S(2)}) collective-permute-start(bf16[48,1024]{1,0:T(8,128)(2,1)S(1)} %pad_maximum_fusion.7), channel_id=1, source_target_pairs={{0,64},{4,68},{8,72},{12,76},{16,80},{20,84},{24,88},{28,92},{32,9... | collective-permute-start | bytes 294920 | tf_op jit(solution)/shard_map/ppermute | solution.py:65
  199.8 6.4 %convolution_reduce_fusion = f32[65]{0:T(128)S(1)} fusion(bf16[65,4096]{1,0:T(8,128)(2,1)S(1)} %fusion.43, bf16[1024,4096]{1,0:T(8,128)(2,1)} %param.39), kind=kOutput, calls=%fused_computation.65 | convolution fusion | flops 545326016 | bytes 8921348 | tf_op jit(solution)/shard_map/dot_general | solution.py:299
  218.2 3.9 %collective-permute-start.32 = (f32[65]{0:T(128)S(1)}, f32[65]{0:T(128)S(1)}, u32[]{:S(2)}, u32[]{:S(2)}) collective-permute-start(f32[65]{0:T(128)S(1)} %maximum_maximum_fusion.1), channel_id=1, source_target_pairs={{0,16},{4,20},{8,24},{12,28},{16,32},{20,36},{24,40},{28,44},{32,4... | collective-permute-start | bytes 788 | tf_op jit(solution)/shard_map/ppermute | solution.py:84
  227.2 3.3 %collective-permute-start.35 = (f32[65]{0:T(128)S(1)}, f32[65]{0:T(128)S(1)}, u32[]{:S(2)}, u32[]{:S(2)}) collective-permute-start(f32[65]{0:T(128)S(1)} %maximum_maximum_fusion), channel_id=1, source_target_pairs={{0,64},{4,68},{8,72},{12,76},{16,80},{20,84},{24,88},{28,92},{32,9... | collective-permute-start | bytes 788 | tf_op jit(solution)/shard_map/ppermute | solution.py:84
  (291 shorter events, 100.3 us)
Async XLA Ops:
  3.9 25.8 %collective-permute-start.2 = (f32[16]{0:T(128)S(1)}, f32[16]{0:T(128)S(1)}, u32[]{:S(2)}, u32[]{:S(2)}) collective-permute-start(f32[16]{0:T(128)S(1)} %slice_reduce_fusion.5), channel_id=1, source_target_pairs={{0,4},{4,8},{8,12},{12,16},{16,20},{20,24},{24,28},{28,32},{32,36}... | collective-permute-start | bytes 200 | tf_op jit(solution)/shard_map/ppermute | solution.py:19
  5.6 24.0 %collective-permute-start.3 = (f32[16]{0:T(128)S(1)}, f32[16]{0:T(128)S(1)}, u32[]{:S(2)}, u32[]{:S(2)}) collective-permute-start(f32[16]{0:T(128)S(1)} %slice_reduce_fusion.5), channel_id=1, source_target_pairs={{0,8},{4,12},{8,16},{12,20},{16,24},{20,28},{24,32},{28,36},{32,40... | collective-permute-start | bytes 200 | tf_op jit(solution)/shard_map/ppermute | solution.py:19
  10.6 23.1 %collective-permute-start.1 = (bf16[3,2,128]{2,0,1:T(4,128)(2,1)S(1)}, bf16[3,2,128]{2,0,1:T(4,128)(2,1)S(1)}, u32[]{:S(2)}, u32[]{:S(2)}) collective-permute-start(bf16[3,2,128]{2,0,1:T(4,128)(2,1)S(1)} %slice.253), channel_id=1, source_target_pairs={{0,4},{4,8},{8,12},{12,16},{16,20},{20,24},{24,28},{28,32},{32,36}... | collective-permute-start | bytes 4616 | tf_op jit(solution)/shard_map/ppermute | solution.py:19
  15.0 19.8 %collective-permute-start = (bf16[3,1024]{1,0:T(4,128)(2,1)S(1)}, bf16[3,1024]{1,0:T(4,128)(2,1)S(1)}, u32[]{:S(2)}, u32[]{:S(2)}) collective-permute-start(bf16[3,1024]{1,0:T(4,128)(2,1)S(1)} %slice.193), channel_id=1, source_target_pairs={{0,4},{4,8},{8,12},{12,16},{16,20},{20,24},{24,28},{28,32},{32,36}... | collective-permute-start | bytes 18440 | tf_op jit(solution)/shard_map/ppermute | solution.py:19
  30.2 13.4 %collective-permute-start.4 = (f32[16]{0:T(128)S(1)}, f32[16]{0:T(128)S(1)}, u32[]{:S(2)}, u32[]{:S(2)}) collective-permute-start(f32[16]{0:T(128)S(1)} %get-tuple-element.39), channel_id=1, source_target_pairs={{0,8},{4,12},{8,16},{12,20},{16,24},{20,28},{24,32},{28,36},{32,40... | collective-permute-start | bytes 200 | tf_op jit(solution)/shard_map/ppermute | solution.py:19
  38.4 17.5 %collective-permute-start.7 = (bf16[16,64,128]{2,1,0:T(8,128)(2,1)S(1)}, bf16[16,64,128]{2,1,0:T(8,128)(2,1)S(1)}, u32[]{:S(2)}, u32[]{:S(2)}) collective-permute-start(bf16[16,64,128]{2,1,0:T(8,128)(2,1)S(1)} %get-tuple-element.93), channel_id=1, source_target_pairs={{0,8},{4,12},{8,16},{12,20},{16,24},{20,28},{24,32},{28,36},{32,40... | collective-permute-start | bytes 786440 | tf_op jit(solution)/shard_map/ppermute | solution.py:19
  40.5 15.5 %collective-permute-start.8 = (bf16[16,64,128]{2,1,0:T(8,128)(2,1)S(1)}, bf16[16,64,128]{2,1,0:T(8,128)(2,1)S(1)}, u32[]{:S(2)}, u32[]{:S(2)}) collective-permute-start(bf16[16,64,128]{2,1,0:T(8,128)(2,1)S(1)} %get-tuple-element.93), channel_id=1, source_target_pairs={{0,4},{4,8},{8,12},{12,16},{16,20},{20,24},{24,28},{28,32},{32,36}... | collective-permute-start | bytes 786440 | tf_op jit(solution)/shard_map/ppermute | solution.py:19
  44.2 6.7 %collective-permute-start.5 = (f32[16]{0:T(128)S(1)}, f32[16]{0:T(128)S(1)}, u32[]{:S(2)}, u32[]{:S(2)}) collective-permute-start(f32[16]{0:T(128)S(1)} %get-tuple-element.37), channel_id=1, source_target_pairs={{0,16},{4,20},{8,24},{12,28},{16,32},{20,36},{24,40},{28,44},{32,4... | collective-permute-start | bytes 200 | tf_op jit(solution)/shard_map/ppermute | solution.py:19
  51.4 8.5 %collective-permute-start.6 = (f32[16]{0:T(128)S(1)}, f32[16]{0:T(128)S(1)}, u32[]{:S(2)}, u32[]{:S(2)}) collective-permute-start(f32[16]{0:T(128)S(1)} %get-tuple-element.35), channel_id=1, source_target_pairs={{0,32},{4,36},{8,40},{12,44},{16,48},{20,52},{24,56},{28,60},{32,6... | collective-permute-start | bytes 200 | tf_op jit(solution)/shard_map/ppermute | solution.py:19
  56.1 9.3 %collective-permute-start.9 = (bf16[16,64,128]{2,1,0:T(8,128)(2,1)S(1)}, bf16[16,64,128]{2,1,0:T(8,128)(2,1)S(1)}, u32[]{:S(2)}, u32[]{:S(2)}) collective-permute-start(bf16[16,64,128]{2,1,0:T(8,128)(2,1)S(1)} %fusion.73), channel_id=1, source_target_pairs={{0,8},{4,12},{8,16},{12,20},{16,24},{20,28},{24,32},{28,36},{32,40... | collective-permute-start | bytes 786440 | tf_op jit(solution)/shard_map/ppermute | solution.py:19
  66.4 9.1 %collective-permute-start.10 = (bf16[16,64,128]{2,1,0:T(8,128)(2,1)S(1)}, bf16[16,64,128]{2,1,0:T(8,128)(2,1)S(1)}, u32[]{:S(2)}, u32[]{:S(2)}) collective-permute-start(bf16[16,64,128]{2,1,0:T(8,128)(2,1)S(1)} %fusion.144), channel_id=1, source_target_pairs={{0,16},{4,20},{8,24},{12,28},{16,32},{20,36},{24,40},{28,44},{32,4... | collective-permute-start | bytes 786440 | tf_op jit(solution)/shard_map/ppermute | solution.py:19
  77.2 15.2 %collective-permute-start.11 = (bf16[16,64,128]{2,1,0:T(8,128)(2,1)}, bf16[16,64,128]{2,1,0:T(8,128)(2,1)}, u32[]{:S(2)}, u32[]{:S(2)}) collective-permute-start(bf16[16,64,128]{2,1,0:T(8,128)(2,1)} %fusion.74), channel_id=1, source_target_pairs={{0,32},{4,36},{8,40},{12,44},{16,48},{20,52},{24,56},{28,60},{32,6... | collective-permute-start | bytes 786440 | tf_op jit(solution)/shard_map/ppermute | solution.py:19
  93.8 6.4 %collective-permute-start.12 = (bf16[16,64,128]{2,1,0:T(8,128)(2,1)S(1)}, bf16[16,64,128]{2,1,0:T(8,128)(2,1)S(1)}, u32[]{:S(2)}, u32[]{:S(2)}) collective-permute-start(bf16[16,64,128]{2,1,0:T(8,128)(2,1)S(1)} %get-tuple-element.32), channel_id=1, source_target_pairs={{0,64},{4,68},{8,72},{12,76},{16,80},{20,84},{24,88},{28,92},{32,9... | collective-permute-start | bytes 786440 | tf_op jit(solution)/shard_map/ppermute | solution.py:19
  111.8 29.2 %collective-permute-start.13 = (bf16[544,1024]{1,0:T(8,128)(2,1)}, bf16[544,1024]{1,0:T(8,128)(2,1)S(1)}, u32[]{:S(2)}, u32[]{:S(2)}) collective-permute-start(bf16[544,1024]{1,0:T(8,128)(2,1)} %fusion.19), channel_id=1, source_target_pairs={{0,2},{1,3},{2,0},{3,1},{4,6},{5,7},{6,4},{7,5},{8,10},{9,11},{10,... | collective-permute-start | bytes 3342344 | tf_op jit(solution)/shard_map/ppermute | solution.py:273
  118.0 43.2 %collective-permute-start.14 = (bf16[544,1024]{1,0:T(8,128)(2,1)}, bf16[544,1024]{1,0:T(8,128)(2,1)}, u32[]{:S(2)}, u32[]{:S(2)}) collective-permute-start(bf16[544,1024]{1,0:T(8,128)(2,1)} %fusion.22), channel_id=1, source_target_pairs={{0,1},{1,2},{2,3},{3,0},{4,5},{5,6},{6,7},{7,4},{8,9},{9,10},{10,1... | collective-permute-start | bytes 3342344 | tf_op jit(solution)/shard_map/ppermute | solution.py:273
  122.1 39.2 %collective-permute-start.15 = (bf16[544,1024]{1,0:T(8,128)(2,1)}, bf16[544,1024]{1,0:T(8,128)(2,1)}, u32[]{:S(2)}, u32[]{:S(2)}) collective-permute-start(bf16[544,1024]{1,0:T(8,128)(2,1)} %fusion.25), channel_id=1, source_target_pairs={{0,3},{1,0},{2,1},{3,2},{4,7},{5,4},{6,5},{7,6},{8,11},{9,8},{10,9... | collective-permute-start | bytes 3342344 | tf_op jit(solution)/shard_map/ppermute | solution.py:273
  171.7 6.5 %collective-permute-start.19 = (bf16[12,1024]{1,0:T(8,128)(2,1)S(1)}, bf16[12,1024]{1,0:T(8,128)(2,1)S(1)}, u32[]{:S(2)}, u32[]{:S(2)}) collective-permute-start(bf16[12,1024]{1,0:T(8,128)(2,1)S(1)} %get-tuple-element.59), channel_id=1, source_target_pairs={{0,16},{4,20},{8,24},{12,28},{16,32},{20,36},{24,40},{28,44},{32,4... | collective-permute-start | bytes 73736 | tf_op jit(solution)/shard_map/ppermute | solution.py:65
  172.2 5.9 %collective-permute-start.20 = (bf16[12,1024]{1,0:T(8,128)(2,1)S(1)}, bf16[12,1024]{1,0:T(8,128)(2,1)S(1)}, u32[]{:S(2)}, u32[]{:S(2)}) collective-permute-start(bf16[12,1024]{1,0:T(8,128)(2,1)S(1)} %get-tuple-element.59), channel_id=1, source_target_pairs={{0,32},{4,36},{8,40},{12,44},{16,48},{20,52},{24,56},{28,60},{32,0... | collective-permute-start | bytes 73736 | tf_op jit(solution)/shard_map/ppermute | solution.py:65
  172.4 6.2 %collective-permute-start.21 = (bf16[12,1024]{1,0:T(8,128)(2,1)S(1)}, bf16[12,1024]{1,0:T(8,128)(2,1)S(1)}, u32[]{:S(2)}, u32[]{:S(2)}) collective-permute-start(bf16[12,1024]{1,0:T(8,128)(2,1)S(1)} %get-tuple-element.59), channel_id=1, source_target_pairs={{0,48},{4,52},{8,56},{12,60},{16,0},{20,4},{24,8},{28,12},{32,16},... | collective-permute-start | bytes 73736 | tf_op jit(solution)/shard_map/ppermute | solution.py:65
  178.7 6.7 %collective-permute-start.22 = (bf16[48,1024]{1,0:T(8,128)(2,1)S(1)}, bf16[48,1024]{1,0:T(8,128)(2,1)S(1)}, u32[]{:S(2)}, u32[]{:S(2)}) collective-permute-start(bf16[48,1024]{1,0:T(8,128)(2,1)S(1)} %pad_maximum_fusion.7), channel_id=1, source_target_pairs={{0,64},{4,68},{8,72},{12,76},{16,80},{20,84},{24,88},{28,92},{32,9... | collective-permute-start | bytes 294920 | tf_op jit(solution)/shard_map/ppermute | solution.py:65
  185.5 7.8 %collective-permute-start.23 = (bf16[96,1024]{1,0:T(8,128)(2,1)S(1)}, bf16[96,1024]{1,0:T(8,128)(2,1)S(1)}, u32[]{:S(2)}, u32[]{:S(2)}) collective-permute-start(bf16[96,1024]{1,0:T(8,128)(2,1)S(1)} %get-tuple-element.51), channel_id=1, source_target_pairs={{0,1},{1,2},{2,3},{3,0},{4,5},{5,6},{6,7},{7,4},{8,9},{9,10},{10,1... | collective-permute-start | bytes 589832 | tf_op jit(solution)/shard_map/ppermute | solution.py:65
  187.0 8.8 %collective-permute-start.24 = (bf16[96,1024]{1,0:T(8,128)(2,1)S(1)}, bf16[96,1024]{1,0:T(8,128)(2,1)S(1)}, u32[]{:S(2)}, u32[]{:S(2)}) collective-permute-start(bf16[96,1024]{1,0:T(8,128)(2,1)S(1)} %get-tuple-element.51), channel_id=1, source_target_pairs={{0,2},{1,3},{2,0},{3,1},{4,6},{5,7},{6,4},{7,5},{8,10},{9,11},{10,... | collective-permute-start | bytes 589832 | tf_op jit(solution)/shard_map/ppermute | solution.py:65
  188.3 9.0 %collective-permute-start.25 = (bf16[96,1024]{1,0:T(8,128)(2,1)S(1)}, bf16[96,1024]{1,0:T(8,128)(2,1)S(1)}, u32[]{:S(2)}, u32[]{:S(2)}) collective-permute-start(bf16[96,1024]{1,0:T(8,128)(2,1)S(1)} %get-tuple-element.51), channel_id=1, source_target_pairs={{0,3},{1,0},{2,1},{3,2},{4,7},{5,4},{6,5},{7,6},{8,11},{9,8},{10,9... | collective-permute-start | bytes 589832 | tf_op jit(solution)/shard_map/ppermute | solution.py:65
  218.2 6.6 %collective-permute-start.32 = (f32[65]{0:T(128)S(1)}, f32[65]{0:T(128)S(1)}, u32[]{:S(2)}, u32[]{:S(2)}) collective-permute-start(f32[65]{0:T(128)S(1)} %maximum_maximum_fusion.1), channel_id=1, source_target_pairs={{0,16},{4,20},{8,24},{12,28},{16,32},{20,36},{24,40},{28,44},{32,4... | collective-permute-start | bytes 788 | tf_op jit(solution)/shard_map/ppermute | solution.py:84
  (65 other events, 695.7 us)

commit v3 on v2

--- a/solution.py
+++ b/solution.py
@@ -90,20 +90,37 @@
     return block
 
 
+def pack(state, log):
+    heads = log.shape[0]
+    high = log.astype(jnp.bfloat16)
+    rest = log - high.astype(jnp.float32)
+    mid = rest.astype(jnp.bfloat16)
+    low = (rest - mid.astype(jnp.float32)).astype(jnp.bfloat16)
+    lanes = state.shape[-1]
+    row = jnp.concatenate([high, mid, low, jnp.zeros((lanes - 3 * heads,), jnp.bfloat16)])
+    flat = state.astype(jnp.bfloat16).reshape(-1, lanes)
+    return jnp.concatenate([flat, row[None]], 0)
+
+
+def unpack(message, heads):
+    lanes = message.shape[-1]
+    state = message[:-1].reshape(heads, -1, lanes).astype(jnp.float32)
+    row = message[-1].astype(jnp.float32)
+    log = (row[:heads] + row[heads : 2 * heads]) + row[2 * heads : 3 * heads]
+    return log, state
+
+
 def carry_scan(total_log, local_state, axis):
-    sent = local_state.astype(jnp.bfloat16)
-    log_one, state_one = passed_along((total_log, sent), axis, 1)
-    log_two, state_two = passed_along((total_log, sent), axis, 2)
+    heads = total_log.shape[0]
+    sent = pack(local_state, total_log)
+    log_one, state_one = unpack(passed_along(sent, axis, 1), heads)
+    log_two, state_two = unpack(passed_along(sent, axis, 2), heads)
     seg_log = log_one + log_two
-    seg_state = jnp.exp(log_one)[:, None, None] * state_two.astype(jnp.float32) + state_one.astype(
-        jnp.float32
-    )
+    seg_state = jnp.exp(log_one)[:, None, None] * state_two + state_one
     distance = 2
     while distance < lax.axis_size(axis):
-        got_log, got_state = passed_along(
-            (seg_log, seg_state.astype(jnp.bfloat16)), axis, distance
-        )
-        seg_state = jnp.exp(seg_log)[:, None, None] * got_state.astype(jnp.float32) + seg_state
+        got_log, got_state = unpack(passed_along(pack(seg_state, seg_log), axis, distance), heads)
+        seg_state = jnp.exp(seg_log)[:, None, None] * got_state + seg_state
         seg_log = seg_log + got_log
         distance *= 2
     return seg_state

time: 236 us -> 236 us (level)
  starting transfers between devices: 89.6 us -> 69.2 us
  other arithmetic: 22.9 us -> 32.7 us
  local copies, waits for them, and re-layouts: 15.2 us -> 21.5 us
  matrix products: 41.8 us -> 45.3 us
    ppermute x13 -> x8, starting transfers between devices: 49.6 us -> 34.3 us  [passed_along(): return lax.ppermute(block, axis, route)]
    convert_element_type x4 -> x20, other arithmetic: 4.12 us -> 8.79 us  [the longest x4 3.96 us: pack(): flat = state.astype(jnp.bfloat16).reshape(-1, lanes)]
    ppermute x10, starting transfers between devices: 17.5 us -> 14.4 us  [max_fast(): lax.ppermute(block, axis, digit_route(count, distance, step, radix))]
    reshape x1, local copies, waits for them, and re-layouts: 0.26 us -> 3.26 us  [local(): y_blocks.reshape(tok_rows, head_count, HEADDIM) + carried]
    unnamed x114 -> x130, local copies, waits for them, and re-layouts: 3.96 us -> 6.55 us
    ppermute x10, waiting for transfers between devices: 11.7 us -> 14.3 us  [gather_fast(): lax.ppermute(block, axis, digit_route(count, distance, step, radix))]
    ppermute x13 -> x8, waiting for transfers between devices: 8.04 us -> 5.64 us  [passed_along(): return lax.ppermute(block, axis, route)]
  transfers between devices with their start and end apart: 36 -> 31, of which waited for: 18 -> 20; matrix products, arithmetic and copies ran while one was open for 20% -> 23% of each run, Pallas kernels for 0% -> 0%
where the time goes in v3:
time: 236 us; the launch traced here: 233 us
  starting transfers between devices  69.2 us (29%)
  waiting for transfers between devices  62.5 us (26%)
  matrix products  45.3 us (19%)
  other arithmetic  32.7 us (14%)
  local copies, waits for them, and re-layouts  21.5 us (9%)
    ppermute x3, waiting for transfers between devices, local(): lax.ppermute(term, 'tp', [(i, (i + step) % tp_count) for i in range(tp_co...  36.6 us
    ppermute x8, starting transfers between devices, passed_along(): return lax.ppermute(block, axis, route)  34.3 us
    dot_general x4, matrix products, local(): jnp.dot(all_normed, piece, preferred_element_type=jnp.float32)  16.4 us
    ppermute x10, starting transfers between devices, gather_fast(): lax.ppermute(block, axis, digit_route(count, distance, step, radix))  16.2 us
    ppermute x10, starting transfers between devices, max_fast(): lax.ppermute(block, axis, digit_route(count, distance, step, radix))  14.4 us
    ppermute x10, waiting for transfers between devices, gather_fast(): lax.ppermute(block, axis, digit_route(count, distance, step, radix))  14.3 us
    dot_general x3, matrix products, ssd_block(): jnp.einsum('hts,shp->thp', weights, x_block, preferred_element_type=jnp.f...  7.87 us
    unnamed x130, local copies, waits for them, and re-layouts  6.55 us
  transfers between devices with their start and end apart: 31, of which 20 were waited for; matrix products, arithmetic and copies ran while one was open for 23% of the time, Pallas kernels for 0%

profile of v3, /device:TPU:8, one launch (start us, length us, event | category | flops | bytes accessed | tf_op | source)
XLA Modules:
  0.0 233.2 jit_solution(10289531682631814733)
XLA Ops:
  4.2 4.1 %collective-permute-start = (bf16[3,1024]{1,0:T(4,128)(2,1)S(1)}, bf16[3,1024]{1,0:T(4,128)(2,1)S(1)}, u32[]{:S(2)}, u32[]{:S(2)}) collective-permute-start(bf16[3,1024]{1,0:T(4,128)(2,1)S(1)} %slice.286), channel_id=1, source_target_pairs={{0,4},{4,8},{8,12},{12,16},{16,20},{20,24},{24,28},{28,32},{32,36}... | collective-permute-start | bytes 18440 | tf_op jit(solution)/shard_map/ppermute | solution.py:19
  32.7 3.8 %collective-permute-start.3 = (bf16[1025,128]{1,0:T(8,128)(2,1)S(1)}, bf16[1025,128]{1,0:T(8,128)(2,1)S(1)}, u32[]{:S(2)}, u32[]{:S(2)}) collective-permute-start(bf16[1025,128]{1,0:T(8,128)(2,1)S(1)} %pad_maximum_fusion.4), channel_id=1, source_target_pairs={{0,8},{4,12},{8,16},{12,20},{16,24},{20,28},{24,32},{28,36},{32,40... | collective-permute-start | bytes 787208 | tf_op jit(solution)/shard_map/ppermute | solution.py:19
  38.2 3.8 %fusion.33 = f32[256,16,64]{0,2,1:T(8,128)} fusion(bf16[256,16,64]{0,2,1:T(8,128)(2,1)S(1)} %bitcast.273, f32[16,256]{1,0:T(8,128)} %get-tuple-element.112, f32[16,256]{1,0:T(8,128)} %copy-done.29, pred[256,256]{1,0:T(8,128)(4,1)} %iota_compare_fusion, bf16[256,128]{1,0:T(8,128)(2,1)} %copy-done.23, bf16[256,128]{1,0:T(8,128)(2,1)} %get-tuple-element.51), kind=kOutput, calls=%fused_computation.41 | convolution fusion | flops 408944640 | bytes 1802240 | tf_op jit(solution)/shard_map/hts,shp->thp/dot_general | solution.py:153
  42.0 3.7 %fusion.34 = f32[256,16,64]{0,2,1:T(8,128)} fusion(bf16[256,16,64]{0,2,1:T(8,128)(2,1)S(1)} %bitcast.277, f32[16,256]{1,0:T(8,128)} %get-tuple-element.113, f32[16,256]{1,0:T(8,128)} %copy-done.30, pred[256,256]{1,0:T(8,128)(4,1)} %iota_compare_fusion, bf16[256,128]{1,0:T(8,128)(2,1)} %copy-done.28, bf16[256,128]{1,0:T(8,128)(2,1)} %get-tuple-element.49), kind=kOutput, calls=%fused_computation.42 | convolution fusion | flops 408944640 | bytes 1802240 | tf_op jit(solution)/shard_map/hts,shp->thp/dot_general | solution.py:153
  48.5 3.8 %collective-permute-start.4 = (bf16[1025,128]{1,0:T(8,128)(2,1)}, bf16[1025,128]{1,0:T(8,128)(2,1)S(1)}, u32[]{:S(2)}, u32[]{:S(2)}) collective-permute-start(bf16[1025,128]{1,0:T(8,128)(2,1)} %pad_maximum_fusion.5), channel_id=1, source_target_pairs={{0,8},{4,12},{8,16},{12,20},{16,24},{20,28},{24,32},{28,36},{32,40... | collective-permute-start | bytes 787208 | tf_op jit(solution)/shard_map/ppermute | solution.py:19
  54.7 3.4 %fusion.37 = f32[1,256,16,64]{1,3,2,0:T(8,128)} fusion(f32[256,16,64]{0,2,1:T(8,128)} %fusion.33, f32[16,64,128]{2,1,0:T(8,128)S(1)} %convolution_add_fusion.2, f32[256,16]{0,1:T(8,128)} %get-tuple-element.72, bf16[256,128]{1,0:T(8,128)(2,1)} %get-tuple-element.51), kind=kOutput, calls=%fused_computation.47 | convolution fusion | flops 403177472 | bytes 2703360 | tf_op jit(solution)/shard_map/thn,hpn->thp/dot_general | solution.py:154
  61.1 6.9 %collective-permute-start.5 = (bf16[1025,128]{1,0:T(8,128)(2,1)}, bf16[1025,128]{1,0:T(8,128)(2,1)}, u32[]{:S(2)}, u32[]{:S(2)}) collective-permute-start(bf16[1025,128]{1,0:T(8,128)(2,1)} %pad_maximum_fusion.6), channel_id=1, source_target_pairs={{0,16},{4,20},{8,24},{12,28},{16,32},{20,36},{24,40},{28,44},{32,4... | collective-permute-start | bytes 787208 | tf_op jit(solution)/shard_map/ppermute | solution.py:19
  70.0 3.3 %copy.111 = f32[2,16,8,8,256]{4,3,0,2,1:T(8,128)} copy(f32[2,16,8,8,256]{4,3,2,1,0:T(8,128)} %maximum_bitcast_fusion) | data formatting | bytes 4194304 | tf_op jit(solution)/shard_map/reshape | solution.py:229
  77.3 6.5 %collective-permute-start.6 = (bf16[1025,128]{1,0:T(8,128)(2,1)}, bf16[1025,128]{1,0:T(8,128)(2,1)S(1)}, u32[]{:S(2)}, u32[]{:S(2)}) collective-permute-start(bf16[1025,128]{1,0:T(8,128)(2,1)} %pad_maximum_fusion.7), channel_id=1, source_target_pairs={{0,32},{4,36},{8,40},{12,44},{16,48},{20,52},{24,56},{28,60},{32,6... | collective-permute-start | bytes 787208 | tf_op jit(solution)/shard_map/ppermute | solution.py:19
  91.0 5.8 %collective-permute-start.7 = (bf16[1025,128]{1,0:T(8,128)(2,1)S(1)}, bf16[1025,128]{1,0:T(8,128)(2,1)S(1)}, u32[]{:S(2)}, u32[]{:S(2)}) collective-permute-start(bf16[1025,128]{1,0:T(8,128)(2,1)S(1)} %pad_maximum_fusion.8), channel_id=1, source_target_pairs={{0,64},{4,68},{8,72},{12,76},{16,80},{20,84},{24,88},{28,92},{32,9... | collective-permute-start | bytes 787208 | tf_op jit(solution)/shard_map/ppermute | solution.py:19
  102.5 3.8 %fusion.10 = f32[512,16,64]{0,2,1:T(8,128)} fusion(f32[512,16,64]{0,2,1:T(8,128)S(1)} %bitcast.265, f32[512,16,64]{0,2,1:T(8,128)S(1)} %bitcast.264, f32[16,64,128]{2,1,0:T(8,128)S(1)} %get-tuple-element.33, f32[16]{0:T(128)S(1)} %copy-done.58, bf16[512,128]{1,0:T(8,128)(2,1)S(1)} %slice_bitcast_fusion, f32[512,16]{0,1:T(8,128)S(1)} %copy-done.24), kind=kOutput, calls=%fused_computation.19 | convolution fusion | flops 807403520 | bytes 6979648 | tf_op jit(solution)/shard_map/thn,hpn->thp/dot_general | solution.py:225
  109.9 4.3 %fusion.19 = bf16[544,1024]{1,0:T(8,128)(2,1)} fusion(bf16[1024,4096]{1,0:T(8,128)(2,1)} %param.37, s32[]{:T(128)S(6)} %select_n.193, bf16[32,1024]{1,0:T(8,128)(2,1)S(1)} %copy-done.27, bf16[512,1024]{1,0:T(8,128)(2,1)S(1)} %multiply_convert_fusion.2), kind=kOutput, calls=%fused_computation.31 | convolution fusion | flops 1143635968 | bytes 4325380 | tf_op jit(solution)/shard_map/dot_general | solution.py:288
  116.5 4.0 %fusion.22 = bf16[544,1024]{1,0:T(8,128)(2,1)} fusion(bf16[1024,4096]{1,0:T(8,128)(2,1)} %param.37, s32[]{:T(128)S(6)} %select_n.195, bf16[32,1024]{1,0:T(8,128)(2,1)S(1)} %copy-done.27, bf16[512,1024]{1,0:T(8,128)(2,1)S(1)} %multiply_convert_fusion.2), kind=kOutput, calls=%fused_computation.32 | convolution fusion | flops 1143635968 | bytes 4325380 | tf_op jit(solution)/shard_map/dot_general | solution.py:288
  120.5 3.9 %fusion.25 = bf16[544,1024]{1,0:T(8,128)(2,1)} fusion(bf16[1024,4096]{1,0:T(8,128)(2,1)} %param.37, s32[]{:T(128)S(6)} %select_n.197, bf16[32,1024]{1,0:T(8,128)(2,1)S(1)} %copy-done.27, bf16[512,1024]{1,0:T(8,128)(2,1)S(1)} %multiply_convert_fusion.2), kind=kOutput, calls=%fused_computation.33 | convolution fusion | flops 1143635968 | bytes 4325380 | tf_op jit(solution)/shard_map/dot_general | solution.py:288
  126.5 16.9 %collective-permute-done.8 = bf16[544,1024]{1,0:T(8,128)(2,1)S(1)} collective-permute-done((bf16[544,1024]{1,0:T(8,128)(2,1)}, bf16[544,1024]{1,0:T(8,128)(2,1)S(1)}, u32[]{:S(2)}, u32[]{:S(2)}) %collective-permute-start.8) | collective-permute-done | bytes 1114144 | tf_op jit(solution)/shard_map/ppermute | solution.py:290
  143.4 19.7 %collective-permute-done.9 = bf16[544,1024]{1,0:T(8,128)(2,1)} collective-permute-done((bf16[544,1024]{1,0:T(8,128)(2,1)}, bf16[544,1024]{1,0:T(8,128)(2,1)}, u32[]{:S(2)}, u32[]{:S(2)}) %collective-permute-start.9) | collective-permute-done | bytes 1114144 | tf_op jit(solution)/shard_map/ppermute | solution.py:290
  163.1 4.2 %add_convert_fusion = bf16[544,1024]{1,0:T(8,128)(2,1)S(1)} fusion(bf16[544,1024]{1,0:T(8,128)(2,1)} %collective-permute-done.10, bf16[544,1024]{1,0:T(8,128)(2,1)} %collective-permute-done.9, bf16[544,1024]{1,0:T(8,128)(2,1)} %copy-done.60, bf16[1024,4096]{1,0:T(8,128)(2,1)} %param.37, s32[]{:T(128)S(6)} %select_n.199, bf16[32,1024]{1,0:T(8,128)(2,1)S(1)} %copy-done.27, ...), kind=kOutput, calls=%fused_computation.6 | convolution fusion | flops 1148092416 | bytes 7667716 | tf_op jit(solution)/shard_map/dot_general | solution.py:288
  173.4 3.2 %collective-permute-start.16 = (bf16[12,1024]{1,0:T(8,128)(2,1)S(1)}, bf16[12,1024]{1,0:T(8,128)(2,1)S(1)}, u32[]{:S(2)}, u32[]{:S(2)}) collective-permute-start(bf16[12,1024]{1,0:T(8,128)(2,1)S(1)} %get-tuple-element.62), channel_id=1, source_target_pairs={{0,48},{4,52},{8,56},{12,60},{16,0},{20,4},{24,8},{28,12},{32,16},... | collective-permute-start | bytes 73736 | tf_op jit(solution)/shard_map/ppermute | solution.py:65
  179.2 4.5 %collective-permute-start.17 = (bf16[48,1024]{1,0:T(8,128)(2,1)S(1)}, bf16[48,1024]{1,0:T(8,128)(2,1)S(1)}, u32[]{:S(2)}, u32[]{:S(2)}) collective-permute-start(bf16[48,1024]{1,0:T(8,128)(2,1)S(1)} %pad_maximum_fusion.12), channel_id=1, source_target_pairs={{0,64},{4,68},{8,72},{12,76},{16,80},{20,84},{24,88},{28,92},{32,9... | collective-permute-start | bytes 294920 | tf_op jit(solution)/shard_map/ppermute | solution.py:65
  191.4 3.0 %collective-permute-done.18 = bf16[96,1024]{1,0:T(8,128)(2,1)S(1)} collective-permute-done((bf16[96,1024]{1,0:T(8,128)(2,1)S(1)}, bf16[96,1024]{1,0:T(8,128)(2,1)S(1)}, u32[]{:S(2)}, u32[]{:S(2)}) %collective-permute-start.18) | collective-permute-done | bytes 196640 | tf_op jit(solution)/shard_map/ppermute | solution.py:65
  194.3 2.9 %collective-permute-done.19 = bf16[96,1024]{1,0:T(8,128)(2,1)S(1)} collective-permute-done((bf16[96,1024]{1,0:T(8,128)(2,1)S(1)}, bf16[96,1024]{1,0:T(8,128)(2,1)S(1)}, u32[]{:S(2)}, u32[]{:S(2)}) %collective-permute-start.19) | collective-permute-done | bytes 196640 | tf_op jit(solution)/shard_map/ppermute | solution.py:65
  201.5 6.5 %convolution_reduce_fusion = f32[65]{0:T(128)S(1)} fusion(bf16[65,4096]{1,0:T(8,128)(2,1)S(1)} %fusion.43, bf16[1024,4096]{1,0:T(8,128)(2,1)} %param.39), kind=kOutput, calls=%fused_computation.65 | convolution fusion | flops 545326016 | bytes 8921348 | tf_op jit(solution)/shard_map/dot_general | solution.py:316
  218.0 3.2 %collective-permute-start.27 = (f32[65]{0:T(128)S(1)}, f32[65]{0:T(128)S(1)}, u32[]{:S(2)}, u32[]{:S(2)}) collective-permute-start(f32[65]{0:T(128)S(1)} %maximum_maximum_fusion.1), channel_id=1, source_target_pairs={{0,16},{4,20},{8,24},{12,28},{16,32},{20,36},{24,40},{28,44},{32,4... | collective-permute-start | bytes 788 | tf_op jit(solution)/shard_map/ppermute | solution.py:84
  226.9 3.4 %collective-permute-start.30 = (f32[65]{0:T(128)S(1)}, f32[65]{0:T(128)S(1)}, u32[]{:S(2)}, u32[]{:S(2)}) collective-permute-start(f32[65]{0:T(128)S(1)} %maximum_maximum_fusion), channel_id=1, source_target_pairs={{0,64},{4,68},{8,72},{12,76},{16,80},{20,84},{24,88},{28,92},{32,9... | collective-permute-start | bytes 788 | tf_op jit(solution)/shard_map/ppermute | solution.py:84
  (333 shorter events, 102.7 us)
Async XLA Ops:
  1.7 24.4 %collective-permute-start.1 = (bf16[3,2,128]{2,0,1:T(4,128)(2,1)S(1)}, bf16[3,2,128]{2,0,1:T(4,128)(2,1)S(1)}, u32[]{:S(2)}, u32[]{:S(2)}) collective-permute-start(bf16[3,2,128]{2,0,1:T(4,128)(2,1)S(1)} %slice.372), channel_id=1, source_target_pairs={{0,4},{4,8},{8,12},{12,16},{16,20},{20,24},{24,28},{28,32},{32,36}... | collective-permute-start | bytes 4616 | tf_op jit(solution)/shard_map/ppermute | solution.py:19
  4.2 23.0 %collective-permute-start = (bf16[3,1024]{1,0:T(4,128)(2,1)S(1)}, bf16[3,1024]{1,0:T(4,128)(2,1)S(1)}, u32[]{:S(2)}, u32[]{:S(2)}) collective-permute-start(bf16[3,1024]{1,0:T(4,128)(2,1)S(1)} %slice.286), channel_id=1, source_target_pairs={{0,4},{4,8},{8,12},{12,16},{16,20},{20,24},{24,28},{28,32},{32,36}... | collective-permute-start | bytes 18440 | tf_op jit(solution)/shard_map/ppermute | solution.py:19
  32.7 13.1 %collective-permute-start.3 = (bf16[1025,128]{1,0:T(8,128)(2,1)S(1)}, bf16[1025,128]{1,0:T(8,128)(2,1)S(1)}, u32[]{:S(2)}, u32[]{:S(2)}) collective-permute-start(bf16[1025,128]{1,0:T(8,128)(2,1)S(1)} %pad_maximum_fusion.4), channel_id=1, source_target_pairs={{0,8},{4,12},{8,16},{12,20},{16,24},{20,28},{24,32},{28,36},{32,40... | collective-permute-start | bytes 787208 | tf_op jit(solution)/shard_map/ppermute | solution.py:19
  36.5 9.2 %collective-permute-start.2 = (bf16[1025,128]{1,0:T(8,128)(2,1)S(1)}, bf16[1025,128]{1,0:T(8,128)(2,1)S(1)}, u32[]{:S(2)}, u32[]{:S(2)}) collective-permute-start(bf16[1025,128]{1,0:T(8,128)(2,1)S(1)} %pad_maximum_fusion.4), channel_id=1, source_target_pairs={{0,4},{4,8},{8,12},{12,16},{16,20},{20,24},{24,28},{28,32},{32,36}... | collective-permute-start | bytes 787208 | tf_op jit(solution)/shard_map/ppermute | solution.py:19
  48.5 10.1 %collective-permute-start.4 = (bf16[1025,128]{1,0:T(8,128)(2,1)}, bf16[1025,128]{1,0:T(8,128)(2,1)S(1)}, u32[]{:S(2)}, u32[]{:S(2)}) collective-permute-start(bf16[1025,128]{1,0:T(8,128)(2,1)} %pad_maximum_fusion.5), channel_id=1, source_target_pairs={{0,8},{4,12},{8,16},{12,20},{16,24},{20,28},{24,32},{28,36},{32,40... | collective-permute-start | bytes 787208 | tf_op jit(solution)/shard_map/ppermute | solution.py:19
  61.1 13.2 %collective-permute-start.5 = (bf16[1025,128]{1,0:T(8,128)(2,1)}, bf16[1025,128]{1,0:T(8,128)(2,1)}, u32[]{:S(2)}, u32[]{:S(2)}) collective-permute-start(bf16[1025,128]{1,0:T(8,128)(2,1)} %pad_maximum_fusion.6), channel_id=1, source_target_pairs={{0,16},{4,20},{8,24},{12,28},{16,32},{20,36},{24,40},{28,44},{32,4... | collective-permute-start | bytes 787208 | tf_op jit(solution)/shard_map/ppermute | solution.py:19
  77.3 10.8 %collective-permute-start.6 = (bf16[1025,128]{1,0:T(8,128)(2,1)}, bf16[1025,128]{1,0:T(8,128)(2,1)S(1)}, u32[]{:S(2)}, u32[]{:S(2)}) collective-permute-start(bf16[1025,128]{1,0:T(8,128)(2,1)} %pad_maximum_fusion.7), channel_id=1, source_target_pairs={{0,32},{4,36},{8,40},{12,44},{16,48},{20,52},{24,56},{28,60},{32,6... | collective-permute-start | bytes 787208 | tf_op jit(solution)/shard_map/ppermute | solution.py:19
  91.0 9.7 %collective-permute-start.7 = (bf16[1025,128]{1,0:T(8,128)(2,1)S(1)}, bf16[1025,128]{1,0:T(8,128)(2,1)S(1)}, u32[]{:S(2)}, u32[]{:S(2)}) collective-permute-start(bf16[1025,128]{1,0:T(8,128)(2,1)S(1)} %pad_maximum_fusion.8), channel_id=1, source_target_pairs={{0,64},{4,68},{8,72},{12,76},{16,80},{20,84},{24,88},{28,92},{32,9... | collective-permute-start | bytes 787208 | tf_op jit(solution)/shard_map/ppermute | solution.py:19
  114.2 29.2 %collective-permute-start.8 = (bf16[544,1024]{1,0:T(8,128)(2,1)}, bf16[544,1024]{1,0:T(8,128)(2,1)S(1)}, u32[]{:S(2)}, u32[]{:S(2)}) collective-permute-start(bf16[544,1024]{1,0:T(8,128)(2,1)} %fusion.19), channel_id=1, source_target_pairs={{0,2},{1,3},{2,0},{3,1},{4,6},{5,7},{6,4},{7,5},{8,10},{9,11},{10,... | collective-permute-start | bytes 3342344 | tf_op jit(solution)/shard_map/ppermute | solution.py:290
  120.5 42.6 %collective-permute-start.9 = (bf16[544,1024]{1,0:T(8,128)(2,1)}, bf16[544,1024]{1,0:T(8,128)(2,1)}, u32[]{:S(2)}, u32[]{:S(2)}) collective-permute-start(bf16[544,1024]{1,0:T(8,128)(2,1)} %fusion.22), channel_id=1, source_target_pairs={{0,1},{1,2},{2,3},{3,0},{4,5},{5,6},{6,7},{7,4},{8,9},{9,10},{10,1... | collective-permute-start | bytes 3342344 | tf_op jit(solution)/shard_map/ppermute | solution.py:290
  124.4 38.7 %collective-permute-start.10 = (bf16[544,1024]{1,0:T(8,128)(2,1)}, bf16[544,1024]{1,0:T(8,128)(2,1)}, u32[]{:S(2)}, u32[]{:S(2)}) collective-permute-start(bf16[544,1024]{1,0:T(8,128)(2,1)} %fusion.25), channel_id=1, source_target_pairs={{0,3},{1,0},{2,1},{3,2},{4,7},{5,4},{6,5},{7,6},{8,11},{9,8},{10,9... | collective-permute-start | bytes 3342344 | tf_op jit(solution)/shard_map/ppermute | solution.py:290
  167.7 3.7 %collective-permute-start.12 = (bf16[3,1024]{1,0:T(4,128)(2,1)S(1)}, bf16[3,1024]{1,0:T(4,128)(2,1)S(1)}, u32[]{:S(2)}, u32[]{:S(2)}) collective-permute-start(bf16[3,1024]{1,0:T(4,128)(2,1)S(1)} %get-tuple-element.82), channel_id=1, source_target_pairs={{0,8},{4,12},{8,0},{12,4},{16,24},{20,28},{24,16},{28,20},{32,40},... | collective-permute-start | bytes 18440 | tf_op jit(solution)/shard_map/ppermute | solution.py:65
  171.5 6.5 %collective-permute-start.14 = (bf16[12,1024]{1,0:T(8,128)(2,1)S(1)}, bf16[12,1024]{1,0:T(8,128)(2,1)S(1)}, u32[]{:S(2)}, u32[]{:S(2)}) collective-permute-start(bf16[12,1024]{1,0:T(8,128)(2,1)S(1)} %get-tuple-element.62), channel_id=1, source_target_pairs={{0,16},{4,20},{8,24},{12,28},{16,32},{20,36},{24,40},{28,44},{32,4... | collective-permute-start | bytes 73736 | tf_op jit(solution)/shard_map/ppermute | solution.py:65
  173.4 4.7 %collective-permute-start.15 = (bf16[12,1024]{1,0:T(8,128)(2,1)S(1)}, bf16[12,1024]{1,0:T(8,128)(2,1)S(1)}, u32[]{:S(2)}, u32[]{:S(2)}) collective-permute-start(bf16[12,1024]{1,0:T(8,128)(2,1)S(1)} %get-tuple-element.62), channel_id=1, source_target_pairs={{0,32},{4,36},{8,40},{12,44},{16,48},{20,52},{24,56},{28,60},{32,0... | collective-permute-start | bytes 73736 | tf_op jit(solution)/shard_map/ppermute | solution.py:65
  173.4 5.7 %collective-permute-start.16 = (bf16[12,1024]{1,0:T(8,128)(2,1)S(1)}, bf16[12,1024]{1,0:T(8,128)(2,1)S(1)}, u32[]{:S(2)}, u32[]{:S(2)}) collective-permute-start(bf16[12,1024]{1,0:T(8,128)(2,1)S(1)} %get-tuple-element.62), channel_id=1, source_target_pairs={{0,48},{4,52},{8,56},{12,60},{16,0},{20,4},{24,8},{28,12},{32,16},... | collective-permute-start | bytes 73736 | tf_op jit(solution)/shard_map/ppermute | solution.py:65
  179.2 7.2 %collective-permute-start.17 = (bf16[48,1024]{1,0:T(8,128)(2,1)S(1)}, bf16[48,1024]{1,0:T(8,128)(2,1)S(1)}, u32[]{:S(2)}, u32[]{:S(2)}) collective-permute-start(bf16[48,1024]{1,0:T(8,128)(2,1)S(1)} %pad_maximum_fusion.12), channel_id=1, source_target_pairs={{0,64},{4,68},{8,72},{12,76},{16,80},{20,84},{24,88},{28,92},{32,9... | collective-permute-start | bytes 294920 | tf_op jit(solution)/shard_map/ppermute | solution.py:65
  186.5 7.8 %collective-permute-start.18 = (bf16[96,1024]{1,0:T(8,128)(2,1)S(1)}, bf16[96,1024]{1,0:T(8,128)(2,1)S(1)}, u32[]{:S(2)}, u32[]{:S(2)}) collective-permute-start(bf16[96,1024]{1,0:T(8,128)(2,1)S(1)} %get-tuple-element.54), channel_id=1, source_target_pairs={{0,1},{1,2},{2,3},{3,0},{4,5},{5,6},{6,7},{7,4},{8,9},{9,10},{10,1... | collective-permute-start | bytes 589832 | tf_op jit(solution)/shard_map/ppermute | solution.py:65
  188.0 9.3 %collective-permute-start.19 = (bf16[96,1024]{1,0:T(8,128)(2,1)S(1)}, bf16[96,1024]{1,0:T(8,128)(2,1)S(1)}, u32[]{:S(2)}, u32[]{:S(2)}) collective-permute-start(bf16[96,1024]{1,0:T(8,128)(2,1)S(1)} %get-tuple-element.54), channel_id=1, source_target_pairs={{0,2},{1,3},{2,0},{3,1},{4,6},{5,7},{6,4},{7,5},{8,10},{9,11},{10,... | collective-permute-start | bytes 589832 | tf_op jit(solution)/shard_map/ppermute | solution.py:65
  189.3 9.7 %collective-permute-start.20 = (bf16[96,1024]{1,0:T(8,128)(2,1)S(1)}, bf16[96,1024]{1,0:T(8,128)(2,1)S(1)}, u32[]{:S(2)}, u32[]{:S(2)}) collective-permute-start(bf16[96,1024]{1,0:T(8,128)(2,1)S(1)} %get-tuple-element.54), channel_id=1, source_target_pairs={{0,3},{1,0},{2,1},{3,2},{4,7},{5,4},{6,5},{7,6},{8,11},{9,8},{10,9... | collective-permute-start | bytes 589832 | tf_op jit(solution)/shard_map/ppermute | solution.py:65
  208.0 6.0 %collective-permute-start.21 = (f32[65]{0:T(128)S(1)}, f32[65]{0:T(128)S(1)}, u32[]{:S(2)}, u32[]{:S(2)}) collective-permute-start(f32[65]{0:T(128)S(1)} %convolution_reduce_fusion), channel_id=1, source_target_pairs={{0,1},{1,2},{2,3},{3,0},{4,5},{5,6},{6,7},{7,4},{8,9},{9,10},{10,1... | collective-permute-start | bytes 788 | tf_op jit(solution)/shard_map/ppermute | solution.py:84
  209.2 5.1 %collective-permute-start.22 = (f32[65]{0:T(128)S(1)}, f32[65]{0:T(128)S(1)}, u32[]{:S(2)}, u32[]{:S(2)}) collective-permute-start(f32[65]{0:T(128)S(1)} %convolution_reduce_fusion), channel_id=1, source_target_pairs={{0,2},{1,3},{2,0},{3,1},{4,6},{5,7},{6,4},{7,5},{8,10},{9,11},{10,... | collective-permute-start | bytes 788 | tf_op jit(solution)/shard_map/ppermute | solution.py:84
  218.0 6.0 %collective-permute-start.27 = (f32[65]{0:T(128)S(1)}, f32[65]{0:T(128)S(1)}, u32[]{:S(2)}, u32[]{:S(2)}) collective-permute-start(f32[65]{0:T(128)S(1)} %maximum_maximum_fusion.1), channel_id=1, source_target_pairs={{0,16},{4,20},{8,24},{12,28},{16,32},{20,36},{24,40},{28,44},{32,4... | collective-permute-start | bytes 788 | tf_op jit(solution)/shard_map/ppermute | solution.py:84
  221.8 5.1 %collective-permute-start.29 = (f32[65]{0:T(128)S(1)}, f32[65]{0:T(128)S(1)}, u32[]{:S(2)}, u32[]{:S(2)}) collective-permute-start(f32[65]{0:T(128)S(1)} %maximum_maximum_fusion.1), channel_id=1, source_target_pairs={{0,48},{4,52},{8,56},{12,60},{16,0},{20,4},{24,8},{28,12},{32,16},... | collective-permute-start | bytes 788 | tf_op jit(solution)/shard_map/ppermute | solution.py:84
  226.9 5.8 %collective-permute-start.30 = (f32[65]{0:T(128)S(1)}, f32[65]{0:T(128)S(1)}, u32[]{:S(2)}, u32[]{:S(2)}) collective-permute-start(f32[65]{0:T(128)S(1)} %maximum_maximum_fusion), channel_id=1, source_target_pairs={{0,64},{4,68},{8,72},{12,76},{16,80},{20,84},{24,88},{28,92},{32,9... | collective-permute-start | bytes 788 | tf_op jit(solution)/shard_map/ppermute | solution.py:84
  (68 other events, 737.6 us)

commit v4 on v3

--- a/solution.py
+++ b/solution.py
@@ -279,28 +279,41 @@
     tp_count = lax.axis_size("tp")
     tp_index = lax.axis_index("tp")
     width = out_weight.shape[1] // tp_count
+    out_terms = jnp.dot(all_normed, out_weight, preferred_element_type=jnp.float32).astype(
+        jnp.bfloat16
+    )
+    last_pick = (jnp.arange(SLEN)[None, :] == lengths[:, None] - 1).astype(jnp.float32)
     total = None
+    row_total = None
     for step in (2, 1, 3, 0):
         if step >= tp_count:
             continue
         target = (tp_index + step) % tp_count
-        piece = lax.dynamic_slice_in_dim(out_weight, target * width, width, 1)
-        term = jnp.dot(all_normed, piece, preferred_element_type=jnp.float32).astype(jnp.bfloat16)
+        term = lax.dynamic_slice_in_dim(out_terms, target * width, width, 1)
         if step:
             term = lax.ppermute(
                 term, "tp", [(i, (i + step) % tp_count) for i in range(tp_count)]
             )
+        picked = jnp.concatenate(
+            [
+                jnp.einsum(
+                    "rs,rsd->rd",
+                    last_pick,
+                    term[tok_rows:].reshape(req_count, SLEN, -1).astype(jnp.float32),
+                    precision=lax.Precision.HIGHEST,
+                ),
+                term[tok_rows - 1 : tok_rows].astype(jnp.float32),
+            ],
+            0,
+        )
         total = term.astype(jnp.float32) if total is None else total + term.astype(jnp.float32)
+        row_total = picked if row_total is None else row_total + picked
     hidden = total.astype(jnp.bfloat16)
     hidden_long = hidden[:tok_rows]
     hidden_short = hidden[tok_rows:].reshape(req_count, SLEN, -1) * is_valid[:, :, None].astype(
         jnp.bfloat16
     )
-    last_pick = (jnp.arange(SLEN)[None, :] == lengths[:, None] - 1).astype(jnp.float32)
-    short_rows = jnp.einsum(
-        "rs,rsd->rd", last_pick, hidden_short.astype(jnp.float32), precision=lax.Precision.HIGHEST
-    ).astype(jnp.bfloat16)
-    packed = jnp.concatenate([short_rows, hidden_long[tok_rows - 1 :]], 0)
+    packed = row_total.astype(jnp.bfloat16)
     seq_rows = gather_fast(packed, "seq", 0)
     full_rows = gather_fast(seq_rows, "tp", 1)
     seq_count = lax.axis_size("seq")

time: 236 us -> 241 us (1.021)
  matrix products: 45.3 us -> 37.3 us
  other arithmetic: 32.7 us -> 37.8 us
  waiting for transfers between devices: 62.5 us -> 67.2 us
    dot_general x5, matrix products: 16.5 us -> 9.04 us  [the longest x1 8.53 us: local(): jnp.dot(all_normed, out_weight, preferred_element_type=jnp.float32)]
    ppermute x3, waiting for transfers between devices: 36.6 us -> 43.5 us  [local(): lax.ppermute(term, 'tp', [(i, (i + step) % tp_count) for i in range(tp_co...]
    ppermute x10, waiting for transfers between devices: 14.3 us -> 11.3 us  [gather_fast(): lax.ppermute(block, axis, digit_route(count, distance, step, radix))]
    unnamed x130 -> x124, local copies, waits for them, and re-layouts: 6.55 us -> 7.22 us
  transfers between devices with their start and end apart: 31 -> 31, of which waited for: 20 -> 16; matrix products, arithmetic and copies ran while one was open for 23% -> 22% of each run, Pallas kernels for 0% -> 0%
where the time goes in v4:
time: 241 us; the launch traced here: 237 us
  starting transfers between devices  70 us (29%)
  waiting for transfers between devices  67.2 us (28%)
  other arithmetic  37.8 us (16%)
  matrix products  37.3 us (15%)
  local copies, waits for them, and re-layouts  22.7 us (9%)
    ppermute x3, waiting for transfers between devices, local(): lax.ppermute(term, 'tp', [(i, (i + step) % tp_count) for i in range(tp_co...  43.5 us
    ppermute x8, starting transfers between devices, passed_along(): return lax.ppermute(block, axis, route)  34.3 us
    ppermute x10, starting transfers between devices, gather_fast(): lax.ppermute(block, axis, digit_route(count, distance, step, radix))  15.8 us
    ppermute x10, starting transfers between devices, max_fast(): lax.ppermute(block, axis, digit_route(count, distance, step, radix))  15.4 us
    ppermute x10, waiting for transfers between devices, gather_fast(): lax.ppermute(block, axis, digit_route(count, distance, step, radix))  11.3 us
    dot_general x1, matrix products, local(): jnp.dot(all_normed, out_weight, preferred_element_type=jnp.float32)  8.53 us
    dot_general x3, matrix products, ssd_block(): jnp.einsum('hts,shp->thp', weights, x_block, preferred_element_type=jnp.f...  7.8 us
    unnamed x124, local copies, waits for them, and re-layouts  7.22 us
  transfers between devices with their start and end apart: 31, of which 16 were waited for; matrix products, arithmetic and copies ran while one was open for 22% of the time, Pallas kernels for 0%

profile of v4, /device:TPU:8, one launch (start us, length us, event | category | flops | bytes accessed | tf_op | source)
XLA Modules:
  0.0 236.9 jit_solution(5230038660956673329)
XLA Ops:
  4.2 4.1 %collective-permute-start.1 = (bf16[3,2,128]{2,0,1:T(4,128)(2,1)S(1)}, bf16[3,2,128]{2,0,1:T(4,128)(2,1)S(1)}, u32[]{:S(2)}, u32[]{:S(2)}) collective-permute-start(bf16[3,2,128]{2,0,1:T(4,128)(2,1)S(1)} %slice.399), channel_id=1, source_target_pairs={{0,4},{4,8},{8,12},{12,16},{16,20},{20,24},{24,28},{28,32},{32,36}... | collective-permute-start | bytes 4616 | tf_op jit(solution)/shard_map/ppermute | solution.py:19
  35.0 3.8 %collective-permute-start.3 = (bf16[1025,128]{1,0:T(8,128)(2,1)S(1)}, bf16[1025,128]{1,0:T(8,128)(2,1)S(1)}, u32[]{:S(2)}, u32[]{:S(2)}) collective-permute-start(bf16[1025,128]{1,0:T(8,128)(2,1)S(1)} %pad_maximum_fusion.3), channel_id=1, source_target_pairs={{0,8},{4,12},{8,16},{12,20},{16,24},{20,28},{24,32},{28,36},{32,40... | collective-permute-start | bytes 787208 | tf_op jit(solution)/shard_map/ppermute | solution.py:19
  40.5 3.7 %fusion.14 = f32[256,16,64]{0,2,1:T(8,128)} fusion(bf16[256,16,64]{0,2,1:T(8,128)(2,1)S(1)} %bitcast.308, f32[16,256]{1,0:T(8,128)} %get-tuple-element.128, f32[16,256]{1,0:T(8,128)} %copy-done.30, pred[256,256]{1,0:T(8,128)(4,1)} %iota_compare_fusion, bf16[256,128]{1,0:T(8,128)(2,1)} %copy-done.28, bf16[256,128]{1,0:T(8,128)(2,1)} %get-tuple-element.58), kind=kOutput, calls=%fused_computation.31 | convolution fusion | flops 408944640 | bytes 1802240 | tf_op jit(solution)/shard_map/hts,shp->thp/dot_general | solution.py:153
  44.3 3.7 %fusion.13 = f32[256,16,64]{0,2,1:T(8,128)} fusion(bf16[256,16,64]{0,2,1:T(8,128)(2,1)S(1)} %bitcast.304, f32[16,256]{1,0:T(8,128)} %get-tuple-element.127, f32[16,256]{1,0:T(8,128)} %copy-done.29, pred[256,256]{1,0:T(8,128)(4,1)} %iota_compare_fusion, bf16[256,128]{1,0:T(8,128)(2,1)} %copy-done.23, bf16[256,128]{1,0:T(8,128)(2,1)} %get-tuple-element.60), kind=kOutput, calls=%fused_computation.30 | convolution fusion | flops 408944640 | bytes 1802240 | tf_op jit(solution)/shard_map/hts,shp->thp/dot_general | solution.py:153
  50.7 3.8 %collective-permute-start.4 = (bf16[1025,128]{1,0:T(8,128)(2,1)}, bf16[1025,128]{1,0:T(8,128)(2,1)S(1)}, u32[]{:S(2)}, u32[]{:S(2)}) collective-permute-start(bf16[1025,128]{1,0:T(8,128)(2,1)} %pad_maximum_fusion.4), channel_id=1, source_target_pairs={{0,8},{4,12},{8,16},{12,20},{16,24},{20,28},{24,32},{28,36},{32,40... | collective-permute-start | bytes 787208 | tf_op jit(solution)/shard_map/ppermute | solution.py:19
  57.0 3.0 %fusion.17 = f32[1,256,16,64]{1,3,2,0:T(8,128)} fusion(f32[256,16,64]{0,2,1:T(8,128)S(1)} %copy-done.16, f32[16,64,128]{2,1,0:T(8,128)S(1)} %convolution_add_fusion.2, f32[256,16]{0,1:T(8,128)} %get-tuple-element.81, bf16[256,128]{1,0:T(8,128)(2,1)} %get-tuple-element.60), kind=kOutput, calls=%fused_computation.36 | convolution fusion | flops 403177472 | bytes 2703360 | tf_op jit(solution)/shard_map/thn,hpn->thp/dot_general | solution.py:154
  63.3 6.9 %collective-permute-start.5 = (bf16[1025,128]{1,0:T(8,128)(2,1)}, bf16[1025,128]{1,0:T(8,128)(2,1)}, u32[]{:S(2)}, u32[]{:S(2)}) collective-permute-start(bf16[1025,128]{1,0:T(8,128)(2,1)} %pad_maximum_fusion.5), channel_id=1, source_target_pairs={{0,16},{4,20},{8,24},{12,28},{16,32},{20,36},{24,40},{28,44},{32,4... | collective-permute-start | bytes 787208 | tf_op jit(solution)/shard_map/ppermute | solution.py:19
  72.3 3.3 %copy.114 = f32[2,16,8,8,256]{4,3,0,2,1:T(8,128)} copy(f32[2,16,8,8,256]{4,3,2,1,0:T(8,128)} %maximum_bitcast_fusion) | data formatting | bytes 4194304 | tf_op jit(solution)/shard_map/reshape | solution.py:229
  79.6 6.4 %collective-permute-start.6 = (bf16[1025,128]{1,0:T(8,128)(2,1)}, bf16[1025,128]{1,0:T(8,128)(2,1)S(1)}, u32[]{:S(2)}, u32[]{:S(2)}) collective-permute-start(bf16[1025,128]{1,0:T(8,128)(2,1)} %pad_maximum_fusion.6), channel_id=1, source_target_pairs={{0,32},{4,36},{8,40},{12,44},{16,48},{20,52},{24,56},{28,60},{32,6... | collective-permute-start | bytes 787208 | tf_op jit(solution)/shard_map/ppermute | solution.py:19
  93.1 5.8 %collective-permute-start.7 = (bf16[1025,128]{1,0:T(8,128)(2,1)S(1)}, bf16[1025,128]{1,0:T(8,128)(2,1)S(1)}, u32[]{:S(2)}, u32[]{:S(2)}) collective-permute-start(bf16[1025,128]{1,0:T(8,128)(2,1)S(1)} %pad_maximum_fusion.7), channel_id=1, source_target_pairs={{0,64},{4,68},{8,72},{12,76},{16,80},{20,84},{24,88},{28,92},{32,9... | collective-permute-start | bytes 787208 | tf_op jit(solution)/shard_map/ppermute | solution.py:19
  100.0 2.8 %collective-permute-done.7 = bf16[1025,128]{1,0:T(8,128)(2,1)S(1)} collective-permute-done((bf16[1025,128]{1,0:T(8,128)(2,1)S(1)}, bf16[1025,128]{1,0:T(8,128)(2,1)S(1)}, u32[]{:S(2)}, u32[]{:S(2)}) %collective-permute-start.7) | collective-permute-done | bytes 262432 | tf_op jit(solution)/shard_map/ppermute | solution.py:19
  104.7 3.8 %fusion.10 = f32[512,16,64]{0,2,1:T(8,128)} fusion(f32[512,16,64]{0,2,1:T(8,128)S(1)} %bitcast.296, f32[512,16,64]{0,2,1:T(8,128)S(1)} %bitcast.295, f32[16,64,128]{2,1,0:T(8,128)S(1)} %get-tuple-element.33, f32[16]{0:T(128)S(1)} %copy-done.56, bf16[512,128]{1,0:T(8,128)(2,1)S(1)} %slice_bitcast_fusion, f32[512,16]{0,1:T(8,128)S(1)} %copy-done.24), kind=kOutput, calls=%fused_computation.20 | convolution fusion | flops 807403520 | bytes 6979648 | tf_op jit(solution)/shard_map/thn,hpn->thp/dot_general | solution.py:225
  112.1 8.5 %convolution_convert_fusion = bf16[544,4096]{1,0:T(8,128)(2,1)S(1)} fusion(bf16[1024,4096]{1,0:T(8,128)(2,1)} %param.37, bf16[32,1024]{1,0:T(8,128)(2,1)S(1)} %copy-done.27, bf16[512,1024]{1,0:T(8,128)(2,1)S(1)} %multiply_convert_fusion.2), kind=kOutput, calls=%fused_computation | convolution fusion | flops 4567859200 | bytes 13959168 | tf_op jit(solution)/shard_map/dot_general | solution.py:282
  126.0 24.2 %collective-permute-done.8 = bf16[544,1024]{1,0:T(8,128)(2,1)S(1)} collective-permute-done((bf16[544,1024]{1,0:T(8,128)(2,1)S(1)}, bf16[544,1024]{1,0:T(8,128)(2,1)S(1)}, u32[]{:S(2)}, u32[]{:S(2)}) %collective-permute-start.8) | collective-permute-done | bytes 1114144 | tf_op jit(solution)/shard_map/ppermute | solution.py:294
  150.3 19.3 %collective-permute-done.10 = bf16[544,1024]{1,0:T(8,128)(2,1)S(1)} collective-permute-done((bf16[544,1024]{1,0:T(8,128)(2,1)S(1)}, bf16[544,1024]{1,0:T(8,128)(2,1)S(1)}, u32[]{:S(2)}, u32[]{:S(2)}) %collective-permute-start.10) | collective-permute-done | bytes 1114144 | tf_op jit(solution)/shard_map/ppermute | solution.py:294
  177.7 3.1 %collective-permute-start.16 = (bf16[12,1024]{1,0:T(8,128)(2,1)S(1)}, bf16[12,1024]{1,0:T(8,128)(2,1)S(1)}, u32[]{:S(2)}, u32[]{:S(2)}) collective-permute-start(bf16[12,1024]{1,0:T(8,128)(2,1)S(1)} %get-tuple-element.71), channel_id=1, source_target_pairs={{0,48},{4,52},{8,56},{12,60},{16,0},{20,4},{24,8},{28,12},{32,16},... | collective-permute-start | bytes 73736 | tf_op jit(solution)/shard_map/ppermute | solution.py:65
  183.2 4.6 %collective-permute-start.17 = (bf16[48,1024]{1,0:T(8,128)(2,1)S(1)}, bf16[48,1024]{1,0:T(8,128)(2,1)S(1)}, u32[]{:S(2)}, u32[]{:S(2)}) collective-permute-start(bf16[48,1024]{1,0:T(8,128)(2,1)S(1)} %pad_maximum_fusion.11), channel_id=1, source_target_pairs={{0,64},{4,68},{8,72},{12,76},{16,80},{20,84},{24,88},{28,92},{32,9... | collective-permute-start | bytes 294920 | tf_op jit(solution)/shard_map/ppermute | solution.py:65
  187.9 2.6 %collective-permute-done.17 = bf16[48,1024]{1,0:T(8,128)(2,1)S(1)} collective-permute-done((bf16[48,1024]{1,0:T(8,128)(2,1)S(1)}, bf16[48,1024]{1,0:T(8,128)(2,1)S(1)}, u32[]{:S(2)}, u32[]{:S(2)}) %collective-permute-start.17) | collective-permute-done | bytes 98336 | tf_op jit(solution)/shard_map/ppermute | solution.py:65
  195.0 2.9 %collective-permute-done.19 = bf16[96,1024]{1,0:T(8,128)(2,1)S(1)} collective-permute-done((bf16[96,1024]{1,0:T(8,128)(2,1)S(1)}, bf16[96,1024]{1,0:T(8,128)(2,1)S(1)}, u32[]{:S(2)}, u32[]{:S(2)}) %collective-permute-start.19) | collective-permute-done | bytes 196640 | tf_op jit(solution)/shard_map/ppermute | solution.py:65
  202.4 6.4 %convolution_reduce_fusion = f32[65]{0:T(128)S(1)} fusion(bf16[65,4096]{1,0:T(8,128)(2,1)S(1)} %fusion.23, bf16[1024,4096]{1,0:T(8,128)(2,1)} %param.39), kind=kOutput, calls=%fused_computation.54 | convolution fusion | flops 545326016 | bytes 8921348 | tf_op jit(solution)/shard_map/dot_general | solution.py:329
  212.2 2.5 %collective-permute-start.21 = (f32[65]{0:T(128)S(1)}, f32[65]{0:T(128)S(1)}, u32[]{:S(2)}, u32[]{:S(2)}) collective-permute-start(f32[65]{0:T(128)S(1)} %convolution_reduce_fusion), channel_id=1, source_target_pairs={{0,1},{1,2},{2,3},{3,0},{4,5},{5,6},{6,7},{7,4},{8,9},{9,10},{10,1... | collective-permute-start | bytes 788 | tf_op jit(solution)/shard_map/ppermute | solution.py:84
  219.6 4.1 %collective-permute-start.29 = (f32[65]{0:T(128)S(1)}, f32[65]{0:T(128)S(1)}, u32[]{:S(2)}, u32[]{:S(2)}) collective-permute-start(f32[65]{0:T(128)S(1)} %maximum_maximum_fusion.1), channel_id=1, source_target_pairs={{0,48},{4,52},{8,56},{12,60},{16,0},{20,4},{24,8},{28,12},{32,16},... | collective-permute-start | bytes 788 | tf_op jit(solution)/shard_map/ppermute | solution.py:84
  227.4 3.7 %collective-permute-done.27 = f32[65]{0:T(128)S(1)} collective-permute-done((f32[65]{0:T(128)S(1)}, f32[65]{0:T(128)S(1)}, u32[]{:S(2)}, u32[]{:S(2)}) %collective-permute-start.27) | collective-permute-done | bytes 292 | tf_op jit(solution)/shard_map/ppermute | solution.py:84
  231.1 3.5 %collective-permute-start.30 = (f32[65]{0:T(128)S(1)}, f32[65]{0:T(128)S(1)}, u32[]{:S(2)}, u32[]{:S(2)}) collective-permute-start(f32[65]{0:T(128)S(1)} %maximum_maximum_fusion), channel_id=1, source_target_pairs={{0,64},{4,68},{8,72},{12,76},{16,80},{20,84},{24,88},{28,92},{32,9... | collective-permute-start | bytes 788 | tf_op jit(solution)/shard_map/ppermute | solution.py:84
  (341 shorter events, 98.3 us)
Async XLA Ops:
  1.4 28.0 %collective-permute-start = (bf16[3,1024]{1,0:T(4,128)(2,1)S(1)}, bf16[3,1024]{1,0:T(4,128)(2,1)S(1)}, u32[]{:S(2)}, u32[]{:S(2)}) collective-permute-start(bf16[3,1024]{1,0:T(4,128)(2,1)S(1)} %slice.306), channel_id=1, source_target_pairs={{0,4},{4,8},{8,12},{12,16},{16,20},{20,24},{24,28},{28,32},{32,36}... | collective-permute-start | bytes 18440 | tf_op jit(solution)/shard_map/ppermute | solution.py:19
  4.2 24.2 %collective-permute-start.1 = (bf16[3,2,128]{2,0,1:T(4,128)(2,1)S(1)}, bf16[3,2,128]{2,0,1:T(4,128)(2,1)S(1)}, u32[]{:S(2)}, u32[]{:S(2)}) collective-permute-start(bf16[3,2,128]{2,0,1:T(4,128)(2,1)S(1)} %slice.399), channel_id=1, source_target_pairs={{0,4},{4,8},{8,12},{12,16},{16,20},{20,24},{24,28},{28,32},{32,36}... | collective-permute-start | bytes 4616 | tf_op jit(solution)/shard_map/ppermute | solution.py:19
  35.0 13.0 %collective-permute-start.3 = (bf16[1025,128]{1,0:T(8,128)(2,1)S(1)}, bf16[1025,128]{1,0:T(8,128)(2,1)S(1)}, u32[]{:S(2)}, u32[]{:S(2)}) collective-permute-start(bf16[1025,128]{1,0:T(8,128)(2,1)S(1)} %pad_maximum_fusion.3), channel_id=1, source_target_pairs={{0,8},{4,12},{8,16},{12,20},{16,24},{20,28},{24,32},{28,36},{32,40... | collective-permute-start | bytes 787208 | tf_op jit(solution)/shard_map/ppermute | solution.py:19
  38.9 9.2 %collective-permute-start.2 = (bf16[1025,128]{1,0:T(8,128)(2,1)S(1)}, bf16[1025,128]{1,0:T(8,128)(2,1)S(1)}, u32[]{:S(2)}, u32[]{:S(2)}) collective-permute-start(bf16[1025,128]{1,0:T(8,128)(2,1)S(1)} %pad_maximum_fusion.3), channel_id=1, source_target_pairs={{0,4},{4,8},{8,12},{12,16},{16,20},{20,24},{24,28},{28,32},{32,36}... | collective-permute-start | bytes 787208 | tf_op jit(solution)/shard_map/ppermute | solution.py:19
  50.7 10.1 %collective-permute-start.4 = (bf16[1025,128]{1,0:T(8,128)(2,1)}, bf16[1025,128]{1,0:T(8,128)(2,1)S(1)}, u32[]{:S(2)}, u32[]{:S(2)}) collective-permute-start(bf16[1025,128]{1,0:T(8,128)(2,1)} %pad_maximum_fusion.4), channel_id=1, source_target_pairs={{0,8},{4,12},{8,16},{12,20},{16,24},{20,28},{24,32},{28,36},{32,40... | collective-permute-start | bytes 787208 | tf_op jit(solution)/shard_map/ppermute | solution.py:19
  63.3 13.2 %collective-permute-start.5 = (bf16[1025,128]{1,0:T(8,128)(2,1)}, bf16[1025,128]{1,0:T(8,128)(2,1)}, u32[]{:S(2)}, u32[]{:S(2)}) collective-permute-start(bf16[1025,128]{1,0:T(8,128)(2,1)} %pad_maximum_fusion.5), channel_id=1, source_target_pairs={{0,16},{4,20},{8,24},{12,28},{16,32},{20,36},{24,40},{28,44},{32,4... | collective-permute-start | bytes 787208 | tf_op jit(solution)/shard_map/ppermute | solution.py:19
  79.6 10.7 %collective-permute-start.6 = (bf16[1025,128]{1,0:T(8,128)(2,1)}, bf16[1025,128]{1,0:T(8,128)(2,1)S(1)}, u32[]{:S(2)}, u32[]{:S(2)}) collective-permute-start(bf16[1025,128]{1,0:T(8,128)(2,1)} %pad_maximum_fusion.6), channel_id=1, source_target_pairs={{0,32},{4,36},{8,40},{12,44},{16,48},{20,52},{24,56},{28,60},{32,6... | collective-permute-start | bytes 787208 | tf_op jit(solution)/shard_map/ppermute | solution.py:19
  93.1 9.7 %collective-permute-start.7 = (bf16[1025,128]{1,0:T(8,128)(2,1)S(1)}, bf16[1025,128]{1,0:T(8,128)(2,1)S(1)}, u32[]{:S(2)}, u32[]{:S(2)}) collective-permute-start(bf16[1025,128]{1,0:T(8,128)(2,1)S(1)} %pad_maximum_fusion.7), channel_id=1, source_target_pairs={{0,64},{4,68},{8,72},{12,76},{16,80},{20,84},{24,88},{28,92},{32,9... | collective-permute-start | bytes 787208 | tf_op jit(solution)/shard_map/ppermute | solution.py:19
  121.1 29.0 %collective-permute-start.8 = (bf16[544,1024]{1,0:T(8,128)(2,1)S(1)}, bf16[544,1024]{1,0:T(8,128)(2,1)S(1)}, u32[]{:S(2)}, u32[]{:S(2)}) collective-permute-start(bf16[544,1024]{1,0:T(8,128)(2,1)S(1)} %get-tuple-element.43), channel_id=1, source_target_pairs={{0,2},{1,3},{2,0},{3,1},{4,6},{5,7},{6,4},{7,5},{8,10},{9,11},{10,... | collective-permute-start | bytes 3342344 | tf_op jit(solution)/shard_map/ppermute | solution.py:294
  123.5 46.0 %collective-permute-start.10 = (bf16[544,1024]{1,0:T(8,128)(2,1)S(1)}, bf16[544,1024]{1,0:T(8,128)(2,1)S(1)}, u32[]{:S(2)}, u32[]{:S(2)}) collective-permute-start(bf16[544,1024]{1,0:T(8,128)(2,1)S(1)} %get-tuple-element.44), channel_id=1, source_target_pairs={{0,3},{1,0},{2,1},{3,2},{4,7},{5,4},{6,5},{7,6},{8,11},{9,8},{10,9... | collective-permute-start | bytes 3342344 | tf_op jit(solution)/shard_map/ppermute | solution.py:294
  124.9 44.8 %collective-permute-start.9 = (bf16[544,1024]{1,0:T(8,128)(2,1)S(1)}, bf16[544,1024]{1,0:T(8,128)(2,1)S(1)}, u32[]{:S(2)}, u32[]{:S(2)}) collective-permute-start(bf16[544,1024]{1,0:T(8,128)(2,1)S(1)} %get-tuple-element.45), channel_id=1, source_target_pairs={{0,1},{1,2},{2,3},{3,0},{4,5},{5,6},{6,7},{7,4},{8,9},{9,10},{10,1... | collective-permute-start | bytes 3342344 | tf_op jit(solution)/shard_map/ppermute | solution.py:294
  175.7 6.7 %collective-permute-start.15 = (bf16[12,1024]{1,0:T(8,128)(2,1)S(1)}, bf16[12,1024]{1,0:T(8,128)(2,1)S(1)}, u32[]{:S(2)}, u32[]{:S(2)}) collective-permute-start(bf16[12,1024]{1,0:T(8,128)(2,1)S(1)} %get-tuple-element.71), channel_id=1, source_target_pairs={{0,32},{4,36},{8,40},{12,44},{16,48},{20,52},{24,56},{28,60},{32,0... | collective-permute-start | bytes 73736 | tf_op jit(solution)/shard_map/ppermute | solution.py:65
  176.4 6.3 %collective-permute-start.14 = (bf16[12,1024]{1,0:T(8,128)(2,1)S(1)}, bf16[12,1024]{1,0:T(8,128)(2,1)S(1)}, u32[]{:S(2)}, u32[]{:S(2)}) collective-permute-start(bf16[12,1024]{1,0:T(8,128)(2,1)S(1)} %get-tuple-element.71), channel_id=1, source_target_pairs={{0,16},{4,20},{8,24},{12,28},{16,32},{20,36},{24,40},{28,44},{32,4... | collective-permute-start | bytes 73736 | tf_op jit(solution)/shard_map/ppermute | solution.py:65
  177.7 5.4 %collective-permute-start.16 = (bf16[12,1024]{1,0:T(8,128)(2,1)S(1)}, bf16[12,1024]{1,0:T(8,128)(2,1)S(1)}, u32[]{:S(2)}, u32[]{:S(2)}) collective-permute-start(bf16[12,1024]{1,0:T(8,128)(2,1)S(1)} %get-tuple-element.71), channel_id=1, source_target_pairs={{0,48},{4,52},{8,56},{12,60},{16,0},{20,4},{24,8},{28,12},{32,16},... | collective-permute-start | bytes 73736 | tf_op jit(solution)/shard_map/ppermute | solution.py:65
  183.2 7.2 %collective-permute-start.17 = (bf16[48,1024]{1,0:T(8,128)(2,1)S(1)}, bf16[48,1024]{1,0:T(8,128)(2,1)S(1)}, u32[]{:S(2)}, u32[]{:S(2)}) collective-permute-start(bf16[48,1024]{1,0:T(8,128)(2,1)S(1)} %pad_maximum_fusion.11), channel_id=1, source_target_pairs={{0,64},{4,68},{8,72},{12,76},{16,80},{20,84},{24,88},{28,92},{32,9... | collective-permute-start | bytes 294920 | tf_op jit(solution)/shard_map/ppermute | solution.py:65
  190.5 7.4 %collective-permute-start.19 = (bf16[96,1024]{1,0:T(8,128)(2,1)S(1)}, bf16[96,1024]{1,0:T(8,128)(2,1)S(1)}, u32[]{:S(2)}, u32[]{:S(2)}) collective-permute-start(bf16[96,1024]{1,0:T(8,128)(2,1)S(1)} %get-tuple-element.63), channel_id=1, source_target_pairs={{0,2},{1,3},{2,0},{3,1},{4,6},{5,7},{6,4},{7,5},{8,10},{9,11},{10,... | collective-permute-start | bytes 589832 | tf_op jit(solution)/shard_map/ppermute | solution.py:65
  192.9 7.0 %collective-permute-start.18 = (bf16[96,1024]{1,0:T(8,128)(2,1)S(1)}, bf16[96,1024]{1,0:T(8,128)(2,1)S(1)}, u32[]{:S(2)}, u32[]{:S(2)}) collective-permute-start(bf16[96,1024]{1,0:T(8,128)(2,1)S(1)} %get-tuple-element.63), channel_id=1, source_target_pairs={{0,1},{1,2},{2,3},{3,0},{4,5},{5,6},{6,7},{7,4},{8,9},{9,10},{10,1... | collective-permute-start | bytes 589832 | tf_op jit(solution)/shard_map/ppermute | solution.py:65
  192.9 7.0 %collective-permute-start.20 = (bf16[96,1024]{1,0:T(8,128)(2,1)S(1)}, bf16[96,1024]{1,0:T(8,128)(2,1)S(1)}, u32[]{:S(2)}, u32[]{:S(2)}) collective-permute-start(bf16[96,1024]{1,0:T(8,128)(2,1)S(1)} %get-tuple-element.63), channel_id=1, source_target_pairs={{0,3},{1,0},{2,1},{3,2},{4,7},{5,4},{6,5},{7,6},{8,11},{9,8},{10,9... | collective-permute-start | bytes 589832 | tf_op jit(solution)/shard_map/ppermute | solution.py:65
  208.9 6.0 %collective-permute-start.23 = (f32[65]{0:T(128)S(1)}, f32[65]{0:T(128)S(1)}, u32[]{:S(2)}, u32[]{:S(2)}) collective-permute-start(f32[65]{0:T(128)S(1)} %convolution_reduce_fusion), channel_id=1, source_target_pairs={{0,3},{1,0},{2,1},{3,2},{4,7},{5,4},{6,5},{7,6},{8,11},{9,8},{10,9... | collective-permute-start | bytes 788 | tf_op jit(solution)/shard_map/ppermute | solution.py:84
  210.0 5.1 %collective-permute-start.22 = (f32[65]{0:T(128)S(1)}, f32[65]{0:T(128)S(1)}, u32[]{:S(2)}, u32[]{:S(2)}) collective-permute-start(f32[65]{0:T(128)S(1)} %convolution_reduce_fusion), channel_id=1, source_target_pairs={{0,2},{1,3},{2,0},{3,1},{4,6},{5,7},{6,4},{7,5},{8,10},{9,11},{10,... | collective-permute-start | bytes 788 | tf_op jit(solution)/shard_map/ppermute | solution.py:84
  212.2 3.8 %collective-permute-start.21 = (f32[65]{0:T(128)S(1)}, f32[65]{0:T(128)S(1)}, u32[]{:S(2)}, u32[]{:S(2)}) collective-permute-start(f32[65]{0:T(128)S(1)} %convolution_reduce_fusion), channel_id=1, source_target_pairs={{0,1},{1,2},{2,3},{3,0},{4,5},{5,6},{6,7},{7,4},{8,9},{9,10},{10,1... | collective-permute-start | bytes 788 | tf_op jit(solution)/shard_map/ppermute | solution.py:84
  219.6 7.8 %collective-permute-start.29 = (f32[65]{0:T(128)S(1)}, f32[65]{0:T(128)S(1)}, u32[]{:S(2)}, u32[]{:S(2)}) collective-permute-start(f32[65]{0:T(128)S(1)} %maximum_maximum_fusion.1), channel_id=1, source_target_pairs={{0,48},{4,52},{8,56},{12,60},{16,0},{20,4},{24,8},{28,12},{32,16},... | collective-permute-start | bytes 788 | tf_op jit(solution)/shard_map/ppermute | solution.py:84
  225.2 6.0 %collective-permute-start.27 = (f32[65]{0:T(128)S(1)}, f32[65]{0:T(128)S(1)}, u32[]{:S(2)}, u32[]{:S(2)}) collective-permute-start(f32[65]{0:T(128)S(1)} %maximum_maximum_fusion.1), channel_id=1, source_target_pairs={{0,16},{4,20},{8,24},{12,28},{16,32},{20,36},{24,40},{28,44},{32,4... | collective-permute-start | bytes 788 | tf_op jit(solution)/shard_map/ppermute | solution.py:84
  231.1 5.3 %collective-permute-start.30 = (f32[65]{0:T(128)S(1)}, f32[65]{0:T(128)S(1)}, u32[]{:S(2)}, u32[]{:S(2)}) collective-permute-start(f32[65]{0:T(128)S(1)} %maximum_maximum_fusion), channel_id=1, source_target_pairs={{0,64},{4,68},{8,72},{12,76},{16,80},{20,84},{24,88},{28,92},{32,9... | collective-permute-start | bytes 788 | tf_op jit(solution)/shard_map/ppermute | solution.py:84
  (65 other events, 599.9 us)

commit v5 on v2

--- a/solution.py
+++ b/solution.py
@@ -262,18 +262,26 @@
     tp_count = lax.axis_size("tp")
     tp_index = lax.axis_index("tp")
     width = out_weight.shape[1] // tp_count
-    total = None
-    for step in (2, 1, 3, 0):
-        if step >= tp_count:
-            continue
+    blocks = []
+    for step in range(tp_count):
         target = (tp_index + step) % tp_count
         piece = lax.dynamic_slice_in_dim(out_weight, target * width, width, 1)
-        term = jnp.dot(all_normed, piece, preferred_element_type=jnp.float32).astype(jnp.bfloat16)
-        if step:
-            term = lax.ppermute(
-                term, "tp", [(i, (i + step) % tp_count) for i in range(tp_count)]
-            )
-        total = term.astype(jnp.float32) if total is None else total + term.astype(jnp.float32)
+        blocks.append(
+            jnp.dot(all_normed, piece, preferred_element_type=jnp.float32).astype(jnp.bfloat16)
+        )
+    rows_all = all_normed.shape[0]
+    half = rows_all // 2
+    ahead = [(i, (i + 1) % tp_count) for i in range(tp_count)]
+    behind = [(i, (i + tp_count - 1) % tp_count) for i in range(tp_count)]
+    from_prev = lax.ppermute(jnp.concatenate([blocks[1], blocks[2][:half]], 0), "tp", ahead)
+    from_next = lax.ppermute(jnp.concatenate([blocks[3], blocks[2][half:]], 0), "tp", behind)
+    far_top = lax.ppermute(from_prev[rows_all:], "tp", ahead)
+    far_bottom = lax.ppermute(from_next[rows_all:], "tp", behind)
+    far = jnp.concatenate([far_top, far_bottom], 0)
+    total = far.astype(jnp.float32)
+    total = total + from_prev[:rows_all].astype(jnp.float32)
+    total = total + from_next[:rows_all].astype(jnp.float32)
+    total = total + blocks[0].astype(jnp.float32)
     hidden = total.astype(jnp.bfloat16)
     hidden_long = hidden[:tok_rows]
     hidden_short = hidden[tok_rows:].reshape(req_count, SLEN, -1) * is_valid[:, :, None].astype(

time: 236 us -> 239 us (1.013)
  waiting for transfers between devices: 61.6 us -> 76.2 us
  starting transfers between devices: 89.6 us -> 80.1 us
  matrix products: 41.8 us -> 38.5 us
    ppermute x3 -> x4, waiting for transfers between devices: 36.8 us -> 44.4 us  [the longest x1 30.6 us: local(): lax.ppermute(jnp.concatenate([blocks[3], blocks[2][half:]], 0), 'tp', beh...]
    ppermute x10, starting transfers between devices: 18.1 us -> 13.5 us  [gather_fast(): lax.ppermute(block, axis, digit_route(count, distance, step, radix))]
    ppermute x10, starting transfers between devices: 17.5 us -> 13 us  [max_fast(): lax.ppermute(block, axis, digit_route(count, distance, step, radix))]
    dot_general x4, matrix products: 16.1 us -> 12.7 us  [local(): jnp.dot(all_normed, piece, preferred_element_type=jnp.float32)]
    ppermute x10, waiting for transfers between devices: 11.7 us -> 14.8 us  [gather_fast(): lax.ppermute(block, axis, digit_route(count, distance, step, radix))]
    ppermute x10, waiting for transfers between devices: 5.09 us -> 8.2 us  [max_fast(): lax.ppermute(block, axis, digit_route(count, distance, step, radix))]
  transfers between devices with their start and end apart: 36 -> 37, of which waited for: 18 -> 22; matrix products, arithmetic and copies ran while one was open for 20% -> 18% of each run, Pallas kernels for 0% -> 0%
where the time goes in v5:
time: 239 us; the launch traced here: 236 us
  starting transfers between devices  80.1 us (34%)
  waiting for transfers between devices  76.2 us (32%)
  matrix products  38.5 us (16%)
  other arithmetic  23.3 us (10%)
  local copies, waits for them, and re-layouts  16.1 us (7%)
    ppermute x13, starting transfers between devices, passed_along(): return lax.ppermute(block, axis, route)  50.1 us
    ppermute x1, waiting for transfers between devices, local(): lax.ppermute(jnp.concatenate([blocks[3], blocks[2][half:]], 0), 'tp', beh...  30.6 us
    ppermute x10, waiting for transfers between devices, gather_fast(): lax.ppermute(block, axis, digit_route(count, distance, step, radix))  14.8 us
    ppermute x10, starting transfers between devices, gather_fast(): lax.ppermute(block, axis, digit_route(count, distance, step, radix))  13.5 us
    ppermute x10, starting transfers between devices, max_fast(): lax.ppermute(block, axis, digit_route(count, distance, step, radix))  13 us
    dot_general x4, matrix products, local(): jnp.dot(all_normed, piece, preferred_element_type=jnp.float32)  12.7 us
    ppermute x13, waiting for transfers between devices, passed_along(): return lax.ppermute(block, axis, route)  8.81 us
    ppermute x10, waiting for transfers between devices, max_fast(): lax.ppermute(block, axis, digit_route(count, distance, step, radix))  8.2 us
  transfers between devices with their start and end apart: 37, of which 22 were waited for; matrix products, arithmetic and copies ran while one was open for 18% of the time, Pallas kernels for 0%

profile of v5, /device:TPU:8, one launch (start us, length us, event | category | flops | bytes accessed | tf_op | source)
XLA Modules:
  0.0 236.3 jit_solution(11693635582652579989)
XLA Ops:
  5.6 4.0 %collective-permute-start.3 = (f32[16]{0:T(128)S(1)}, f32[16]{0:T(128)S(1)}, u32[]{:S(2)}, u32[]{:S(2)}) collective-permute-start(f32[16]{0:T(128)S(1)} %slice_reduce_fusion.5), channel_id=1, source_target_pairs={{0,8},{4,12},{8,16},{12,20},{16,24},{20,28},{24,32},{28,36},{32,40... | collective-permute-start | bytes 200 | tf_op jit(solution)/shard_map/ppermute | solution.py:19
  10.4 3.6 %collective-permute-start = (bf16[3,1024]{1,0:T(4,128)(2,1)S(1)}, bf16[3,1024]{1,0:T(4,128)(2,1)S(1)}, u32[]{:S(2)}, u32[]{:S(2)}) collective-permute-start(bf16[3,1024]{1,0:T(4,128)(2,1)S(1)} %slice.211), channel_id=1, source_target_pairs={{0,4},{4,8},{8,12},{12,16},{16,20},{20,24},{24,28},{28,32},{32,36}... | collective-permute-start | bytes 18440 | tf_op jit(solution)/shard_map/ppermute | solution.py:19
  29.6 3.5 %collective-permute-start.4 = (f32[16]{0:T(128)S(1)}, f32[16]{0:T(128)S(1)}, u32[]{:S(2)}, u32[]{:S(2)}) collective-permute-start(f32[16]{0:T(128)S(1)} %get-tuple-element.39), channel_id=1, source_target_pairs={{0,8},{4,12},{8,16},{12,20},{16,24},{20,28},{24,32},{28,36},{32,40... | collective-permute-start | bytes 200 | tf_op jit(solution)/shard_map/ppermute | solution.py:19
  39.6 3.7 %collective-permute-start.7 = (bf16[16,64,128]{2,1,0:T(8,128)(2,1)S(1)}, bf16[16,64,128]{2,1,0:T(8,128)(2,1)S(1)}, u32[]{:S(2)}, u32[]{:S(2)}) collective-permute-start(bf16[16,64,128]{2,1,0:T(8,128)(2,1)S(1)} %get-tuple-element.95), channel_id=1, source_target_pairs={{0,8},{4,12},{8,16},{12,20},{16,24},{20,28},{24,32},{28,36},{32,40... | collective-permute-start | bytes 786440 | tf_op jit(solution)/shard_map/ppermute | solution.py:19
  43.8 5.5 %collective-permute-start.5 = (f32[16]{0:T(128)S(1)}, f32[16]{0:T(128)S(1)}, u32[]{:S(2)}, u32[]{:S(2)}) collective-permute-start(f32[16]{0:T(128)S(1)} %get-tuple-element.37), channel_id=1, source_target_pairs={{0,16},{4,20},{8,24},{12,28},{16,32},{20,36},{24,40},{28,44},{32,4... | collective-permute-start | bytes 200 | tf_op jit(solution)/shard_map/ppermute | solution.py:19
  51.1 4.5 %collective-permute-start.6 = (f32[16]{0:T(128)S(1)}, f32[16]{0:T(128)S(1)}, u32[]{:S(2)}, u32[]{:S(2)}) collective-permute-start(f32[16]{0:T(128)S(1)} %get-tuple-element.35), channel_id=1, source_target_pairs={{0,32},{4,36},{8,40},{12,44},{16,48},{20,52},{24,56},{28,60},{32,6... | collective-permute-start | bytes 200 | tf_op jit(solution)/shard_map/ppermute | solution.py:19
  55.8 4.0 %collective-permute-start.9 = (bf16[16,64,128]{2,1,0:T(8,128)(2,1)S(1)}, bf16[16,64,128]{2,1,0:T(8,128)(2,1)S(1)}, u32[]{:S(2)}, u32[]{:S(2)}) collective-permute-start(bf16[16,64,128]{2,1,0:T(8,128)(2,1)S(1)} %fusion.71), channel_id=1, source_target_pairs={{0,8},{4,12},{8,16},{12,20},{16,24},{20,28},{24,32},{28,36},{32,40... | collective-permute-start | bytes 786440 | tf_op jit(solution)/shard_map/ppermute | solution.py:19
  60.4 4.9 %collective-permute-done.9 = bf16[16,64,128]{2,1,0:T(8,128)(2,1)S(1)} collective-permute-done((bf16[16,64,128]{2,1,0:T(8,128)(2,1)S(1)}, bf16[16,64,128]{2,1,0:T(8,128)(2,1)S(1)}, u32[]{:S(2)}, u32[]{:S(2)}) %collective-permute-start.9) | collective-permute-done | bytes 262176 | tf_op jit(solution)/shard_map/ppermute | solution.py:19
  66.3 4.7 %collective-permute-start.10 = (bf16[16,64,128]{2,1,0:T(8,128)(2,1)S(1)}, bf16[16,64,128]{2,1,0:T(8,128)(2,1)S(1)}, u32[]{:S(2)}, u32[]{:S(2)}) collective-permute-start(bf16[16,64,128]{2,1,0:T(8,128)(2,1)S(1)} %fusion.144), channel_id=1, source_target_pairs={{0,16},{4,20},{8,24},{12,28},{16,32},{20,36},{24,40},{28,44},{32,4... | collective-permute-start | bytes 786440 | tf_op jit(solution)/shard_map/ppermute | solution.py:19
  71.0 3.8 %fusion.33 = f32[256,16,64]{0,2,1:T(8,128)} fusion(bf16[256,16,64]{0,2,1:T(8,128)(2,1)S(1)} %bitcast.222, f32[16,256]{1,0:T(8,128)} %get-tuple-element.97, f32[16,256]{1,0:T(8,128)} %copy-done.34, pred[256,256]{1,0:T(8,128)(4,1)} %iota_compare_fusion, bf16[256,128]{1,0:T(8,128)(2,1)} %copy-done.25, bf16[256,128]{1,0:T(8,128)(2,1)} %get-tuple-element.50), kind=kOutput, calls=%fused_computation.43 | convolution fusion | flops 408944640 | bytes 1802240 | tf_op jit(solution)/shard_map/hts,shp->thp/dot_general | solution.py:136
  77.2 6.8 %collective-permute-start.11 = (bf16[16,64,128]{2,1,0:T(8,128)(2,1)}, bf16[16,64,128]{2,1,0:T(8,128)(2,1)}, u32[]{:S(2)}, u32[]{:S(2)}) collective-permute-start(bf16[16,64,128]{2,1,0:T(8,128)(2,1)} %fusion.72), channel_id=1, source_target_pairs={{0,32},{4,36},{8,40},{12,44},{16,48},{20,52},{24,56},{28,60},{32,6... | collective-permute-start | bytes 786440 | tf_op jit(solution)/shard_map/ppermute | solution.py:19
  83.9 3.7 %fusion.34 = f32[256,16,64]{0,2,1:T(8,128)} fusion(bf16[256,16,64]{0,2,1:T(8,128)(2,1)S(1)} %bitcast.224, f32[16,256]{1,0:T(8,128)} %get-tuple-element.98, f32[16,256]{1,0:T(8,128)} %copy-done.33, pred[256,256]{1,0:T(8,128)(4,1)} %iota_compare_fusion, bf16[256,128]{1,0:T(8,128)(2,1)} %copy-done.32, bf16[256,128]{1,0:T(8,128)(2,1)} %get-tuple-element.48), kind=kOutput, calls=%fused_computation.44 | convolution fusion | flops 408944640 | bytes 1802240 | tf_op jit(solution)/shard_map/hts,shp->thp/dot_general | solution.py:136
  92.4 4.1 %collective-permute-start.12 = (bf16[16,64,128]{2,1,0:T(8,128)(2,1)S(1)}, bf16[16,64,128]{2,1,0:T(8,128)(2,1)S(1)}, u32[]{:S(2)}, u32[]{:S(2)}) collective-permute-start(bf16[16,64,128]{2,1,0:T(8,128)(2,1)S(1)} %get-tuple-element.32), channel_id=1, source_target_pairs={{0,64},{4,68},{8,72},{12,76},{16,80},{20,84},{24,88},{28,92},{32,9... | collective-permute-start | bytes 786440 | tf_op jit(solution)/shard_map/ppermute | solution.py:19
  100.3 3.8 %fusion.10 = f32[512,16,64]{0,2,1:T(8,128)} fusion(f32[512,16,64]{0,2,1:T(8,128)S(1)} %bitcast.219, f32[512,16,64]{0,2,1:T(8,128)S(1)} %bitcast.218, f32[16]{0:T(128)S(1)} %copy-done.61, bf16[512,128]{1,0:T(8,128)(2,1)S(1)} %slice_bitcast_fusion, f32[512,16]{0,1:T(8,128)S(1)} %copy-done.26, f32[16,64,128]{2,1,0:T(8,128)S(1)} %get-tuple-element.33, ...), kind=kOutput, calls=%fused_computation.19 | convolution fusion | flops 807796736 | bytes 7241856 | tf_op jit(solution)/shard_map/thn,hpn->thp/dot_general | solution.py:208
  107.7 3.3 %fusion.22 = bf16[544,1024]{1,0:T(8,128)(2,1)S(1)} fusion(bf16[1024,4096]{1,0:T(8,128)(2,1)} %param.37, s32[]{:T(128)S(6)} %select_n.195, bf16[32,1024]{1,0:T(8,128)(2,1)S(1)} %copy-done.31, bf16[512,1024]{1,0:T(8,128)(2,1)S(1)} %multiply_convert_fusion.2), kind=kOutput, calls=%fused_computation.34 | convolution fusion | flops 1143635968 | bytes 4325380 | tf_op jit(solution)/shard_map/dot_general | solution.py:270
  119.4 30.6 %collective-permute-done.15 = bf16[816,1024]{1,0:T(8,128)(2,1)} collective-permute-done((bf16[816,1024]{1,0:T(8,128)(2,1)S(1)}, bf16[816,1024]{1,0:T(8,128)(2,1)}, u32[]{:S(2)}, u32[]{:S(2)}) %collective-permute-start.15) | collective-permute-done | bytes 1671200 | tf_op jit(solution)/shard_map/ppermute | solution.py:277
  156.4 5.6 %collective-permute-done.16 = bf16[272,1024]{1,0:T(8,128)(2,1)S(1)} collective-permute-done((bf16[272,1024]{1,0:T(8,128)(2,1)S(1)}, bf16[272,1024]{1,0:T(8,128)(2,1)S(1)}, u32[]{:S(2)}, u32[]{:S(2)}) %collective-permute-start.16) | collective-permute-done | bytes 557088 | tf_op jit(solution)/shard_map/ppermute | solution.py:279
  162.1 5.6 %collective-permute-done.14 = bf16[272,1024]{1,0:T(8,128)(2,1)S(1)} collective-permute-done((bf16[272,1024]{1,0:T(8,128)(2,1)S(1)}, bf16[272,1024]{1,0:T(8,128)(2,1)S(1)}, u32[]{:S(2)}, u32[]{:S(2)}) %collective-permute-start.14) | collective-permute-done | bytes 557088 | tf_op jit(solution)/shard_map/ppermute | solution.py:278
  167.7 3.6 %add_convert_fusion = bf16[544,1024]{1,0:T(8,128)(2,1)S(1)} fusion(bf16[816,1024]{1,0:T(8,128)(2,1)} %collective-permute-done.15, bf16[816,1024]{1,0:T(8,128)(2,1)} %collective-permute-done.13, bf16[272,1024]{1,0:T(8,128)(2,1)S(1)} %collective-permute-done.16, bf16[272,1024]{1,0:T(8,128)(2,1)S(1)} %collective-permute-done.14, bf16[1024,4096]{1,0:T(8,128)(2,1)} %param.37, ...), kind=kOutput, calls=%fused_computation.6 | convolution fusion | flops 1149763584 | bytes 7667716 | tf_op jit(solution)/shard_map/dot_general | solution.py:270
  181.3 3.4 %collective-permute-done.20 = bf16[12,1024]{1,0:T(8,128)(2,1)S(1)} collective-permute-done((bf16[12,1024]{1,0:T(8,128)(2,1)S(1)}, bf16[12,1024]{1,0:T(8,128)(2,1)S(1)}, u32[]{:S(2)}, u32[]{:S(2)}) %collective-permute-start.20) | collective-permute-done | bytes 24608 | tf_op jit(solution)/shard_map/ppermute | solution.py:65
  184.8 4.1 %collective-permute-start.23 = (bf16[48,1024]{1,0:T(8,128)(2,1)S(1)}, bf16[48,1024]{1,0:T(8,128)(2,1)S(1)}, u32[]{:S(2)}, u32[]{:S(2)}) collective-permute-start(bf16[48,1024]{1,0:T(8,128)(2,1)S(1)} %pad_maximum_fusion.9), channel_id=1, source_target_pairs={{0,64},{4,68},{8,72},{12,76},{16,80},{20,84},{24,88},{28,92},{32,9... | collective-permute-start | bytes 294920 | tf_op jit(solution)/shard_map/ppermute | solution.py:65
  196.3 3.1 %collective-permute-done.26 = bf16[96,1024]{1,0:T(8,128)(2,1)S(1)} collective-permute-done((bf16[96,1024]{1,0:T(8,128)(2,1)S(1)}, bf16[96,1024]{1,0:T(8,128)(2,1)S(1)}, u32[]{:S(2)}, u32[]{:S(2)}) %collective-permute-start.26) | collective-permute-done | bytes 196640 | tf_op jit(solution)/shard_map/ppermute | solution.py:65
  204.4 6.4 %convolution_reduce_fusion = f32[65]{0:T(128)S(1)} fusion(bf16[65,4096]{1,0:T(8,128)(2,1)S(1)} %fusion.43, bf16[1024,4096]{1,0:T(8,128)(2,1)} %param.39), kind=kOutput, calls=%fused_computation.67 | convolution fusion | flops 545326016 | bytes 8921348 | tf_op jit(solution)/shard_map/dot_general | solution.py:307
  230.3 3.4 %collective-permute-start.36 = (f32[65]{0:T(128)S(1)}, f32[65]{0:T(128)S(1)}, u32[]{:S(2)}, u32[]{:S(2)}) collective-permute-start(f32[65]{0:T(128)S(1)} %maximum_maximum_fusion), channel_id=1, source_target_pairs={{0,64},{4,68},{8,72},{12,76},{16,80},{20,84},{24,88},{28,92},{32,9... | collective-permute-start | bytes 788 | tf_op jit(solution)/shard_map/ppermute | solution.py:84
  (316 shorter events, 104.5 us)
Async XLA Ops:
  3.9 25.2 %collective-permute-start.2 = (f32[16]{0:T(128)S(1)}, f32[16]{0:T(128)S(1)}, u32[]{:S(2)}, u32[]{:S(2)}) collective-permute-start(f32[16]{0:T(128)S(1)} %slice_reduce_fusion.5), channel_id=1, source_target_pairs={{0,4},{4,8},{8,12},{12,16},{16,20},{20,24},{24,28},{28,32},{32,36}... | collective-permute-start | bytes 200 | tf_op jit(solution)/shard_map/ppermute | solution.py:19
  5.6 23.4 %collective-permute-start.3 = (f32[16]{0:T(128)S(1)}, f32[16]{0:T(128)S(1)}, u32[]{:S(2)}, u32[]{:S(2)}) collective-permute-start(f32[16]{0:T(128)S(1)} %slice_reduce_fusion.5), channel_id=1, source_target_pairs={{0,8},{4,12},{8,16},{12,20},{16,24},{20,28},{24,32},{28,36},{32,40... | collective-permute-start | bytes 200 | tf_op jit(solution)/shard_map/ppermute | solution.py:19
  10.4 23.8 %collective-permute-start = (bf16[3,1024]{1,0:T(4,128)(2,1)S(1)}, bf16[3,1024]{1,0:T(4,128)(2,1)S(1)}, u32[]{:S(2)}, u32[]{:S(2)}) collective-permute-start(bf16[3,1024]{1,0:T(4,128)(2,1)S(1)} %slice.211), channel_id=1, source_target_pairs={{0,4},{4,8},{8,12},{12,16},{16,20},{20,24},{24,28},{28,32},{32,36}... | collective-permute-start | bytes 18440 | tf_op jit(solution)/shard_map/ppermute | solution.py:19
  15.0 18.1 %collective-permute-start.1 = (bf16[3,2,128]{2,0,1:T(4,128)(2,1)S(1)}, bf16[3,2,128]{2,0,1:T(4,128)(2,1)S(1)}, u32[]{:S(2)}, u32[]{:S(2)}) collective-permute-start(bf16[3,2,128]{2,0,1:T(4,128)(2,1)S(1)} %slice.277), channel_id=1, source_target_pairs={{0,4},{4,8},{8,12},{12,16},{16,20},{20,24},{24,28},{28,32},{32,36}... | collective-permute-start | bytes 4616 | tf_op jit(solution)/shard_map/ppermute | solution.py:19
  29.6 13.7 %collective-permute-start.4 = (f32[16]{0:T(128)S(1)}, f32[16]{0:T(128)S(1)}, u32[]{:S(2)}, u32[]{:S(2)}) collective-permute-start(f32[16]{0:T(128)S(1)} %get-tuple-element.39), channel_id=1, source_target_pairs={{0,8},{4,12},{8,16},{12,20},{16,24},{20,28},{24,32},{28,36},{32,40... | collective-permute-start | bytes 200 | tf_op jit(solution)/shard_map/ppermute | solution.py:19
  37.8 17.8 %collective-permute-start.8 = (bf16[16,64,128]{2,1,0:T(8,128)(2,1)S(1)}, bf16[16,64,128]{2,1,0:T(8,128)(2,1)S(1)}, u32[]{:S(2)}, u32[]{:S(2)}) collective-permute-start(bf16[16,64,128]{2,1,0:T(8,128)(2,1)S(1)} %get-tuple-element.95), channel_id=1, source_target_pairs={{0,4},{4,8},{8,12},{12,16},{16,20},{20,24},{24,28},{28,32},{32,36}... | collective-permute-start | bytes 786440 | tf_op jit(solution)/shard_map/ppermute | solution.py:19
  39.6 16.0 %collective-permute-start.7 = (bf16[16,64,128]{2,1,0:T(8,128)(2,1)S(1)}, bf16[16,64,128]{2,1,0:T(8,128)(2,1)S(1)}, u32[]{:S(2)}, u32[]{:S(2)}) collective-permute-start(bf16[16,64,128]{2,1,0:T(8,128)(2,1)S(1)} %get-tuple-element.95), channel_id=1, source_target_pairs={{0,8},{4,12},{8,16},{12,20},{16,24},{20,28},{24,32},{28,36},{32,40... | collective-permute-start | bytes 786440 | tf_op jit(solution)/shard_map/ppermute | solution.py:19
  43.8 6.7 %collective-permute-start.5 = (f32[16]{0:T(128)S(1)}, f32[16]{0:T(128)S(1)}, u32[]{:S(2)}, u32[]{:S(2)}) collective-permute-start(f32[16]{0:T(128)S(1)} %get-tuple-element.37), channel_id=1, source_target_pairs={{0,16},{4,20},{8,24},{12,28},{16,32},{20,36},{24,40},{28,44},{32,4... | collective-permute-start | bytes 200 | tf_op jit(solution)/shard_map/ppermute | solution.py:19
  51.1 8.7 %collective-permute-start.6 = (f32[16]{0:T(128)S(1)}, f32[16]{0:T(128)S(1)}, u32[]{:S(2)}, u32[]{:S(2)}) collective-permute-start(f32[16]{0:T(128)S(1)} %get-tuple-element.35), channel_id=1, source_target_pairs={{0,32},{4,36},{8,40},{12,44},{16,48},{20,52},{24,56},{28,60},{32,6... | collective-permute-start | bytes 200 | tf_op jit(solution)/shard_map/ppermute | solution.py:19
  55.8 9.6 %collective-permute-start.9 = (bf16[16,64,128]{2,1,0:T(8,128)(2,1)S(1)}, bf16[16,64,128]{2,1,0:T(8,128)(2,1)S(1)}, u32[]{:S(2)}, u32[]{:S(2)}) collective-permute-start(bf16[16,64,128]{2,1,0:T(8,128)(2,1)S(1)} %fusion.71), channel_id=1, source_target_pairs={{0,8},{4,12},{8,16},{12,20},{16,24},{20,28},{24,32},{28,36},{32,40... | collective-permute-start | bytes 786440 | tf_op jit(solution)/shard_map/ppermute | solution.py:19
  66.3 9.2 %collective-permute-start.10 = (bf16[16,64,128]{2,1,0:T(8,128)(2,1)S(1)}, bf16[16,64,128]{2,1,0:T(8,128)(2,1)S(1)}, u32[]{:S(2)}, u32[]{:S(2)}) collective-permute-start(bf16[16,64,128]{2,1,0:T(8,128)(2,1)S(1)} %fusion.144), channel_id=1, source_target_pairs={{0,16},{4,20},{8,24},{12,28},{16,32},{20,36},{24,40},{28,44},{32,4... | collective-permute-start | bytes 786440 | tf_op jit(solution)/shard_map/ppermute | solution.py:19
  77.2 13.9 %collective-permute-start.11 = (bf16[16,64,128]{2,1,0:T(8,128)(2,1)}, bf16[16,64,128]{2,1,0:T(8,128)(2,1)}, u32[]{:S(2)}, u32[]{:S(2)}) collective-permute-start(bf16[16,64,128]{2,1,0:T(8,128)(2,1)} %fusion.72), channel_id=1, source_target_pairs={{0,32},{4,36},{8,40},{12,44},{16,48},{20,52},{24,56},{28,60},{32,6... | collective-permute-start | bytes 786440 | tf_op jit(solution)/shard_map/ppermute | solution.py:19
  92.4 7.8 %collective-permute-start.12 = (bf16[16,64,128]{2,1,0:T(8,128)(2,1)S(1)}, bf16[16,64,128]{2,1,0:T(8,128)(2,1)S(1)}, u32[]{:S(2)}, u32[]{:S(2)}) collective-permute-start(bf16[16,64,128]{2,1,0:T(8,128)(2,1)S(1)} %get-tuple-element.32), channel_id=1, source_target_pairs={{0,64},{4,68},{8,72},{12,76},{16,80},{20,84},{24,88},{28,92},{32,9... | collective-permute-start | bytes 786440 | tf_op jit(solution)/shard_map/ppermute | solution.py:19
  114.1 35.9 %collective-permute-start.15 = (bf16[816,1024]{1,0:T(8,128)(2,1)S(1)}, bf16[816,1024]{1,0:T(8,128)(2,1)}, u32[]{:S(2)}, u32[]{:S(2)}) collective-permute-start(bf16[816,1024]{1,0:T(8,128)(2,1)S(1)} %pad_maximum_fusion.1), channel_id=1, source_target_pairs={{0,3},{1,0},{2,1},{3,2},{4,7},{5,4},{6,5},{7,6},{8,11},{9,8},{10,9... | collective-permute-start | bytes 5013512 | tf_op jit(solution)/shard_map/ppermute | solution.py:277
  117.8 36.9 %collective-permute-start.13 = (bf16[816,1024]{1,0:T(8,128)(2,1)S(1)}, bf16[816,1024]{1,0:T(8,128)(2,1)}, u32[]{:S(2)}, u32[]{:S(2)}) collective-permute-start(bf16[816,1024]{1,0:T(8,128)(2,1)S(1)} %pad_maximum_fusion), channel_id=1, source_target_pairs={{0,1},{1,2},{2,3},{3,0},{4,5},{5,6},{6,7},{7,4},{8,9},{9,10},{10,1... | collective-permute-start | bytes 5013512 | tf_op jit(solution)/shard_map/ppermute | solution.py:276
  151.1 11.0 %collective-permute-start.16 = (bf16[272,1024]{1,0:T(8,128)(2,1)S(1)}, bf16[272,1024]{1,0:T(8,128)(2,1)S(1)}, u32[]{:S(2)}, u32[]{:S(2)}) collective-permute-start(bf16[272,1024]{1,0:T(8,128)(2,1)S(1)} %slice.301), channel_id=1, source_target_pairs={{0,3},{1,0},{2,1},{3,2},{4,7},{5,4},{6,5},{7,6},{8,11},{9,8},{10,9... | collective-permute-start | bytes 1671176 | tf_op jit(solution)/shard_map/ppermute | solution.py:279
  155.7 11.9 %collective-permute-start.14 = (bf16[272,1024]{1,0:T(8,128)(2,1)S(1)}, bf16[272,1024]{1,0:T(8,128)(2,1)S(1)}, u32[]{:S(2)}, u32[]{:S(2)}) collective-permute-start(bf16[272,1024]{1,0:T(8,128)(2,1)S(1)} %slice.299), channel_id=1, source_target_pairs={{0,1},{1,2},{2,3},{3,0},{4,5},{5,6},{6,7},{7,4},{8,9},{9,10},{10,1... | collective-permute-start | bytes 1671176 | tf_op jit(solution)/shard_map/ppermute | solution.py:278
  175.5 5.7 %collective-permute-start.22 = (bf16[12,1024]{1,0:T(8,128)(2,1)S(1)}, bf16[12,1024]{1,0:T(8,128)(2,1)S(1)}, u32[]{:S(2)}, u32[]{:S(2)}) collective-permute-start(bf16[12,1024]{1,0:T(8,128)(2,1)S(1)} %get-tuple-element.61), channel_id=1, source_target_pairs={{0,48},{4,52},{8,56},{12,60},{16,0},{20,4},{24,8},{28,12},{32,16},... | collective-permute-start | bytes 73736 | tf_op jit(solution)/shard_map/ppermute | solution.py:65
  178.4 6.3 %collective-permute-start.20 = (bf16[12,1024]{1,0:T(8,128)(2,1)S(1)}, bf16[12,1024]{1,0:T(8,128)(2,1)S(1)}, u32[]{:S(2)}, u32[]{:S(2)}) collective-permute-start(bf16[12,1024]{1,0:T(8,128)(2,1)S(1)} %get-tuple-element.61), channel_id=1, source_target_pairs={{0,16},{4,20},{8,24},{12,28},{16,32},{20,36},{24,40},{28,44},{32,4... | collective-permute-start | bytes 73736 | tf_op jit(solution)/shard_map/ppermute | solution.py:65
  184.8 6.7 %collective-permute-start.23 = (bf16[48,1024]{1,0:T(8,128)(2,1)S(1)}, bf16[48,1024]{1,0:T(8,128)(2,1)S(1)}, u32[]{:S(2)}, u32[]{:S(2)}) collective-permute-start(bf16[48,1024]{1,0:T(8,128)(2,1)S(1)} %pad_maximum_fusion.9), channel_id=1, source_target_pairs={{0,64},{4,68},{8,72},{12,76},{16,80},{20,84},{24,88},{28,92},{32,9... | collective-permute-start | bytes 294920 | tf_op jit(solution)/shard_map/ppermute | solution.py:65
  191.7 7.8 %collective-permute-start.26 = (bf16[96,1024]{1,0:T(8,128)(2,1)S(1)}, bf16[96,1024]{1,0:T(8,128)(2,1)S(1)}, u32[]{:S(2)}, u32[]{:S(2)}) collective-permute-start(bf16[96,1024]{1,0:T(8,128)(2,1)S(1)} %get-tuple-element.53), channel_id=1, source_target_pairs={{0,3},{1,0},{2,1},{3,2},{4,7},{5,4},{6,5},{7,6},{8,11},{9,8},{10,9... | collective-permute-start | bytes 589832 | tf_op jit(solution)/shard_map/ppermute | solution.py:65
  194.7 7.2 %collective-permute-start.25 = (bf16[96,1024]{1,0:T(8,128)(2,1)S(1)}, bf16[96,1024]{1,0:T(8,128)(2,1)S(1)}, u32[]{:S(2)}, u32[]{:S(2)}) collective-permute-start(bf16[96,1024]{1,0:T(8,128)(2,1)S(1)} %get-tuple-element.53), channel_id=1, source_target_pairs={{0,2},{1,3},{2,0},{3,1},{4,6},{5,7},{6,4},{7,5},{8,10},{9,11},{10,... | collective-permute-start | bytes 589832 | tf_op jit(solution)/shard_map/ppermute | solution.py:65
  194.7 7.2 %collective-permute-start.24 = (bf16[96,1024]{1,0:T(8,128)(2,1)S(1)}, bf16[96,1024]{1,0:T(8,128)(2,1)S(1)}, u32[]{:S(2)}, u32[]{:S(2)}) collective-permute-start(bf16[96,1024]{1,0:T(8,128)(2,1)S(1)} %get-tuple-element.53), channel_id=1, source_target_pairs={{0,1},{1,2},{2,3},{3,0},{4,5},{5,6},{6,7},{7,4},{8,9},{9,10},{10,1... | collective-permute-start | bytes 589832 | tf_op jit(solution)/shard_map/ppermute | solution.py:65
  224.4 6.0 %collective-permute-start.33 = (f32[65]{0:T(128)S(1)}, f32[65]{0:T(128)S(1)}, u32[]{:S(2)}, u32[]{:S(2)}) collective-permute-start(f32[65]{0:T(128)S(1)} %maximum_maximum_fusion.1), channel_id=1, source_target_pairs={{0,16},{4,20},{8,24},{12,28},{16,32},{20,36},{24,40},{28,44},{32,4... | collective-permute-start | bytes 788 | tf_op jit(solution)/shard_map/ppermute | solution.py:84
  (75 other events, 893.2 us)

commit v6 on v2

--- a/solution.py
+++ b/solution.py
@@ -270,8 +270,10 @@
         piece = lax.dynamic_slice_in_dim(out_weight, target * width, width, 1)
         term = jnp.dot(all_normed, piece, preferred_element_type=jnp.float32).astype(jnp.bfloat16)
         if step:
-            term = lax.ppermute(
-                term, "tp", [(i, (i + step) % tp_count) for i in range(tp_count)]
+            route = [(i, (i + step) % tp_count) for i in range(tp_count)]
+            half = term.shape[0] // 2
+            term = jnp.concatenate(
+                [lax.ppermute(term[:half], "tp", route), lax.ppermute(term[half:], "tp", route)], 0
             )
         total = term.astype(jnp.float32) if total is None else total + term.astype(jnp.float32)
     hidden = total.astype(jnp.bfloat16)

time: 236 us -> 239 us (1.013)
  matrix products: 41.8 us -> 34.3 us
  starting transfers between devices: 89.6 us -> 94.6 us
  other arithmetic: 22.9 us -> 26.1 us
    dot_general x4, matrix products: 16.1 us -> 8.75 us  [local(): jnp.dot(all_normed, piece, preferred_element_type=jnp.float32)]
    ppermute x3 -> x6, starting transfers between devices: 4.34 us -> 8.84 us  [the longest x3 5.24 us: local(): lax.ppermute(term[half:], 'tp', route)]
    ppermute x3 -> x6, waiting for transfers between devices: 36.8 us -> 39.5 us  [the longest x3 35 us: local(): lax.ppermute(term[half:], 'tp', route)]
  transfers between devices with their start and end apart: 36 -> 39, of which waited for: 18 -> 20; matrix products, arithmetic and copies ran while one was open for 20% -> 20% of each run, Pallas kernels for 0% -> 0%
where the time goes in v6:
time: 239 us; the launch traced here: 237 us
  starting transfers between devices  94.6 us (40%)
  waiting for transfers between devices  63.9 us (27%)
  matrix products  34.3 us (14%)
  other arithmetic  26.1 us (11%)
  local copies, waits for them, and re-layouts  15.6 us (7%)
    ppermute x13, starting transfers between devices, passed_along(): return lax.ppermute(block, axis, route)  49.6 us
    ppermute x3, waiting for transfers between devices, local(): lax.ppermute(term[half:], 'tp', route)  35 us
    ppermute x10, starting transfers between devices, gather_fast(): lax.ppermute(block, axis, digit_route(count, distance, step, radix))  18.3 us
    ppermute x10, starting transfers between devices, max_fast(): lax.ppermute(block, axis, digit_route(count, distance, step, radix))  17.8 us
    ppermute x10, waiting for transfers between devices, gather_fast(): lax.ppermute(block, axis, digit_route(count, distance, step, radix))  11 us
    dot_general x4, matrix products, local(): jnp.dot(all_normed, piece, preferred_element_type=jnp.float32)  8.75 us
    ppermute x13, waiting for transfers between devices, passed_along(): return lax.ppermute(block, axis, route)  8.08 us
    dot_general x3, matrix products, ssd_block(): jnp.einsum('hts,shp->thp', weights, x_block, preferred_element_type=jnp.f...  7.69 us
  transfers between devices with their start and end apart: 39, of which 20 were waited for; matrix products, arithmetic and copies ran while one was open for 20% of the time, Pallas kernels for 0%

profile of v6, /device:TPU:8, one launch (start us, length us, event | category | flops | bytes accessed | tf_op | source)
XLA Modules:
  0.0 236.5 jit_solution(14659221806035516786)
XLA Ops:
  5.6 4.0 %collective-permute-start.3 = (f32[16]{0:T(128)S(1)}, f32[16]{0:T(128)S(1)}, u32[]{:S(2)}, u32[]{:S(2)}) collective-permute-start(f32[16]{0:T(128)S(1)} %slice_reduce_fusion.5), channel_id=1, source_target_pairs={{0,8},{4,12},{8,16},{12,20},{16,24},{20,28},{24,32},{28,36},{32,40... | collective-permute-start | bytes 200 | tf_op jit(solution)/shard_map/ppermute | solution.py:19
  10.6 3.6 %collective-permute-start.1 = (bf16[3,2,128]{2,0,1:T(4,128)(2,1)S(1)}, bf16[3,2,128]{2,0,1:T(4,128)(2,1)S(1)}, u32[]{:S(2)}, u32[]{:S(2)}) collective-permute-start(bf16[3,2,128]{2,0,1:T(4,128)(2,1)S(1)} %slice.277), channel_id=1, source_target_pairs={{0,4},{4,8},{8,12},{12,16},{16,20},{20,24},{24,28},{28,32},{32,36}... | collective-permute-start | bytes 4616 | tf_op jit(solution)/shard_map/ppermute | solution.py:19
  32.6 3.5 %collective-permute-start.4 = (f32[16]{0:T(128)S(1)}, f32[16]{0:T(128)S(1)}, u32[]{:S(2)}, u32[]{:S(2)}) collective-permute-start(f32[16]{0:T(128)S(1)} %get-tuple-element.39), channel_id=1, source_target_pairs={{0,8},{4,12},{8,16},{12,20},{16,24},{20,28},{24,32},{28,36},{32,40... | collective-permute-start | bytes 200 | tf_op jit(solution)/shard_map/ppermute | solution.py:19
  42.9 3.1 %collective-permute-start.8 = (bf16[16,64,128]{2,1,0:T(8,128)(2,1)S(1)}, bf16[16,64,128]{2,1,0:T(8,128)(2,1)S(1)}, u32[]{:S(2)}, u32[]{:S(2)}) collective-permute-start(bf16[16,64,128]{2,1,0:T(8,128)(2,1)S(1)} %get-tuple-element.99), channel_id=1, source_target_pairs={{0,4},{4,8},{8,12},{12,16},{16,20},{20,24},{24,28},{28,32},{32,36}... | collective-permute-start | bytes 786440 | tf_op jit(solution)/shard_map/ppermute | solution.py:19
  46.6 5.5 %collective-permute-start.5 = (f32[16]{0:T(128)S(1)}, f32[16]{0:T(128)S(1)}, u32[]{:S(2)}, u32[]{:S(2)}) collective-permute-start(f32[16]{0:T(128)S(1)} %get-tuple-element.37), channel_id=1, source_target_pairs={{0,16},{4,20},{8,24},{12,28},{16,32},{20,36},{24,40},{28,44},{32,4... | collective-permute-start | bytes 200 | tf_op jit(solution)/shard_map/ppermute | solution.py:19
  53.9 4.5 %collective-permute-start.6 = (f32[16]{0:T(128)S(1)}, f32[16]{0:T(128)S(1)}, u32[]{:S(2)}, u32[]{:S(2)}) collective-permute-start(f32[16]{0:T(128)S(1)} %get-tuple-element.35), channel_id=1, source_target_pairs={{0,32},{4,36},{8,40},{12,44},{16,48},{20,52},{24,56},{28,60},{32,6... | collective-permute-start | bytes 200 | tf_op jit(solution)/shard_map/ppermute | solution.py:19
  59.3 3.8 %collective-permute-start.9 = (bf16[16,64,128]{2,1,0:T(8,128)(2,1)S(1)}, bf16[16,64,128]{2,1,0:T(8,128)(2,1)S(1)}, u32[]{:S(2)}, u32[]{:S(2)}) collective-permute-start(bf16[16,64,128]{2,1,0:T(8,128)(2,1)S(1)} %fusion.71), channel_id=1, source_target_pairs={{0,8},{4,12},{8,16},{12,20},{16,24},{20,28},{24,32},{28,36},{32,40... | collective-permute-start | bytes 786440 | tf_op jit(solution)/shard_map/ppermute | solution.py:19
  64.3 4.3 %collective-permute-done.9 = bf16[16,64,128]{2,1,0:T(8,128)(2,1)S(1)} collective-permute-done((bf16[16,64,128]{2,1,0:T(8,128)(2,1)S(1)}, bf16[16,64,128]{2,1,0:T(8,128)(2,1)S(1)}, u32[]{:S(2)}, u32[]{:S(2)}) %collective-permute-start.9) | collective-permute-done | bytes 262176 | tf_op jit(solution)/shard_map/ppermute | solution.py:19
  69.5 4.9 %collective-permute-start.10 = (bf16[16,64,128]{2,1,0:T(8,128)(2,1)S(1)}, bf16[16,64,128]{2,1,0:T(8,128)(2,1)S(1)}, u32[]{:S(2)}, u32[]{:S(2)}) collective-permute-start(bf16[16,64,128]{2,1,0:T(8,128)(2,1)S(1)} %fusion.144), channel_id=1, source_target_pairs={{0,16},{4,20},{8,24},{12,28},{16,32},{20,36},{24,40},{28,44},{32,4... | collective-permute-start | bytes 786440 | tf_op jit(solution)/shard_map/ppermute | solution.py:19
  74.4 3.7 %fusion.33 = f32[256,16,64]{0,2,1:T(8,128)} fusion(bf16[256,16,64]{0,2,1:T(8,128)(2,1)S(1)} %bitcast.222, f32[16,256]{1,0:T(8,128)} %get-tuple-element.101, f32[16,256]{1,0:T(8,128)} %copy-done.29, pred[256,256]{1,0:T(8,128)(4,1)} %iota_compare_fusion, bf16[256,128]{1,0:T(8,128)(2,1)S(1)} %get-tuple-element.53, bf16[256,128]{1,0:T(8,128)(2,1)} %get-tuple-element.54), kind=kOutput, calls=%fused_computation.41 | convolution fusion | flops 408944640 | bytes 1802240 | tf_op jit(solution)/shard_map/hts,shp->thp/dot_general | solution.py:136
  80.4 8.1 %collective-permute-start.11 = (bf16[16,64,128]{2,1,0:T(8,128)(2,1)}, bf16[16,64,128]{2,1,0:T(8,128)(2,1)}, u32[]{:S(2)}, u32[]{:S(2)}) collective-permute-start(bf16[16,64,128]{2,1,0:T(8,128)(2,1)} %fusion.72), channel_id=1, source_target_pairs={{0,32},{4,36},{8,40},{12,44},{16,48},{20,52},{24,56},{28,60},{32,6... | collective-permute-start | bytes 786440 | tf_op jit(solution)/shard_map/ppermute | solution.py:19
  88.5 3.7 %fusion.34 = f32[256,16,64]{0,2,1:T(8,128)} fusion(bf16[256,16,64]{0,2,1:T(8,128)(2,1)S(1)} %bitcast.224, f32[16,256]{1,0:T(8,128)} %get-tuple-element.102, f32[16,256]{1,0:T(8,128)} %copy-done.28, pred[256,256]{1,0:T(8,128)(4,1)} %iota_compare_fusion, bf16[256,128]{1,0:T(8,128)(2,1)} %copy-done.27, bf16[256,128]{1,0:T(8,128)(2,1)S(1)} %get-tuple-element.52), kind=kOutput, calls=%fused_computation.42 | convolution fusion | flops 408944640 | bytes 1802240 | tf_op jit(solution)/shard_map/hts,shp->thp/dot_general | solution.py:136
  103.4 3.7 %fusion.10 = f32[512,16,64]{0,2,1:T(8,128)} fusion(f32[512,16,64]{0,2,1:T(8,128)S(1)} %bitcast.219, f32[512,16,64]{0,2,1:T(8,128)S(1)} %bitcast.218, f32[16]{0:T(128)S(1)} %copy-done.51, bf16[512,128]{1,0:T(8,128)(2,1)S(1)} %copy-done.16, f32[512,16]{0,1:T(8,128)S(1)} %copy-done.22, f32[16,64,128]{2,1,0:T(8,128)S(1)} %get-tuple-element.33, ...), kind=kOutput, calls=%fused_computation.19 | convolution fusion | flops 807796736 | bytes 7241856 | tf_op jit(solution)/shard_map/thn,hpn->thp/dot_general | solution.py:208
  110.8 3.1 %fusion.22 = bf16[544,1024]{1,0:T(8,128)(2,1)S(1)} fusion(bf16[1024,4096]{1,0:T(8,128)(2,1)} %param.37, s32[]{:T(128)S(6)} %select_n.195, bf16[32,1024]{1,0:T(8,128)(2,1)S(1)} %copy-done.26, bf16[512,1024]{1,0:T(8,128)(2,1)S(1)} %multiply_convert_fusion.2), kind=kOutput, calls=%fused_computation.32 | convolution fusion | flops 1143635968 | bytes 4325380 | tf_op jit(solution)/shard_map/dot_general | solution.py:271
  125.0 4.5 %collective-permute-done.15 = bf16[272,1024]{1,0:T(8,128)(2,1)S(1)} collective-permute-done((bf16[272,1024]{1,0:T(8,128)(2,1)S(1)}, bf16[272,1024]{1,0:T(8,128)(2,1)S(1)}, u32[]{:S(2)}, u32[]{:S(2)}) %collective-permute-start.15) | collective-permute-done | bytes 557088 | tf_op jit(solution)/shard_map/ppermute | solution.py:276
  132.2 9.3 %collective-permute-done.16 = bf16[272,1024]{1,0:T(8,128)(2,1)S(1)} collective-permute-done((bf16[272,1024]{1,0:T(8,128)(2,1)S(1)}, bf16[272,1024]{1,0:T(8,128)(2,1)S(1)}, u32[]{:S(2)}, u32[]{:S(2)}) %collective-permute-start.16) | collective-permute-done | bytes 557088 | tf_op jit(solution)/shard_map/ppermute | solution.py:276
  141.5 25.7 %collective-permute-done.18 = bf16[272,1024]{1,0:T(8,128)(2,1)S(1)} collective-permute-done((bf16[272,1024]{1,0:T(8,128)(2,1)S(1)}, bf16[272,1024]{1,0:T(8,128)(2,1)S(1)}, u32[]{:S(2)}, u32[]{:S(2)}) %collective-permute-start.18) | collective-permute-done | bytes 557088 | tf_op jit(solution)/shard_map/ppermute | solution.py:276
  169.0 3.4 %collective-permute-start.20 = (bf16[3,1024]{1,0:T(4,128)(2,1)S(1)}, bf16[3,1024]{1,0:T(4,128)(2,1)S(1)}, u32[]{:S(2)}, u32[]{:S(2)}) collective-permute-start(bf16[3,1024]{1,0:T(4,128)(2,1)S(1)} %get-tuple-element.85), channel_id=1, source_target_pairs={{0,8},{4,12},{8,0},{12,4},{16,24},{20,28},{24,16},{28,20},{32,40},... | collective-permute-start | bytes 18440 | tf_op jit(solution)/shard_map/ppermute | solution.py:65
  175.8 3.9 %collective-permute-start.24 = (bf16[12,1024]{1,0:T(8,128)(2,1)S(1)}, bf16[12,1024]{1,0:T(8,128)(2,1)S(1)}, u32[]{:S(2)}, u32[]{:S(2)}) collective-permute-start(bf16[12,1024]{1,0:T(8,128)(2,1)S(1)} %get-tuple-element.65), channel_id=1, source_target_pairs={{0,48},{4,52},{8,56},{12,60},{16,0},{20,4},{24,8},{28,12},{32,16},... | collective-permute-start | bytes 73736 | tf_op jit(solution)/shard_map/ppermute | solution.py:65
  182.2 4.1 %collective-permute-start.25 = (bf16[48,1024]{1,0:T(8,128)(2,1)S(1)}, bf16[48,1024]{1,0:T(8,128)(2,1)S(1)}, u32[]{:S(2)}, u32[]{:S(2)}) collective-permute-start(bf16[48,1024]{1,0:T(8,128)(2,1)S(1)} %pad_maximum_fusion.7), channel_id=1, source_target_pairs={{0,64},{4,68},{8,72},{12,76},{16,80},{20,84},{24,88},{28,92},{32,9... | collective-permute-start | bytes 294920 | tf_op jit(solution)/shard_map/ppermute | solution.py:65
  202.8 6.4 %convolution_reduce_fusion = f32[65]{0:T(128)S(1)} fusion(bf16[65,4096]{1,0:T(8,128)(2,1)S(1)} %fusion.43, bf16[1024,4096]{1,0:T(8,128)(2,1)} %param.39), kind=kOutput, calls=%fused_computation.65 | convolution fusion | flops 545326016 | bytes 8921348 | tf_op jit(solution)/shard_map/dot_general | solution.py:301
  216.2 2.9 %collective-permute-start.33 = (f32[65]{0:T(128)S(1)}, f32[65]{0:T(128)S(1)}, u32[]{:S(2)}, u32[]{:S(2)}) collective-permute-start(f32[65]{0:T(128)S(1)} %maximum_maximum_fusion.2), channel_id=1, source_target_pairs={{0,8},{4,12},{8,0},{12,4},{16,24},{20,28},{24,16},{28,20},{32,40},... | collective-permute-start | bytes 788 | tf_op jit(solution)/shard_map/ppermute | solution.py:84
  221.8 3.9 %collective-permute-start.35 = (f32[65]{0:T(128)S(1)}, f32[65]{0:T(128)S(1)}, u32[]{:S(2)}, u32[]{:S(2)}) collective-permute-start(f32[65]{0:T(128)S(1)} %maximum_maximum_fusion.1), channel_id=1, source_target_pairs={{0,16},{4,20},{8,24},{12,28},{16,32},{20,36},{24,40},{28,44},{32,4... | collective-permute-start | bytes 788 | tf_op jit(solution)/shard_map/ppermute | solution.py:84
  230.8 3.2 %collective-permute-start.38 = (f32[65]{0:T(128)S(1)}, f32[65]{0:T(128)S(1)}, u32[]{:S(2)}, u32[]{:S(2)}) collective-permute-start(f32[65]{0:T(128)S(1)} %maximum_maximum_fusion), channel_id=1, source_target_pairs={{0,64},{4,68},{8,72},{12,76},{16,80},{20,84},{24,88},{28,92},{32,9... | collective-permute-start | bytes 788 | tf_op jit(solution)/shard_map/ppermute | solution.py:84
  (307 shorter events, 107.9 us)
Async XLA Ops:
  3.9 28.1 %collective-permute-start.2 = (f32[16]{0:T(128)S(1)}, f32[16]{0:T(128)S(1)}, u32[]{:S(2)}, u32[]{:S(2)}) collective-permute-start(f32[16]{0:T(128)S(1)} %slice_reduce_fusion.5), channel_id=1, source_target_pairs={{0,4},{4,8},{8,12},{12,16},{16,20},{20,24},{24,28},{28,32},{32,36}... | collective-permute-start | bytes 200 | tf_op jit(solution)/shard_map/ppermute | solution.py:19
  5.6 26.4 %collective-permute-start.3 = (f32[16]{0:T(128)S(1)}, f32[16]{0:T(128)S(1)}, u32[]{:S(2)}, u32[]{:S(2)}) collective-permute-start(f32[16]{0:T(128)S(1)} %slice_reduce_fusion.5), channel_id=1, source_target_pairs={{0,8},{4,12},{8,16},{12,20},{16,24},{20,28},{24,32},{28,36},{32,40... | collective-permute-start | bytes 200 | tf_op jit(solution)/shard_map/ppermute | solution.py:19
  10.6 25.5 %collective-permute-start.1 = (bf16[3,2,128]{2,0,1:T(4,128)(2,1)S(1)}, bf16[3,2,128]{2,0,1:T(4,128)(2,1)S(1)}, u32[]{:S(2)}, u32[]{:S(2)}) collective-permute-start(bf16[3,2,128]{2,0,1:T(4,128)(2,1)S(1)} %slice.277), channel_id=1, source_target_pairs={{0,4},{4,8},{8,12},{12,16},{16,20},{20,24},{24,28},{28,32},{32,36}... | collective-permute-start | bytes 4616 | tf_op jit(solution)/shard_map/ppermute | solution.py:19
  15.0 22.2 %collective-permute-start = (bf16[3,1024]{1,0:T(4,128)(2,1)S(1)}, bf16[3,1024]{1,0:T(4,128)(2,1)S(1)}, u32[]{:S(2)}, u32[]{:S(2)}) collective-permute-start(bf16[3,1024]{1,0:T(4,128)(2,1)S(1)} %slice.211), channel_id=1, source_target_pairs={{0,4},{4,8},{8,12},{12,16},{16,20},{20,24},{24,28},{28,32},{32,36}... | collective-permute-start | bytes 18440 | tf_op jit(solution)/shard_map/ppermute | solution.py:19
  32.6 13.4 %collective-permute-start.4 = (f32[16]{0:T(128)S(1)}, f32[16]{0:T(128)S(1)}, u32[]{:S(2)}, u32[]{:S(2)}) collective-permute-start(f32[16]{0:T(128)S(1)} %get-tuple-element.39), channel_id=1, source_target_pairs={{0,8},{4,12},{8,16},{12,20},{16,24},{20,28},{24,32},{28,36},{32,40... | collective-permute-start | bytes 200 | tf_op jit(solution)/shard_map/ppermute | solution.py:19
  40.8 17.6 %collective-permute-start.7 = (bf16[16,64,128]{2,1,0:T(8,128)(2,1)S(1)}, bf16[16,64,128]{2,1,0:T(8,128)(2,1)S(1)}, u32[]{:S(2)}, u32[]{:S(2)}) collective-permute-start(bf16[16,64,128]{2,1,0:T(8,128)(2,1)S(1)} %get-tuple-element.99), channel_id=1, source_target_pairs={{0,8},{4,12},{8,16},{12,20},{16,24},{20,28},{24,32},{28,36},{32,40... | collective-permute-start | bytes 786440 | tf_op jit(solution)/shard_map/ppermute | solution.py:19
  42.9 15.5 %collective-permute-start.8 = (bf16[16,64,128]{2,1,0:T(8,128)(2,1)S(1)}, bf16[16,64,128]{2,1,0:T(8,128)(2,1)S(1)}, u32[]{:S(2)}, u32[]{:S(2)}) collective-permute-start(bf16[16,64,128]{2,1,0:T(8,128)(2,1)S(1)} %get-tuple-element.99), channel_id=1, source_target_pairs={{0,4},{4,8},{8,12},{12,16},{16,20},{20,24},{24,28},{28,32},{32,36}... | collective-permute-start | bytes 786440 | tf_op jit(solution)/shard_map/ppermute | solution.py:19
  46.6 6.7 %collective-permute-start.5 = (f32[16]{0:T(128)S(1)}, f32[16]{0:T(128)S(1)}, u32[]{:S(2)}, u32[]{:S(2)}) collective-permute-start(f32[16]{0:T(128)S(1)} %get-tuple-element.37), channel_id=1, source_target_pairs={{0,16},{4,20},{8,24},{12,28},{16,32},{20,36},{24,40},{28,44},{32,4... | collective-permute-start | bytes 200 | tf_op jit(solution)/shard_map/ppermute | solution.py:19
  53.9 9.2 %collective-permute-start.6 = (f32[16]{0:T(128)S(1)}, f32[16]{0:T(128)S(1)}, u32[]{:S(2)}, u32[]{:S(2)}) collective-permute-start(f32[16]{0:T(128)S(1)} %get-tuple-element.35), channel_id=1, source_target_pairs={{0,32},{4,36},{8,40},{12,44},{16,48},{20,52},{24,56},{28,60},{32,6... | collective-permute-start | bytes 200 | tf_op jit(solution)/shard_map/ppermute | solution.py:19
  59.3 9.3 %collective-permute-start.9 = (bf16[16,64,128]{2,1,0:T(8,128)(2,1)S(1)}, bf16[16,64,128]{2,1,0:T(8,128)(2,1)S(1)}, u32[]{:S(2)}, u32[]{:S(2)}) collective-permute-start(bf16[16,64,128]{2,1,0:T(8,128)(2,1)S(1)} %fusion.71), channel_id=1, source_target_pairs={{0,8},{4,12},{8,16},{12,20},{16,24},{20,28},{24,32},{28,36},{32,40... | collective-permute-start | bytes 786440 | tf_op jit(solution)/shard_map/ppermute | solution.py:19
  69.5 9.2 %collective-permute-start.10 = (bf16[16,64,128]{2,1,0:T(8,128)(2,1)S(1)}, bf16[16,64,128]{2,1,0:T(8,128)(2,1)S(1)}, u32[]{:S(2)}, u32[]{:S(2)}) collective-permute-start(bf16[16,64,128]{2,1,0:T(8,128)(2,1)S(1)} %fusion.144), channel_id=1, source_target_pairs={{0,16},{4,20},{8,24},{12,28},{16,32},{20,36},{24,40},{28,44},{32,4... | collective-permute-start | bytes 786440 | tf_op jit(solution)/shard_map/ppermute | solution.py:19
  80.4 15.3 %collective-permute-start.11 = (bf16[16,64,128]{2,1,0:T(8,128)(2,1)}, bf16[16,64,128]{2,1,0:T(8,128)(2,1)}, u32[]{:S(2)}, u32[]{:S(2)}) collective-permute-start(bf16[16,64,128]{2,1,0:T(8,128)(2,1)} %fusion.72), channel_id=1, source_target_pairs={{0,32},{4,36},{8,40},{12,44},{16,48},{20,52},{24,56},{28,60},{32,6... | collective-permute-start | bytes 786440 | tf_op jit(solution)/shard_map/ppermute | solution.py:19
  114.0 15.6 %collective-permute-start.15 = (bf16[272,1024]{1,0:T(8,128)(2,1)S(1)}, bf16[272,1024]{1,0:T(8,128)(2,1)S(1)}, u32[]{:S(2)}, u32[]{:S(2)}) collective-permute-start(bf16[272,1024]{1,0:T(8,128)(2,1)S(1)} %get-tuple-element.42), channel_id=1, source_target_pairs={{0,1},{1,2},{2,3},{3,0},{4,5},{5,6},{6,7},{7,4},{8,9},{9,10},{10,1... | collective-permute-start | bytes 1671176 | tf_op jit(solution)/shard_map/ppermute | solution.py:276
  115.6 25.9 %collective-permute-start.16 = (bf16[272,1024]{1,0:T(8,128)(2,1)S(1)}, bf16[272,1024]{1,0:T(8,128)(2,1)S(1)}, u32[]{:S(2)}, u32[]{:S(2)}) collective-permute-start(bf16[272,1024]{1,0:T(8,128)(2,1)S(1)} %get-tuple-element.43), channel_id=1, source_target_pairs={{0,1},{1,2},{2,3},{3,0},{4,5},{5,6},{6,7},{7,4},{8,9},{9,10},{10,1... | collective-permute-start | bytes 1671176 | tf_op jit(solution)/shard_map/ppermute | solution.py:276
  119.9 21.6 %collective-permute-start.17 = (bf16[272,1024]{1,0:T(8,128)(2,1)S(1)}, bf16[272,1024]{1,0:T(8,128)(2,1)S(1)}, u32[]{:S(2)}, u32[]{:S(2)}) collective-permute-start(bf16[272,1024]{1,0:T(8,128)(2,1)S(1)} %get-tuple-element.40), channel_id=1, source_target_pairs={{0,3},{1,0},{2,1},{3,2},{4,7},{5,4},{6,5},{7,6},{8,11},{9,8},{10,9... | collective-permute-start | bytes 1671176 | tf_op jit(solution)/shard_map/ppermute | solution.py:276
  120.7 46.4 %collective-permute-start.18 = (bf16[272,1024]{1,0:T(8,128)(2,1)S(1)}, bf16[272,1024]{1,0:T(8,128)(2,1)S(1)}, u32[]{:S(2)}, u32[]{:S(2)}) collective-permute-start(bf16[272,1024]{1,0:T(8,128)(2,1)S(1)} %get-tuple-element.41), channel_id=1, source_target_pairs={{0,3},{1,0},{2,1},{3,2},{4,7},{5,4},{6,5},{7,6},{8,11},{9,8},{10,9... | collective-permute-start | bytes 1671176 | tf_op jit(solution)/shard_map/ppermute | solution.py:276
  123.8 43.3 %collective-permute-start.13 = (bf16[272,1024]{1,0:T(8,128)(2,1)S(1)}, bf16[272,1024]{1,0:T(8,128)(2,1)S(1)}, u32[]{:S(2)}, u32[]{:S(2)}) collective-permute-start(bf16[272,1024]{1,0:T(8,128)(2,1)S(1)} %get-tuple-element.44), channel_id=1, source_target_pairs={{0,2},{1,3},{2,0},{3,1},{4,6},{5,7},{6,4},{7,5},{8,10},{9,11},{10,... | collective-permute-start | bytes 1671176 | tf_op jit(solution)/shard_map/ppermute | solution.py:276
  129.5 37.6 %collective-permute-start.14 = (bf16[272,1024]{1,0:T(8,128)(2,1)S(1)}, bf16[272,1024]{1,0:T(8,128)(2,1)S(1)}, u32[]{:S(2)}, u32[]{:S(2)}) collective-permute-start(bf16[272,1024]{1,0:T(8,128)(2,1)S(1)} %get-tuple-element.45), channel_id=1, source_target_pairs={{0,2},{1,3},{2,0},{3,1},{4,6},{5,7},{6,4},{7,5},{8,10},{9,11},{10,... | collective-permute-start | bytes 1671176 | tf_op jit(solution)/shard_map/ppermute | solution.py:276
  175.2 6.5 %collective-permute-start.22 = (bf16[12,1024]{1,0:T(8,128)(2,1)S(1)}, bf16[12,1024]{1,0:T(8,128)(2,1)S(1)}, u32[]{:S(2)}, u32[]{:S(2)}) collective-permute-start(bf16[12,1024]{1,0:T(8,128)(2,1)S(1)} %get-tuple-element.65), channel_id=1, source_target_pairs={{0,16},{4,20},{8,24},{12,28},{16,32},{20,36},{24,40},{28,44},{32,4... | collective-permute-start | bytes 73736 | tf_op jit(solution)/shard_map/ppermute | solution.py:65
  182.2 6.7 %collective-permute-start.25 = (bf16[48,1024]{1,0:T(8,128)(2,1)S(1)}, bf16[48,1024]{1,0:T(8,128)(2,1)S(1)}, u32[]{:S(2)}, u32[]{:S(2)}) collective-permute-start(bf16[48,1024]{1,0:T(8,128)(2,1)S(1)} %pad_maximum_fusion.7), channel_id=1, source_target_pairs={{0,64},{4,68},{8,72},{12,76},{16,80},{20,84},{24,88},{28,92},{32,9... | collective-permute-start | bytes 294920 | tf_op jit(solution)/shard_map/ppermute | solution.py:65
  189.0 7.7 %collective-permute-start.26 = (bf16[96,1024]{1,0:T(8,128)(2,1)S(1)}, bf16[96,1024]{1,0:T(8,128)(2,1)S(1)}, u32[]{:S(2)}, u32[]{:S(2)}) collective-permute-start(bf16[96,1024]{1,0:T(8,128)(2,1)S(1)} %get-tuple-element.57), channel_id=1, source_target_pairs={{0,1},{1,2},{2,3},{3,0},{4,5},{5,6},{6,7},{7,4},{8,9},{9,10},{10,1... | collective-permute-start | bytes 589832 | tf_op jit(solution)/shard_map/ppermute | solution.py:65
  189.1 9.0 %collective-permute-start.27 = (bf16[96,1024]{1,0:T(8,128)(2,1)S(1)}, bf16[96,1024]{1,0:T(8,128)(2,1)S(1)}, u32[]{:S(2)}, u32[]{:S(2)}) collective-permute-start(bf16[96,1024]{1,0:T(8,128)(2,1)S(1)} %get-tuple-element.57), channel_id=1, source_target_pairs={{0,2},{1,3},{2,0},{3,1},{4,6},{5,7},{6,4},{7,5},{8,10},{9,11},{10,... | collective-permute-start | bytes 589832 | tf_op jit(solution)/shard_map/ppermute | solution.py:65
  191.4 8.8 %collective-permute-start.28 = (bf16[96,1024]{1,0:T(8,128)(2,1)S(1)}, bf16[96,1024]{1,0:T(8,128)(2,1)S(1)}, u32[]{:S(2)}, u32[]{:S(2)}) collective-permute-start(bf16[96,1024]{1,0:T(8,128)(2,1)S(1)} %get-tuple-element.57), channel_id=1, source_target_pairs={{0,3},{1,0},{2,1},{3,2},{4,7},{5,4},{6,5},{7,6},{8,11},{9,8},{10,9... | collective-permute-start | bytes 589832 | tf_op jit(solution)/shard_map/ppermute | solution.py:65
  221.8 6.6 %collective-permute-start.35 = (f32[65]{0:T(128)S(1)}, f32[65]{0:T(128)S(1)}, u32[]{:S(2)}, u32[]{:S(2)}) collective-permute-start(f32[65]{0:T(128)S(1)} %maximum_maximum_fusion.1), channel_id=1, source_target_pairs={{0,16},{4,20},{8,24},{12,28},{16,32},{20,36},{24,40},{28,44},{32,4... | collective-permute-start | bytes 788 | tf_op jit(solution)/shard_map/ppermute | solution.py:84
  (71 other events, 745.0 us)

commit v7 on v2

--- a/solution.py
+++ b/solution.py
@@ -285,12 +285,12 @@
     ).astype(jnp.bfloat16)
     packed = jnp.concatenate([short_rows, hidden_long[tok_rows - 1 :]], 0)
     seq_rows = gather_fast(packed, "seq", 0)
-    full_rows = gather_fast(seq_rows, "tp", 1)
     seq_count = lax.axis_size("seq")
-    shaped = full_rows.reshape(seq_count, req_count + 1, D)
+    shaped = seq_rows.reshape(seq_count, req_count + 1, -1)
     long_row = shaped[seq_count - 1, req_count][None]
-    short_all = shaped[:, :req_count].reshape(seq_count * req_count, D)
-    row_block = jnp.concatenate([long_row, short_all], 0).astype(jnp.float32)
+    short_all = shaped[:, :req_count].reshape(seq_count * req_count, -1)
+    needed = jnp.concatenate([long_row, short_all], 0)
+    row_block = gather_fast(needed, "tp", 1).astype(jnp.float32)
     last_norm = (
         row_block
         * lax.rsqrt(jnp.mean(row_block * row_block, axis=-1, keepdims=True) + 1e-05)

time: 236 us -> 232 us (0.983)
  no operation moved by 1% of the time
where the time goes in v7:
time: 232 us; the launch traced here: 229 us
  starting transfers between devices  89.8 us (39%)
  waiting for transfers between devices  59.4 us (26%)
  matrix products  41.8 us (18%)
  other arithmetic  22.8 us (10%)
  local copies, waits for them, and re-layouts  13.8 us (6%)
    ppermute x13, starting transfers between devices, passed_along(): return lax.ppermute(block, axis, route)  49.6 us
    ppermute x3, waiting for transfers between devices, local(): lax.ppermute(term, 'tp', [(i, (i + step) % tp_count) for i in range(tp_co...  36.8 us
    ppermute x10, starting transfers between devices, gather_fast(): lax.ppermute(block, axis, digit_route(count, distance, step, radix))  18.1 us
    ppermute x10, starting transfers between devices, max_fast(): lax.ppermute(block, axis, digit_route(count, distance, step, radix))  17.7 us
    dot_general x4, matrix products, local(): jnp.dot(all_normed, piece, preferred_element_type=jnp.float32)  16.1 us
    ppermute x10, waiting for transfers between devices, gather_fast(): lax.ppermute(block, axis, digit_route(count, distance, step, radix))  9.59 us
    ppermute x13, waiting for transfers between devices, passed_along(): return lax.ppermute(block, axis, route)  8.04 us
    dot_general x3, matrix products, ssd_block(): jnp.einsum('hts,shp->thp', weights, x_block, preferred_element_type=jnp.f...  7.72 us
  transfers between devices with their start and end apart: 36, of which 18 were waited for; matrix products, arithmetic and copies ran while one was open for 20% of the time, Pallas kernels for 0%

profile of v7, /device:TPU:8, one launch (start us, length us, event | category | flops | bytes accessed | tf_op | source)
XLA Modules:
  0.0 229.4 jit_solution(10223454712931184820)
XLA Ops:
  5.6 4.0 %collective-permute-start.3 = (f32[16]{0:T(128)S(1)}, f32[16]{0:T(128)S(1)}, u32[]{:S(2)}, u32[]{:S(2)}) collective-permute-start(f32[16]{0:T(128)S(1)} %slice_reduce_fusion.5), channel_id=1, source_target_pairs={{0,8},{4,12},{8,16},{12,20},{16,24},{20,28},{24,32},{28,36},{32,40... | collective-permute-start | bytes 200 | tf_op jit(solution)/shard_map/ppermute | solution.py:19
  10.6 3.6 %collective-permute-start.1 = (bf16[3,2,128]{2,0,1:T(4,128)(2,1)S(1)}, bf16[3,2,128]{2,0,1:T(4,128)(2,1)S(1)}, u32[]{:S(2)}, u32[]{:S(2)}) collective-permute-start(bf16[3,2,128]{2,0,1:T(4,128)(2,1)S(1)} %slice.253), channel_id=1, source_target_pairs={{0,4},{4,8},{8,12},{12,16},{16,20},{20,24},{24,28},{28,32},{32,36}... | collective-permute-start | bytes 4616 | tf_op jit(solution)/shard_map/ppermute | solution.py:19
  30.2 3.5 %collective-permute-start.4 = (f32[16]{0:T(128)S(1)}, f32[16]{0:T(128)S(1)}, u32[]{:S(2)}, u32[]{:S(2)}) collective-permute-start(f32[16]{0:T(128)S(1)} %get-tuple-element.39), channel_id=1, source_target_pairs={{0,8},{4,12},{8,16},{12,20},{16,24},{20,28},{24,32},{28,36},{32,40... | collective-permute-start | bytes 200 | tf_op jit(solution)/shard_map/ppermute | solution.py:19
  44.2 5.5 %collective-permute-start.5 = (f32[16]{0:T(128)S(1)}, f32[16]{0:T(128)S(1)}, u32[]{:S(2)}, u32[]{:S(2)}) collective-permute-start(f32[16]{0:T(128)S(1)} %get-tuple-element.37), channel_id=1, source_target_pairs={{0,16},{4,20},{8,24},{12,28},{16,32},{20,36},{24,40},{28,44},{32,4... | collective-permute-start | bytes 200 | tf_op jit(solution)/shard_map/ppermute | solution.py:19
  51.4 4.5 %collective-permute-start.6 = (f32[16]{0:T(128)S(1)}, f32[16]{0:T(128)S(1)}, u32[]{:S(2)}, u32[]{:S(2)}) collective-permute-start(f32[16]{0:T(128)S(1)} %get-tuple-element.35), channel_id=1, source_target_pairs={{0,32},{4,36},{8,40},{12,44},{16,48},{20,52},{24,56},{28,60},{32,6... | collective-permute-start | bytes 200 | tf_op jit(solution)/shard_map/ppermute | solution.py:19
  56.1 3.8 %collective-permute-start.9 = (bf16[16,64,128]{2,1,0:T(8,128)(2,1)S(1)}, bf16[16,64,128]{2,1,0:T(8,128)(2,1)S(1)}, u32[]{:S(2)}, u32[]{:S(2)}) collective-permute-start(bf16[16,64,128]{2,1,0:T(8,128)(2,1)S(1)} %fusion.73), channel_id=1, source_target_pairs={{0,8},{4,12},{8,16},{12,20},{16,24},{20,28},{24,32},{28,36},{32,40... | collective-permute-start | bytes 786440 | tf_op jit(solution)/shard_map/ppermute | solution.py:19
  61.2 4.3 %collective-permute-done.9 = bf16[16,64,128]{2,1,0:T(8,128)(2,1)S(1)} collective-permute-done((bf16[16,64,128]{2,1,0:T(8,128)(2,1)S(1)}, bf16[16,64,128]{2,1,0:T(8,128)(2,1)S(1)}, u32[]{:S(2)}, u32[]{:S(2)}) %collective-permute-start.9) | collective-permute-done | bytes 262176 | tf_op jit(solution)/shard_map/ppermute | solution.py:19
  66.4 4.8 %collective-permute-start.10 = (bf16[16,64,128]{2,1,0:T(8,128)(2,1)S(1)}, bf16[16,64,128]{2,1,0:T(8,128)(2,1)S(1)}, u32[]{:S(2)}, u32[]{:S(2)}) collective-permute-start(bf16[16,64,128]{2,1,0:T(8,128)(2,1)S(1)} %fusion.144), channel_id=1, source_target_pairs={{0,16},{4,20},{8,24},{12,28},{16,32},{20,36},{24,40},{28,44},{32,4... | collective-permute-start | bytes 786440 | tf_op jit(solution)/shard_map/ppermute | solution.py:19
  71.2 3.7 %fusion.33 = f32[256,16,64]{0,2,1:T(8,128)} fusion(bf16[256,16,64]{0,2,1:T(8,128)(2,1)S(1)} %bitcast.230, f32[16,256]{1,0:T(8,128)} %get-tuple-element.95, f32[16,256]{1,0:T(8,128)} %copy-done.28, pred[256,256]{1,0:T(8,128)(4,1)} %iota_compare_fusion, bf16[256,128]{1,0:T(8,128)(2,1)} %copy-done.22, bf16[256,128]{1,0:T(8,128)(2,1)} %get-tuple-element.48), kind=kOutput, calls=%fused_computation.41 | convolution fusion | flops 408944640 | bytes 1802240 | tf_op jit(solution)/shard_map/hts,shp->thp/dot_general | solution.py:136
  77.2 8.1 %collective-permute-start.11 = (bf16[16,64,128]{2,1,0:T(8,128)(2,1)}, bf16[16,64,128]{2,1,0:T(8,128)(2,1)}, u32[]{:S(2)}, u32[]{:S(2)}) collective-permute-start(bf16[16,64,128]{2,1,0:T(8,128)(2,1)} %fusion.74), channel_id=1, source_target_pairs={{0,32},{4,36},{8,40},{12,44},{16,48},{20,52},{24,56},{28,60},{32,6... | collective-permute-start | bytes 786440 | tf_op jit(solution)/shard_map/ppermute | solution.py:19
  85.3 3.7 %fusion.34 = f32[256,16,64]{0,2,1:T(8,128)} fusion(bf16[256,16,64]{0,2,1:T(8,128)(2,1)S(1)} %bitcast.232, f32[16,256]{1,0:T(8,128)} %get-tuple-element.96, f32[16,256]{1,0:T(8,128)} %copy-done.27, pred[256,256]{1,0:T(8,128)(4,1)} %iota_compare_fusion, bf16[256,128]{1,0:T(8,128)(2,1)} %copy-done.26, bf16[256,128]{1,0:T(8,128)(2,1)S(1)} %get-tuple-element.46), kind=kOutput, calls=%fused_computation.42 | convolution fusion | flops 408944640 | bytes 1802240 | tf_op jit(solution)/shard_map/hts,shp->thp/dot_general | solution.py:136
  100.2 3.8 %fusion.10 = f32[512,16,64]{0,2,1:T(8,128)} fusion(f32[512,16,64]{0,2,1:T(8,128)S(1)} %bitcast.227, f32[512,16,64]{0,2,1:T(8,128)S(1)} %bitcast.226, f32[16]{0:T(128)S(1)} %copy-done.52, bf16[512,128]{1,0:T(8,128)(2,1)S(1)} %copy-done.17, f32[512,16]{0,1:T(8,128)S(1)} %exponential_bitcast_fusion, f32[16,64,128]{2,1,0:T(8,128)S(1)} %get-tuple-element.33, ...), kind=kOutput, calls=%fused_computation.19 | convolution fusion | flops 807796736 | bytes 7241856 | tf_op jit(solution)/shard_map/thn,hpn->thp/dot_general | solution.py:208
  107.5 4.3 %fusion.19 = bf16[544,1024]{1,0:T(8,128)(2,1)} fusion(bf16[1024,4096]{1,0:T(8,128)(2,1)} %param.37, s32[]{:T(128)S(6)} %select_n.193, bf16[32,1024]{1,0:T(8,128)(2,1)S(1)} %copy-done.25, bf16[512,1024]{1,0:T(8,128)(2,1)S(1)} %multiply_convert_fusion.2), kind=kOutput, calls=%fused_computation.31 | convolution fusion | flops 1143635968 | bytes 4325380 | tf_op jit(solution)/shard_map/dot_general | solution.py:271
  114.1 3.9 %fusion.22 = bf16[544,1024]{1,0:T(8,128)(2,1)} fusion(bf16[1024,4096]{1,0:T(8,128)(2,1)} %param.37, s32[]{:T(128)S(6)} %select_n.195, bf16[32,1024]{1,0:T(8,128)(2,1)S(1)} %copy-done.25, bf16[512,1024]{1,0:T(8,128)(2,1)S(1)} %multiply_convert_fusion.2), kind=kOutput, calls=%fused_computation.32 | convolution fusion | flops 1143635968 | bytes 4325380 | tf_op jit(solution)/shard_map/dot_general | solution.py:271
  118.1 4.0 %fusion.25 = bf16[544,1024]{1,0:T(8,128)(2,1)} fusion(bf16[1024,4096]{1,0:T(8,128)(2,1)} %param.37, s32[]{:T(128)S(6)} %select_n.197, bf16[32,1024]{1,0:T(8,128)(2,1)S(1)} %copy-done.25, bf16[512,1024]{1,0:T(8,128)(2,1)S(1)} %multiply_convert_fusion.2), kind=kOutput, calls=%fused_computation.33 | convolution fusion | flops 1143635968 | bytes 4325380 | tf_op jit(solution)/shard_map/dot_general | solution.py:271
  124.5 16.5 %collective-permute-done.13 = bf16[544,1024]{1,0:T(8,128)(2,1)S(1)} collective-permute-done((bf16[544,1024]{1,0:T(8,128)(2,1)}, bf16[544,1024]{1,0:T(8,128)(2,1)S(1)}, u32[]{:S(2)}, u32[]{:S(2)}) %collective-permute-start.13) | collective-permute-done | bytes 1114144 | tf_op jit(solution)/shard_map/ppermute | solution.py:273
  141.0 20.2 %collective-permute-done.14 = bf16[544,1024]{1,0:T(8,128)(2,1)} collective-permute-done((bf16[544,1024]{1,0:T(8,128)(2,1)}, bf16[544,1024]{1,0:T(8,128)(2,1)}, u32[]{:S(2)}, u32[]{:S(2)}) %collective-permute-start.14) | collective-permute-done | bytes 1114144 | tf_op jit(solution)/shard_map/ppermute | solution.py:273
  161.3 3.9 %add_convert_fusion = bf16[544,1024]{1,0:T(8,128)(2,1)S(1)} fusion(bf16[544,1024]{1,0:T(8,128)(2,1)} %collective-permute-done.15, bf16[544,1024]{1,0:T(8,128)(2,1)} %collective-permute-done.14, bf16[544,1024]{1,0:T(8,128)(2,1)S(1)} %collective-permute-done.13, bf16[1024,4096]{1,0:T(8,128)(2,1)} %param.37, s32[]{:T(128)S(6)} %select_n.199, ...), kind=kOutput, calls=%fused_computation.6 | convolution fusion | flops 1148092416 | bytes 7667716 | tf_op jit(solution)/shard_map/dot_general | solution.py:271
  165.5 3.3 %collective-permute-start.17 = (bf16[3,1024]{1,0:T(4,128)(2,1)S(1)}, bf16[3,1024]{1,0:T(4,128)(2,1)S(1)}, u32[]{:S(2)}, u32[]{:S(2)}) collective-permute-start(bf16[3,1024]{1,0:T(4,128)(2,1)S(1)} %get-tuple-element.79), channel_id=1, source_target_pairs={{0,8},{4,12},{8,0},{12,4},{16,24},{20,28},{24,16},{28,20},{32,40},... | collective-permute-start | bytes 18440 | tf_op jit(solution)/shard_map/ppermute | solution.py:65
  172.4 3.8 %collective-permute-start.21 = (bf16[12,1024]{1,0:T(8,128)(2,1)S(1)}, bf16[12,1024]{1,0:T(8,128)(2,1)S(1)}, u32[]{:S(2)}, u32[]{:S(2)}) collective-permute-start(bf16[12,1024]{1,0:T(8,128)(2,1)S(1)} %get-tuple-element.59), channel_id=1, source_target_pairs={{0,48},{4,52},{8,56},{12,60},{16,0},{20,4},{24,8},{28,12},{32,16},... | collective-permute-start | bytes 73736 | tf_op jit(solution)/shard_map/ppermute | solution.py:65
  178.7 4.1 %collective-permute-start.22 = (bf16[48,1024]{1,0:T(8,128)(2,1)S(1)}, bf16[48,1024]{1,0:T(8,128)(2,1)S(1)}, u32[]{:S(2)}, u32[]{:S(2)}) collective-permute-start(bf16[48,1024]{1,0:T(8,128)(2,1)S(1)} %pad_maximum_fusion.8), channel_id=1, source_target_pairs={{0,64},{4,68},{8,72},{12,76},{16,80},{20,84},{24,88},{28,92},{32,9... | collective-permute-start | bytes 294920 | tf_op jit(solution)/shard_map/ppermute | solution.py:65
  196.2 6.4 %convolution_reduce_fusion = f32[65]{0:T(128)S(1)} fusion(bf16[65,4096]{1,0:T(8,128)(2,1)S(1)} %fusion.43, bf16[1024,4096]{1,0:T(8,128)(2,1)} %param.39), kind=kOutput, calls=%fused_computation.65 | convolution fusion | flops 545326016 | bytes 8921348 | tf_op jit(solution)/shard_map/dot_general | solution.py:299
  214.6 3.9 %collective-permute-start.32 = (f32[65]{0:T(128)S(1)}, f32[65]{0:T(128)S(1)}, u32[]{:S(2)}, u32[]{:S(2)}) collective-permute-start(f32[65]{0:T(128)S(1)} %maximum_maximum_fusion.1), channel_id=1, source_target_pairs={{0,16},{4,20},{8,24},{12,28},{16,32},{20,36},{24,40},{28,44},{32,4... | collective-permute-start | bytes 788 | tf_op jit(solution)/shard_map/ppermute | solution.py:84
  223.6 3.3 %collective-permute-start.35 = (f32[65]{0:T(128)S(1)}, f32[65]{0:T(128)S(1)}, u32[]{:S(2)}, u32[]{:S(2)}) collective-permute-start(f32[65]{0:T(128)S(1)} %maximum_maximum_fusion), channel_id=1, source_target_pairs={{0,64},{4,68},{8,72},{12,76},{16,80},{20,84},{24,88},{28,92},{32,9... | collective-permute-start | bytes 788 | tf_op jit(solution)/shard_map/ppermute | solution.py:84
  (285 shorter events, 96.7 us)
Async XLA Ops:
  3.9 25.8 %collective-permute-start.2 = (f32[16]{0:T(128)S(1)}, f32[16]{0:T(128)S(1)}, u32[]{:S(2)}, u32[]{:S(2)}) collective-permute-start(f32[16]{0:T(128)S(1)} %slice_reduce_fusion.5), channel_id=1, source_target_pairs={{0,4},{4,8},{8,12},{12,16},{16,20},{20,24},{24,28},{28,32},{32,36}... | collective-permute-start | bytes 200 | tf_op jit(solution)/shard_map/ppermute | solution.py:19
  5.6 24.0 %collective-permute-start.3 = (f32[16]{0:T(128)S(1)}, f32[16]{0:T(128)S(1)}, u32[]{:S(2)}, u32[]{:S(2)}) collective-permute-start(f32[16]{0:T(128)S(1)} %slice_reduce_fusion.5), channel_id=1, source_target_pairs={{0,8},{4,12},{8,16},{12,20},{16,24},{20,28},{24,32},{28,36},{32,40... | collective-permute-start | bytes 200 | tf_op jit(solution)/shard_map/ppermute | solution.py:19
  10.6 23.1 %collective-permute-start.1 = (bf16[3,2,128]{2,0,1:T(4,128)(2,1)S(1)}, bf16[3,2,128]{2,0,1:T(4,128)(2,1)S(1)}, u32[]{:S(2)}, u32[]{:S(2)}) collective-permute-start(bf16[3,2,128]{2,0,1:T(4,128)(2,1)S(1)} %slice.253), channel_id=1, source_target_pairs={{0,4},{4,8},{8,12},{12,16},{16,20},{20,24},{24,28},{28,32},{32,36}... | collective-permute-start | bytes 4616 | tf_op jit(solution)/shard_map/ppermute | solution.py:19
  15.0 19.8 %collective-permute-start = (bf16[3,1024]{1,0:T(4,128)(2,1)S(1)}, bf16[3,1024]{1,0:T(4,128)(2,1)S(1)}, u32[]{:S(2)}, u32[]{:S(2)}) collective-permute-start(bf16[3,1024]{1,0:T(4,128)(2,1)S(1)} %slice.193), channel_id=1, source_target_pairs={{0,4},{4,8},{8,12},{12,16},{16,20},{20,24},{24,28},{28,32},{32,36}... | collective-permute-start | bytes 18440 | tf_op jit(solution)/shard_map/ppermute | solution.py:19
  30.2 13.4 %collective-permute-start.4 = (f32[16]{0:T(128)S(1)}, f32[16]{0:T(128)S(1)}, u32[]{:S(2)}, u32[]{:S(2)}) collective-permute-start(f32[16]{0:T(128)S(1)} %get-tuple-element.39), channel_id=1, source_target_pairs={{0,8},{4,12},{8,16},{12,20},{16,24},{20,28},{24,32},{28,36},{32,40... | collective-permute-start | bytes 200 | tf_op jit(solution)/shard_map/ppermute | solution.py:19
  38.4 17.5 %collective-permute-start.7 = (bf16[16,64,128]{2,1,0:T(8,128)(2,1)S(1)}, bf16[16,64,128]{2,1,0:T(8,128)(2,1)S(1)}, u32[]{:S(2)}, u32[]{:S(2)}) collective-permute-start(bf16[16,64,128]{2,1,0:T(8,128)(2,1)S(1)} %get-tuple-element.93), channel_id=1, source_target_pairs={{0,8},{4,12},{8,16},{12,20},{16,24},{20,28},{24,32},{28,36},{32,40... | collective-permute-start | bytes 786440 | tf_op jit(solution)/shard_map/ppermute | solution.py:19
  40.5 15.5 %collective-permute-start.8 = (bf16[16,64,128]{2,1,0:T(8,128)(2,1)S(1)}, bf16[16,64,128]{2,1,0:T(8,128)(2,1)S(1)}, u32[]{:S(2)}, u32[]{:S(2)}) collective-permute-start(bf16[16,64,128]{2,1,0:T(8,128)(2,1)S(1)} %get-tuple-element.93), channel_id=1, source_target_pairs={{0,4},{4,8},{8,12},{12,16},{16,20},{20,24},{24,28},{28,32},{32,36}... | collective-permute-start | bytes 786440 | tf_op jit(solution)/shard_map/ppermute | solution.py:19
  44.2 6.7 %collective-permute-start.5 = (f32[16]{0:T(128)S(1)}, f32[16]{0:T(128)S(1)}, u32[]{:S(2)}, u32[]{:S(2)}) collective-permute-start(f32[16]{0:T(128)S(1)} %get-tuple-element.37), channel_id=1, source_target_pairs={{0,16},{4,20},{8,24},{12,28},{16,32},{20,36},{24,40},{28,44},{32,4... | collective-permute-start | bytes 200 | tf_op jit(solution)/shard_map/ppermute | solution.py:19
  51.4 8.5 %collective-permute-start.6 = (f32[16]{0:T(128)S(1)}, f32[16]{0:T(128)S(1)}, u32[]{:S(2)}, u32[]{:S(2)}) collective-permute-start(f32[16]{0:T(128)S(1)} %get-tuple-element.35), channel_id=1, source_target_pairs={{0,32},{4,36},{8,40},{12,44},{16,48},{20,52},{24,56},{28,60},{32,6... | collective-permute-start | bytes 200 | tf_op jit(solution)/shard_map/ppermute | solution.py:19
  56.1 9.3 %collective-permute-start.9 = (bf16[16,64,128]{2,1,0:T(8,128)(2,1)S(1)}, bf16[16,64,128]{2,1,0:T(8,128)(2,1)S(1)}, u32[]{:S(2)}, u32[]{:S(2)}) collective-permute-start(bf16[16,64,128]{2,1,0:T(8,128)(2,1)S(1)} %fusion.73), channel_id=1, source_target_pairs={{0,8},{4,12},{8,16},{12,20},{16,24},{20,28},{24,32},{28,36},{32,40... | collective-permute-start | bytes 786440 | tf_op jit(solution)/shard_map/ppermute | solution.py:19
  66.4 9.1 %collective-permute-start.10 = (bf16[16,64,128]{2,1,0:T(8,128)(2,1)S(1)}, bf16[16,64,128]{2,1,0:T(8,128)(2,1)S(1)}, u32[]{:S(2)}, u32[]{:S(2)}) collective-permute-start(bf16[16,64,128]{2,1,0:T(8,128)(2,1)S(1)} %fusion.144), channel_id=1, source_target_pairs={{0,16},{4,20},{8,24},{12,28},{16,32},{20,36},{24,40},{28,44},{32,4... | collective-permute-start | bytes 786440 | tf_op jit(solution)/shard_map/ppermute | solution.py:19
  77.2 15.2 %collective-permute-start.11 = (bf16[16,64,128]{2,1,0:T(8,128)(2,1)}, bf16[16,64,128]{2,1,0:T(8,128)(2,1)}, u32[]{:S(2)}, u32[]{:S(2)}) collective-permute-start(bf16[16,64,128]{2,1,0:T(8,128)(2,1)} %fusion.74), channel_id=1, source_target_pairs={{0,32},{4,36},{8,40},{12,44},{16,48},{20,52},{24,56},{28,60},{32,6... | collective-permute-start | bytes 786440 | tf_op jit(solution)/shard_map/ppermute | solution.py:19
  93.8 6.4 %collective-permute-start.12 = (bf16[16,64,128]{2,1,0:T(8,128)(2,1)S(1)}, bf16[16,64,128]{2,1,0:T(8,128)(2,1)S(1)}, u32[]{:S(2)}, u32[]{:S(2)}) collective-permute-start(bf16[16,64,128]{2,1,0:T(8,128)(2,1)S(1)} %get-tuple-element.32), channel_id=1, source_target_pairs={{0,64},{4,68},{8,72},{12,76},{16,80},{20,84},{24,88},{28,92},{32,9... | collective-permute-start | bytes 786440 | tf_op jit(solution)/shard_map/ppermute | solution.py:19
  111.8 29.2 %collective-permute-start.13 = (bf16[544,1024]{1,0:T(8,128)(2,1)}, bf16[544,1024]{1,0:T(8,128)(2,1)S(1)}, u32[]{:S(2)}, u32[]{:S(2)}) collective-permute-start(bf16[544,1024]{1,0:T(8,128)(2,1)} %fusion.19), channel_id=1, source_target_pairs={{0,2},{1,3},{2,0},{3,1},{4,6},{5,7},{6,4},{7,5},{8,10},{9,11},{10,... | collective-permute-start | bytes 3342344 | tf_op jit(solution)/shard_map/ppermute | solution.py:273
  118.0 43.2 %collective-permute-start.14 = (bf16[544,1024]{1,0:T(8,128)(2,1)}, bf16[544,1024]{1,0:T(8,128)(2,1)}, u32[]{:S(2)}, u32[]{:S(2)}) collective-permute-start(bf16[544,1024]{1,0:T(8,128)(2,1)} %fusion.22), channel_id=1, source_target_pairs={{0,1},{1,2},{2,3},{3,0},{4,5},{5,6},{6,7},{7,4},{8,9},{9,10},{10,1... | collective-permute-start | bytes 3342344 | tf_op jit(solution)/shard_map/ppermute | solution.py:273
  122.1 39.2 %collective-permute-start.15 = (bf16[544,1024]{1,0:T(8,128)(2,1)}, bf16[544,1024]{1,0:T(8,128)(2,1)}, u32[]{:S(2)}, u32[]{:S(2)}) collective-permute-start(bf16[544,1024]{1,0:T(8,128)(2,1)} %fusion.25), channel_id=1, source_target_pairs={{0,3},{1,0},{2,1},{3,2},{4,7},{5,4},{6,5},{7,6},{8,11},{9,8},{10,9... | collective-permute-start | bytes 3342344 | tf_op jit(solution)/shard_map/ppermute | solution.py:273
  171.7 6.5 %collective-permute-start.19 = (bf16[12,1024]{1,0:T(8,128)(2,1)S(1)}, bf16[12,1024]{1,0:T(8,128)(2,1)S(1)}, u32[]{:S(2)}, u32[]{:S(2)}) collective-permute-start(bf16[12,1024]{1,0:T(8,128)(2,1)S(1)} %get-tuple-element.59), channel_id=1, source_target_pairs={{0,16},{4,20},{8,24},{12,28},{16,32},{20,36},{24,40},{28,44},{32,4... | collective-permute-start | bytes 73736 | tf_op jit(solution)/shard_map/ppermute | solution.py:65
  172.2 5.9 %collective-permute-start.20 = (bf16[12,1024]{1,0:T(8,128)(2,1)S(1)}, bf16[12,1024]{1,0:T(8,128)(2,1)S(1)}, u32[]{:S(2)}, u32[]{:S(2)}) collective-permute-start(bf16[12,1024]{1,0:T(8,128)(2,1)S(1)} %get-tuple-element.59), channel_id=1, source_target_pairs={{0,32},{4,36},{8,40},{12,44},{16,48},{20,52},{24,56},{28,60},{32,0... | collective-permute-start | bytes 73736 | tf_op jit(solution)/shard_map/ppermute | solution.py:65
  172.4 6.2 %collective-permute-start.21 = (bf16[12,1024]{1,0:T(8,128)(2,1)S(1)}, bf16[12,1024]{1,0:T(8,128)(2,1)S(1)}, u32[]{:S(2)}, u32[]{:S(2)}) collective-permute-start(bf16[12,1024]{1,0:T(8,128)(2,1)S(1)} %get-tuple-element.59), channel_id=1, source_target_pairs={{0,48},{4,52},{8,56},{12,60},{16,0},{20,4},{24,8},{28,12},{32,16},... | collective-permute-start | bytes 73736 | tf_op jit(solution)/shard_map/ppermute | solution.py:65
  178.7 6.7 %collective-permute-start.22 = (bf16[48,1024]{1,0:T(8,128)(2,1)S(1)}, bf16[48,1024]{1,0:T(8,128)(2,1)S(1)}, u32[]{:S(2)}, u32[]{:S(2)}) collective-permute-start(bf16[48,1024]{1,0:T(8,128)(2,1)S(1)} %pad_maximum_fusion.8), channel_id=1, source_target_pairs={{0,64},{4,68},{8,72},{12,76},{16,80},{20,84},{24,88},{28,92},{32,9... | collective-permute-start | bytes 294920 | tf_op jit(solution)/shard_map/ppermute | solution.py:65
  185.9 6.8 %collective-permute-start.23 = (bf16[65,1024]{1,0:T(8,128)(2,1)S(1)}, bf16[65,1024]{1,0:T(8,128)(2,1)S(1)}, u32[]{:S(2)}, u32[]{:S(2)}) collective-permute-start(bf16[65,1024]{1,0:T(8,128)(2,1)S(1)} %get-tuple-element.53), channel_id=1, source_target_pairs={{0,1},{1,2},{2,3},{3,0},{4,5},{5,6},{6,7},{7,4},{8,9},{9,10},{10,1... | collective-permute-start | bytes 399368 | tf_op jit(solution)/shard_map/ppermute | solution.py:65
  187.4 7.2 %collective-permute-start.24 = (bf16[65,1024]{1,0:T(8,128)(2,1)S(1)}, bf16[65,1024]{1,0:T(8,128)(2,1)S(1)}, u32[]{:S(2)}, u32[]{:S(2)}) collective-permute-start(bf16[65,1024]{1,0:T(8,128)(2,1)S(1)} %get-tuple-element.53), channel_id=1, source_target_pairs={{0,2},{1,3},{2,0},{3,1},{4,6},{5,7},{6,4},{7,5},{8,10},{9,11},{10,... | collective-permute-start | bytes 399368 | tf_op jit(solution)/shard_map/ppermute | solution.py:65
  188.7 6.9 %collective-permute-start.25 = (bf16[65,1024]{1,0:T(8,128)(2,1)S(1)}, bf16[65,1024]{1,0:T(8,128)(2,1)S(1)}, u32[]{:S(2)}, u32[]{:S(2)}) collective-permute-start(bf16[65,1024]{1,0:T(8,128)(2,1)S(1)} %get-tuple-element.53), channel_id=1, source_target_pairs={{0,3},{1,0},{2,1},{3,2},{4,7},{5,4},{6,5},{7,6},{8,11},{9,8},{10,9... | collective-permute-start | bytes 399368 | tf_op jit(solution)/shard_map/ppermute | solution.py:65
  214.6 6.6 %collective-permute-start.32 = (f32[65]{0:T(128)S(1)}, f32[65]{0:T(128)S(1)}, u32[]{:S(2)}, u32[]{:S(2)}) collective-permute-start(f32[65]{0:T(128)S(1)} %maximum_maximum_fusion.1), channel_id=1, source_target_pairs={{0,16},{4,20},{8,24},{12,28},{16,32},{20,36},{24,40},{28,44},{32,4... | collective-permute-start | bytes 788 | tf_op jit(solution)/shard_map/ppermute | solution.py:84
  (65 other events, 693.5 us)

commit v8 on v7

--- a/solution.py
+++ b/solution.py
@@ -262,7 +262,9 @@
     tp_count = lax.axis_size("tp")
     tp_index = lax.axis_index("tp")
     width = out_weight.shape[1] // tp_count
+    last_pick = (jnp.arange(SLEN)[None, :] == lengths[:, None] - 1).astype(jnp.float32)
     total = None
+    row_total = None
     for step in (2, 1, 3, 0):
         if step >= tp_count:
             continue
@@ -273,17 +275,26 @@
             term = lax.ppermute(
                 term, "tp", [(i, (i + step) % tp_count) for i in range(tp_count)]
             )
+        picked = jnp.concatenate(
+            [
+                jnp.einsum(
+                    "rs,rsd->rd",
+                    last_pick,
+                    term[tok_rows:].reshape(req_count, SLEN, -1).astype(jnp.float32),
+                    precision=lax.Precision.HIGHEST,
+                ),
+                term[tok_rows - 1 : tok_rows].astype(jnp.float32),
+            ],
+            0,
+        )
+        row_total = picked if total is None else row_total + picked
         total = term.astype(jnp.float32) if total is None else total + term.astype(jnp.float32)
     hidden = total.astype(jnp.bfloat16)
+    packed = row_total.astype(jnp.bfloat16)
     hidden_long = hidden[:tok_rows]
     hidden_short = hidden[tok_rows:].reshape(req_count, SLEN, -1) * is_valid[:, :, None].astype(
         jnp.bfloat16
     )
-    last_pick = (jnp.arange(SLEN)[None, :] == lengths[:, None] - 1).astype(jnp.float32)
-    short_rows = jnp.einsum(
-        "rs,rsd->rd", last_pick, hidden_short.astype(jnp.float32), precision=lax.Precision.HIGHEST
-    ).astype(jnp.bfloat16)
-    packed = jnp.concatenate([short_rows, hidden_long[tok_rows - 1 :]], 0)
     seq_rows = gather_fast(packed, "seq", 0)
     seq_count = lax.axis_size("seq")
     shaped = seq_rows.reshape(seq_count, req_count + 1, -1)

time: 232 us -> 232 us (level)
  waiting for transfers between devices: 59.4 us -> 68.7 us
  matrix products: 41.8 us -> 35.2 us
  starting transfers between devices: 89.8 us -> 85.2 us
    dot_general x4, matrix products: 16.1 us -> 9.04 us  [local(): jnp.dot(all_normed, piece, preferred_element_type=jnp.float32)]
    ppermute x10, waiting for transfers between devices: 9.59 us -> 15.4 us  [gather_fast(): lax.ppermute(block, axis, digit_route(count, distance, step, radix))]
    ppermute x10, starting transfers between devices: 17.7 us -> 13 us  [max_fast(): lax.ppermute(block, axis, digit_route(count, distance, step, radix))]
    ppermute x10, waiting for transfers between devices: 4.93 us -> 7.52 us  [max_fast(): lax.ppermute(block, axis, digit_route(count, distance, step, radix))]
  transfers between devices with their start and end apart: 36 -> 36, of which waited for: 18 -> 21; matrix products, arithmetic and copies ran while one was open for 20% -> 19% of each run, Pallas kernels for 0% -> 0%
where the time goes in v8:
time: 232 us; the launch traced here: 228 us
  starting transfers between devices  85.2 us (37%)
  waiting for transfers between devices  68.7 us (30%)
  matrix products  35.2 us (15%)
  other arithmetic  23.8 us (10%)
  local copies, waits for them, and re-layouts  13.1 us (6%)
    ppermute x13, starting transfers between devices, passed_along(): return lax.ppermute(block, axis, route)  50 us
    ppermute x3, waiting for transfers between devices, local(): lax.ppermute(term, 'tp', [(i, (i + step) % tp_count) for i in range(tp_co...  36.8 us
    ppermute x10, starting transfers between devices, gather_fast(): lax.ppermute(block, axis, digit_route(count, distance, step, radix))  16.8 us
    ppermute x10, waiting for transfers between devices, gather_fast(): lax.ppermute(block, axis, digit_route(count, distance, step, radix))  15.4 us
    ppermute x10, starting transfers between devices, max_fast(): lax.ppermute(block, axis, digit_route(count, distance, step, radix))  13 us
    ppermute x13, waiting for transfers between devices, passed_along(): return lax.ppermute(block, axis, route)  9.04 us
    dot_general x4, matrix products, local(): jnp.dot(all_normed, piece, preferred_element_type=jnp.float32)  9.04 us
    dot_general x3, matrix products, ssd_block(): jnp.einsum('hts,shp->thp', weights, x_block, preferred_element_type=jnp.f...  7.76 us
  transfers between devices with their start and end apart: 36, of which 21 were waited for; matrix products, arithmetic and copies ran while one was open for 19% of the time, Pallas kernels for 0%

profile of v8, /device:TPU:8, one launch (start us, length us, event | category | flops | bytes accessed | tf_op | source)
XLA Modules:
  0.0 228.0 jit_solution(3704871866678975937)
XLA Ops:
  5.6 4.0 %collective-permute-start.3 = (f32[16]{0:T(128)S(1)}, f32[16]{0:T(128)S(1)}, u32[]{:S(2)}, u32[]{:S(2)}) collective-permute-start(f32[16]{0:T(128)S(1)} %slice_reduce_fusion.5), channel_id=1, source_target_pairs={{0,8},{4,12},{8,16},{12,20},{16,24},{20,28},{24,32},{28,36},{32,40... | collective-permute-start | bytes 200 | tf_op jit(solution)/shard_map/ppermute | solution.py:19
  10.4 3.6 %collective-permute-start = (bf16[3,1024]{1,0:T(4,128)(2,1)S(1)}, bf16[3,1024]{1,0:T(4,128)(2,1)S(1)}, u32[]{:S(2)}, u32[]{:S(2)}) collective-permute-start(bf16[3,1024]{1,0:T(4,128)(2,1)S(1)} %slice.213), channel_id=1, source_target_pairs={{0,4},{4,8},{8,12},{12,16},{16,20},{20,24},{24,28},{28,32},{32,36}... | collective-permute-start | bytes 18440 | tf_op jit(solution)/shard_map/ppermute | solution.py:19
  30.4 3.5 %collective-permute-start.4 = (f32[16]{0:T(128)S(1)}, f32[16]{0:T(128)S(1)}, u32[]{:S(2)}, u32[]{:S(2)}) collective-permute-start(f32[16]{0:T(128)S(1)} %get-tuple-element.39), channel_id=1, source_target_pairs={{0,8},{4,12},{8,16},{12,20},{16,24},{20,28},{24,32},{28,36},{32,40... | collective-permute-start | bytes 200 | tf_op jit(solution)/shard_map/ppermute | solution.py:19
  40.4 3.7 %collective-permute-start.7 = (bf16[16,64,128]{2,1,0:T(8,128)(2,1)S(1)}, bf16[16,64,128]{2,1,0:T(8,128)(2,1)S(1)}, u32[]{:S(2)}, u32[]{:S(2)}) collective-permute-start(bf16[16,64,128]{2,1,0:T(8,128)(2,1)S(1)} %get-tuple-element.107), channel_id=1, source_target_pairs={{0,8},{4,12},{8,16},{12,20},{16,24},{20,28},{24,32},{28,36},{32,40... | collective-permute-start | bytes 786440 | tf_op jit(solution)/shard_map/ppermute | solution.py:19
  44.6 5.5 %collective-permute-start.5 = (f32[16]{0:T(128)S(1)}, f32[16]{0:T(128)S(1)}, u32[]{:S(2)}, u32[]{:S(2)}) collective-permute-start(f32[16]{0:T(128)S(1)} %get-tuple-element.37), channel_id=1, source_target_pairs={{0,16},{4,20},{8,24},{12,28},{16,32},{20,36},{24,40},{28,44},{32,4... | collective-permute-start | bytes 200 | tf_op jit(solution)/shard_map/ppermute | solution.py:19
  51.9 4.5 %collective-permute-start.6 = (f32[16]{0:T(128)S(1)}, f32[16]{0:T(128)S(1)}, u32[]{:S(2)}, u32[]{:S(2)}) collective-permute-start(f32[16]{0:T(128)S(1)} %get-tuple-element.35), channel_id=1, source_target_pairs={{0,32},{4,36},{8,40},{12,44},{16,48},{20,52},{24,56},{28,60},{32,6... | collective-permute-start | bytes 200 | tf_op jit(solution)/shard_map/ppermute | solution.py:19
  56.6 4.1 %collective-permute-start.9 = (bf16[16,64,128]{2,1,0:T(8,128)(2,1)S(1)}, bf16[16,64,128]{2,1,0:T(8,128)(2,1)S(1)}, u32[]{:S(2)}, u32[]{:S(2)}) collective-permute-start(bf16[16,64,128]{2,1,0:T(8,128)(2,1)S(1)} %fusion.71), channel_id=1, source_target_pairs={{0,8},{4,12},{8,16},{12,20},{16,24},{20,28},{24,32},{28,36},{32,40... | collective-permute-start | bytes 786440 | tf_op jit(solution)/shard_map/ppermute | solution.py:19
  61.3 5.0 %collective-permute-done.9 = bf16[16,64,128]{2,1,0:T(8,128)(2,1)S(1)} collective-permute-done((bf16[16,64,128]{2,1,0:T(8,128)(2,1)S(1)}, bf16[16,64,128]{2,1,0:T(8,128)(2,1)S(1)}, u32[]{:S(2)}, u32[]{:S(2)}) %collective-permute-start.9) | collective-permute-done | bytes 262176 | tf_op jit(solution)/shard_map/ppermute | solution.py:19
  67.2 4.7 %collective-permute-start.10 = (bf16[16,64,128]{2,1,0:T(8,128)(2,1)S(1)}, bf16[16,64,128]{2,1,0:T(8,128)(2,1)S(1)}, u32[]{:S(2)}, u32[]{:S(2)}) collective-permute-start(bf16[16,64,128]{2,1,0:T(8,128)(2,1)S(1)} %fusion.157), channel_id=1, source_target_pairs={{0,16},{4,20},{8,24},{12,28},{16,32},{20,36},{24,40},{28,44},{32,4... | collective-permute-start | bytes 786440 | tf_op jit(solution)/shard_map/ppermute | solution.py:19
  72.0 3.7 %fusion.33 = f32[256,16,64]{0,2,1:T(8,128)} fusion(bf16[256,16,64]{0,2,1:T(8,128)(2,1)S(1)} %bitcast.260, f32[16,256]{1,0:T(8,128)} %get-tuple-element.111, f32[16,256]{1,0:T(8,128)} %copy-done.29, pred[256,256]{1,0:T(8,128)(4,1)} %iota_compare_fusion, bf16[256,128]{1,0:T(8,128)(2,1)} %copy-done.20, bf16[256,128]{1,0:T(8,128)(2,1)} %get-tuple-element.56), kind=kOutput, calls=%fused_computation.41 | convolution fusion | flops 408944640 | bytes 1802240 | tf_op jit(solution)/shard_map/hts,shp->thp/dot_general | solution.py:136
  78.2 6.7 %collective-permute-start.11 = (bf16[16,64,128]{2,1,0:T(8,128)(2,1)}, bf16[16,64,128]{2,1,0:T(8,128)(2,1)}, u32[]{:S(2)}, u32[]{:S(2)}) collective-permute-start(bf16[16,64,128]{2,1,0:T(8,128)(2,1)} %fusion.72), channel_id=1, source_target_pairs={{0,32},{4,36},{8,40},{12,44},{16,48},{20,52},{24,56},{28,60},{32,6... | collective-permute-start | bytes 786440 | tf_op jit(solution)/shard_map/ppermute | solution.py:19
  84.9 3.7 %fusion.34 = f32[256,16,64]{0,2,1:T(8,128)} fusion(bf16[256,16,64]{0,2,1:T(8,128)(2,1)S(1)} %bitcast.262, f32[16,256]{1,0:T(8,128)} %get-tuple-element.112, f32[16,256]{1,0:T(8,128)} %copy-done.28, pred[256,256]{1,0:T(8,128)(4,1)} %iota_compare_fusion, bf16[256,128]{1,0:T(8,128)(2,1)} %copy-done.27, bf16[256,128]{1,0:T(8,128)(2,1)} %get-tuple-element.54), kind=kOutput, calls=%fused_computation.42 | convolution fusion | flops 408944640 | bytes 1802240 | tf_op jit(solution)/shard_map/hts,shp->thp/dot_general | solution.py:136
  93.4 4.1 %collective-permute-start.12 = (bf16[16,64,128]{2,1,0:T(8,128)(2,1)S(1)}, bf16[16,64,128]{2,1,0:T(8,128)(2,1)S(1)}, u32[]{:S(2)}, u32[]{:S(2)}) collective-permute-start(bf16[16,64,128]{2,1,0:T(8,128)(2,1)S(1)} %get-tuple-element.32), channel_id=1, source_target_pairs={{0,64},{4,68},{8,72},{12,76},{16,80},{20,84},{24,88},{28,92},{32,9... | collective-permute-start | bytes 786440 | tf_op jit(solution)/shard_map/ppermute | solution.py:19
  101.2 3.8 %fusion.10 = f32[512,16,64]{0,2,1:T(8,128)} fusion(f32[512,16,64]{0,2,1:T(8,128)S(1)} %bitcast.257, f32[512,16,64]{0,2,1:T(8,128)S(1)} %bitcast.256, f32[16]{0:T(128)S(1)} %copy-done.57, bf16[512,128]{1,0:T(8,128)(2,1)S(1)} %slice_bitcast_fusion, f32[512,16]{0,1:T(8,128)S(1)} %copy-done.21, f32[16,64,128]{2,1,0:T(8,128)S(1)} %get-tuple-element.33, ...), kind=kOutput, calls=%fused_computation.19 | convolution fusion | flops 807796736 | bytes 7241856 | tf_op jit(solution)/shard_map/thn,hpn->thp/dot_general | solution.py:208
  118.4 3.3 %collective-permute-start.13 = (bf16[544,1024]{1,0:T(8,128)(2,1)S(1)}, bf16[544,1024]{1,0:T(8,128)(2,1)S(1)}, u32[]{:S(2)}, u32[]{:S(2)}) collective-permute-start(bf16[544,1024]{1,0:T(8,128)(2,1)S(1)} %fusion.19), channel_id=1, source_target_pairs={{0,2},{1,3},{2,0},{3,1},{4,6},{5,7},{6,4},{7,5},{8,10},{9,11},{10,... | collective-permute-start | bytes 3342344 | tf_op jit(solution)/shard_map/ppermute | solution.py:275
  123.5 14.6 %collective-permute-done.15 = bf16[544,1024]{1,0:T(8,128)(2,1)S(1)} collective-permute-done((bf16[544,1024]{1,0:T(8,128)(2,1)S(1)}, bf16[544,1024]{1,0:T(8,128)(2,1)S(1)}, u32[]{:S(2)}, u32[]{:S(2)}) %collective-permute-start.15) | collective-permute-done | bytes 1114144 | tf_op jit(solution)/shard_map/ppermute | solution.py:275
  138.1 5.5 %collective-permute-done.14 = bf16[544,1024]{1,0:T(8,128)(2,1)S(1)} collective-permute-done((bf16[544,1024]{1,0:T(8,128)(2,1)S(1)}, bf16[544,1024]{1,0:T(8,128)(2,1)S(1)}, u32[]{:S(2)}, u32[]{:S(2)}) %collective-permute-start.14) | collective-permute-done | bytes 1114144 | tf_op jit(solution)/shard_map/ppermute | solution.py:275
  143.7 16.7 %collective-permute-done.13 = bf16[544,1024]{1,0:T(8,128)(2,1)S(1)} collective-permute-done((bf16[544,1024]{1,0:T(8,128)(2,1)S(1)}, bf16[544,1024]{1,0:T(8,128)(2,1)S(1)}, u32[]{:S(2)}, u32[]{:S(2)}) %collective-permute-start.13) | collective-permute-done | bytes 1114144 | tf_op jit(solution)/shard_map/ppermute | solution.py:275
  172.1 3.2 %collective-permute-done.19 = bf16[12,1024]{1,0:T(8,128)(2,1)S(1)} collective-permute-done((bf16[12,1024]{1,0:T(8,128)(2,1)S(1)}, bf16[12,1024]{1,0:T(8,128)(2,1)S(1)}, u32[]{:S(2)}, u32[]{:S(2)}) %collective-permute-start.19) | collective-permute-done | bytes 24608 | tf_op jit(solution)/shard_map/ppermute | solution.py:65
  175.4 4.1 %collective-permute-start.22 = (bf16[48,1024]{1,0:T(8,128)(2,1)S(1)}, bf16[48,1024]{1,0:T(8,128)(2,1)S(1)}, u32[]{:S(2)}, u32[]{:S(2)}) collective-permute-start(bf16[48,1024]{1,0:T(8,128)(2,1)S(1)} %pad_maximum_fusion.8), channel_id=1, source_target_pairs={{0,64},{4,68},{8,72},{12,76},{16,80},{20,84},{24,88},{28,92},{32,9... | collective-permute-start | bytes 294920 | tf_op jit(solution)/shard_map/ppermute | solution.py:65
  182.5 6.5 %collective-permute-start.25 = (bf16[65,1024]{1,0:T(8,128)(2,1)S(1)}, bf16[65,1024]{1,0:T(8,128)(2,1)S(1)}, u32[]{:S(2)}, u32[]{:S(2)}) collective-permute-start(bf16[65,1024]{1,0:T(8,128)(2,1)S(1)} %get-tuple-element.61), channel_id=1, source_target_pairs={{0,3},{1,0},{2,1},{3,2},{4,7},{5,4},{6,5},{7,6},{8,11},{9,8},{10,9... | collective-permute-start | bytes 399368 | tf_op jit(solution)/shard_map/ppermute | solution.py:65
  192.3 3.4 %collective-permute-done.24 = bf16[65,1024]{1,0:T(8,128)(2,1)S(1)} collective-permute-done((bf16[65,1024]{1,0:T(8,128)(2,1)S(1)}, bf16[65,1024]{1,0:T(8,128)(2,1)S(1)}, u32[]{:S(2)}, u32[]{:S(2)}) %collective-permute-start.24) | collective-permute-done | bytes 133152 | tf_op jit(solution)/shard_map/ppermute | solution.py:65
  196.4 6.4 %convolution_reduce_fusion = f32[65]{0:T(128)S(1)} fusion(bf16[65,4096]{1,0:T(8,128)(2,1)S(1)} %fusion.43, bf16[1024,4096]{1,0:T(8,128)(2,1)} %param.39), kind=kOutput, calls=%fused_computation.65 | convolution fusion | flops 545326016 | bytes 8921348 | tf_op jit(solution)/shard_map/dot_general | solution.py:310
  222.2 3.5 %collective-permute-start.35 = (f32[65]{0:T(128)S(1)}, f32[65]{0:T(128)S(1)}, u32[]{:S(2)}, u32[]{:S(2)}) collective-permute-start(f32[65]{0:T(128)S(1)} %maximum_maximum_fusion), channel_id=1, source_target_pairs={{0,64},{4,68},{8,72},{12,76},{16,80},{20,84},{24,88},{28,92},{32,9... | collective-permute-start | bytes 788 | tf_op jit(solution)/shard_map/ppermute | solution.py:84
  (314 shorter events, 98.2 us)
Async XLA Ops:
  3.9 26.0 %collective-permute-start.2 = (f32[16]{0:T(128)S(1)}, f32[16]{0:T(128)S(1)}, u32[]{:S(2)}, u32[]{:S(2)}) collective-permute-start(f32[16]{0:T(128)S(1)} %slice_reduce_fusion.5), channel_id=1, source_target_pairs={{0,4},{4,8},{8,12},{12,16},{16,20},{20,24},{24,28},{28,32},{32,36}... | collective-permute-start | bytes 200 | tf_op jit(solution)/shard_map/ppermute | solution.py:19
  5.6 24.2 %collective-permute-start.3 = (f32[16]{0:T(128)S(1)}, f32[16]{0:T(128)S(1)}, u32[]{:S(2)}, u32[]{:S(2)}) collective-permute-start(f32[16]{0:T(128)S(1)} %slice_reduce_fusion.5), channel_id=1, source_target_pairs={{0,8},{4,12},{8,16},{12,20},{16,24},{20,28},{24,32},{28,36},{32,40... | collective-permute-start | bytes 200 | tf_op jit(solution)/shard_map/ppermute | solution.py:19
  10.4 24.6 %collective-permute-start = (bf16[3,1024]{1,0:T(4,128)(2,1)S(1)}, bf16[3,1024]{1,0:T(4,128)(2,1)S(1)}, u32[]{:S(2)}, u32[]{:S(2)}) collective-permute-start(bf16[3,1024]{1,0:T(4,128)(2,1)S(1)} %slice.213), channel_id=1, source_target_pairs={{0,4},{4,8},{8,12},{12,16},{16,20},{20,24},{24,28},{28,32},{32,36}... | collective-permute-start | bytes 18440 | tf_op jit(solution)/shard_map/ppermute | solution.py:19
  15.0 18.9 %collective-permute-start.1 = (bf16[3,2,128]{2,0,1:T(4,128)(2,1)S(1)}, bf16[3,2,128]{2,0,1:T(4,128)(2,1)S(1)}, u32[]{:S(2)}, u32[]{:S(2)}) collective-permute-start(bf16[3,2,128]{2,0,1:T(4,128)(2,1)S(1)} %slice.280), channel_id=1, source_target_pairs={{0,4},{4,8},{8,12},{12,16},{16,20},{20,24},{24,28},{28,32},{32,36}... | collective-permute-start | bytes 4616 | tf_op jit(solution)/shard_map/ppermute | solution.py:19
  30.4 13.7 %collective-permute-start.4 = (f32[16]{0:T(128)S(1)}, f32[16]{0:T(128)S(1)}, u32[]{:S(2)}, u32[]{:S(2)}) collective-permute-start(f32[16]{0:T(128)S(1)} %get-tuple-element.39), channel_id=1, source_target_pairs={{0,8},{4,12},{8,16},{12,20},{16,24},{20,28},{24,32},{28,36},{32,40... | collective-permute-start | bytes 200 | tf_op jit(solution)/shard_map/ppermute | solution.py:19
  38.6 17.8 %collective-permute-start.8 = (bf16[16,64,128]{2,1,0:T(8,128)(2,1)S(1)}, bf16[16,64,128]{2,1,0:T(8,128)(2,1)S(1)}, u32[]{:S(2)}, u32[]{:S(2)}) collective-permute-start(bf16[16,64,128]{2,1,0:T(8,128)(2,1)S(1)} %get-tuple-element.107), channel_id=1, source_target_pairs={{0,4},{4,8},{8,12},{12,16},{16,20},{20,24},{24,28},{28,32},{32,36}... | collective-permute-start | bytes 786440 | tf_op jit(solution)/shard_map/ppermute | solution.py:19
  40.4 16.0 %collective-permute-start.7 = (bf16[16,64,128]{2,1,0:T(8,128)(2,1)S(1)}, bf16[16,64,128]{2,1,0:T(8,128)(2,1)S(1)}, u32[]{:S(2)}, u32[]{:S(2)}) collective-permute-start(bf16[16,64,128]{2,1,0:T(8,128)(2,1)S(1)} %get-tuple-element.107), channel_id=1, source_target_pairs={{0,8},{4,12},{8,16},{12,20},{16,24},{20,28},{24,32},{28,36},{32,40... | collective-permute-start | bytes 786440 | tf_op jit(solution)/shard_map/ppermute | solution.py:19
  44.6 6.7 %collective-permute-start.5 = (f32[16]{0:T(128)S(1)}, f32[16]{0:T(128)S(1)}, u32[]{:S(2)}, u32[]{:S(2)}) collective-permute-start(f32[16]{0:T(128)S(1)} %get-tuple-element.37), channel_id=1, source_target_pairs={{0,16},{4,20},{8,24},{12,28},{16,32},{20,36},{24,40},{28,44},{32,4... | collective-permute-start | bytes 200 | tf_op jit(solution)/shard_map/ppermute | solution.py:19
  51.9 8.8 %collective-permute-start.6 = (f32[16]{0:T(128)S(1)}, f32[16]{0:T(128)S(1)}, u32[]{:S(2)}, u32[]{:S(2)}) collective-permute-start(f32[16]{0:T(128)S(1)} %get-tuple-element.35), channel_id=1, source_target_pairs={{0,32},{4,36},{8,40},{12,44},{16,48},{20,52},{24,56},{28,60},{32,6... | collective-permute-start | bytes 200 | tf_op jit(solution)/shard_map/ppermute | solution.py:19
  56.6 9.7 %collective-permute-start.9 = (bf16[16,64,128]{2,1,0:T(8,128)(2,1)S(1)}, bf16[16,64,128]{2,1,0:T(8,128)(2,1)S(1)}, u32[]{:S(2)}, u32[]{:S(2)}) collective-permute-start(bf16[16,64,128]{2,1,0:T(8,128)(2,1)S(1)} %fusion.71), channel_id=1, source_target_pairs={{0,8},{4,12},{8,16},{12,20},{16,24},{20,28},{24,32},{28,36},{32,40... | collective-permute-start | bytes 786440 | tf_op jit(solution)/shard_map/ppermute | solution.py:19
  67.2 9.3 %collective-permute-start.10 = (bf16[16,64,128]{2,1,0:T(8,128)(2,1)S(1)}, bf16[16,64,128]{2,1,0:T(8,128)(2,1)S(1)}, u32[]{:S(2)}, u32[]{:S(2)}) collective-permute-start(bf16[16,64,128]{2,1,0:T(8,128)(2,1)S(1)} %fusion.157), channel_id=1, source_target_pairs={{0,16},{4,20},{8,24},{12,28},{16,32},{20,36},{24,40},{28,44},{32,4... | collective-permute-start | bytes 786440 | tf_op jit(solution)/shard_map/ppermute | solution.py:19
  78.2 13.8 %collective-permute-start.11 = (bf16[16,64,128]{2,1,0:T(8,128)(2,1)}, bf16[16,64,128]{2,1,0:T(8,128)(2,1)}, u32[]{:S(2)}, u32[]{:S(2)}) collective-permute-start(bf16[16,64,128]{2,1,0:T(8,128)(2,1)} %fusion.72), channel_id=1, source_target_pairs={{0,32},{4,36},{8,40},{12,44},{16,48},{20,52},{24,56},{28,60},{32,6... | collective-permute-start | bytes 786440 | tf_op jit(solution)/shard_map/ppermute | solution.py:19
  93.4 7.8 %collective-permute-start.12 = (bf16[16,64,128]{2,1,0:T(8,128)(2,1)S(1)}, bf16[16,64,128]{2,1,0:T(8,128)(2,1)S(1)}, u32[]{:S(2)}, u32[]{:S(2)}) collective-permute-start(bf16[16,64,128]{2,1,0:T(8,128)(2,1)S(1)} %get-tuple-element.32), channel_id=1, source_target_pairs={{0,64},{4,68},{8,72},{12,76},{16,80},{20,84},{24,88},{28,92},{32,9... | collective-permute-start | bytes 786440 | tf_op jit(solution)/shard_map/ppermute | solution.py:19
  111.6 26.5 %collective-permute-start.15 = (bf16[544,1024]{1,0:T(8,128)(2,1)S(1)}, bf16[544,1024]{1,0:T(8,128)(2,1)S(1)}, u32[]{:S(2)}, u32[]{:S(2)}) collective-permute-start(bf16[544,1024]{1,0:T(8,128)(2,1)S(1)} %fusion.25), channel_id=1, source_target_pairs={{0,3},{1,0},{2,1},{3,2},{4,7},{5,4},{6,5},{7,6},{8,11},{9,8},{10,9... | collective-permute-start | bytes 3342344 | tf_op jit(solution)/shard_map/ppermute | solution.py:275
  115.4 28.2 %collective-permute-start.14 = (bf16[544,1024]{1,0:T(8,128)(2,1)S(1)}, bf16[544,1024]{1,0:T(8,128)(2,1)S(1)}, u32[]{:S(2)}, u32[]{:S(2)}) collective-permute-start(bf16[544,1024]{1,0:T(8,128)(2,1)S(1)} %fusion.22), channel_id=1, source_target_pairs={{0,1},{1,2},{2,3},{3,0},{4,5},{5,6},{6,7},{7,4},{8,9},{9,10},{10,1... | collective-permute-start | bytes 3342344 | tf_op jit(solution)/shard_map/ppermute | solution.py:275
  118.4 41.9 %collective-permute-start.13 = (bf16[544,1024]{1,0:T(8,128)(2,1)S(1)}, bf16[544,1024]{1,0:T(8,128)(2,1)S(1)}, u32[]{:S(2)}, u32[]{:S(2)}) collective-permute-start(bf16[544,1024]{1,0:T(8,128)(2,1)S(1)} %fusion.19), channel_id=1, source_target_pairs={{0,2},{1,3},{2,0},{3,1},{4,6},{5,7},{6,4},{7,5},{8,10},{9,11},{10,... | collective-permute-start | bytes 3342344 | tf_op jit(solution)/shard_map/ppermute | solution.py:275
  166.6 5.5 %collective-permute-start.21 = (bf16[12,1024]{1,0:T(8,128)(2,1)S(1)}, bf16[12,1024]{1,0:T(8,128)(2,1)S(1)}, u32[]{:S(2)}, u32[]{:S(2)}) collective-permute-start(bf16[12,1024]{1,0:T(8,128)(2,1)S(1)} %get-tuple-element.67), channel_id=1, source_target_pairs={{0,48},{4,52},{8,56},{12,60},{16,0},{20,4},{24,8},{28,12},{32,16},... | collective-permute-start | bytes 73736 | tf_op jit(solution)/shard_map/ppermute | solution.py:65
  166.7 5.4 %collective-permute-start.20 = (bf16[12,1024]{1,0:T(8,128)(2,1)S(1)}, bf16[12,1024]{1,0:T(8,128)(2,1)S(1)}, u32[]{:S(2)}, u32[]{:S(2)}) collective-permute-start(bf16[12,1024]{1,0:T(8,128)(2,1)S(1)} %get-tuple-element.67), channel_id=1, source_target_pairs={{0,32},{4,36},{8,40},{12,44},{16,48},{20,52},{24,56},{28,60},{32,0... | collective-permute-start | bytes 73736 | tf_op jit(solution)/shard_map/ppermute | solution.py:65
  169.0 6.3 %collective-permute-start.19 = (bf16[12,1024]{1,0:T(8,128)(2,1)S(1)}, bf16[12,1024]{1,0:T(8,128)(2,1)S(1)}, u32[]{:S(2)}, u32[]{:S(2)}) collective-permute-start(bf16[12,1024]{1,0:T(8,128)(2,1)S(1)} %get-tuple-element.67), channel_id=1, source_target_pairs={{0,16},{4,20},{8,24},{12,28},{16,32},{20,36},{24,40},{28,44},{32,4... | collective-permute-start | bytes 73736 | tf_op jit(solution)/shard_map/ppermute | solution.py:65
  175.4 6.7 %collective-permute-start.22 = (bf16[48,1024]{1,0:T(8,128)(2,1)S(1)}, bf16[48,1024]{1,0:T(8,128)(2,1)S(1)}, u32[]{:S(2)}, u32[]{:S(2)}) collective-permute-start(bf16[48,1024]{1,0:T(8,128)(2,1)S(1)} %pad_maximum_fusion.8), channel_id=1, source_target_pairs={{0,64},{4,68},{8,72},{12,76},{16,80},{20,84},{24,88},{28,92},{32,9... | collective-permute-start | bytes 294920 | tf_op jit(solution)/shard_map/ppermute | solution.py:65
  182.5 9.7 %collective-permute-start.25 = (bf16[65,1024]{1,0:T(8,128)(2,1)S(1)}, bf16[65,1024]{1,0:T(8,128)(2,1)S(1)}, u32[]{:S(2)}, u32[]{:S(2)}) collective-permute-start(bf16[65,1024]{1,0:T(8,128)(2,1)S(1)} %get-tuple-element.61), channel_id=1, source_target_pairs={{0,3},{1,0},{2,1},{3,2},{4,7},{5,4},{6,5},{7,6},{8,11},{9,8},{10,9... | collective-permute-start | bytes 399368 | tf_op jit(solution)/shard_map/ppermute | solution.py:65
  189.1 6.6 %collective-permute-start.24 = (bf16[65,1024]{1,0:T(8,128)(2,1)S(1)}, bf16[65,1024]{1,0:T(8,128)(2,1)S(1)}, u32[]{:S(2)}, u32[]{:S(2)}) collective-permute-start(bf16[65,1024]{1,0:T(8,128)(2,1)S(1)} %get-tuple-element.61), channel_id=1, source_target_pairs={{0,2},{1,3},{2,0},{3,1},{4,6},{5,7},{6,4},{7,5},{8,10},{9,11},{10,... | collective-permute-start | bytes 399368 | tf_op jit(solution)/shard_map/ppermute | solution.py:65
  189.1 6.6 %collective-permute-start.23 = (bf16[65,1024]{1,0:T(8,128)(2,1)S(1)}, bf16[65,1024]{1,0:T(8,128)(2,1)S(1)}, u32[]{:S(2)}, u32[]{:S(2)}) collective-permute-start(bf16[65,1024]{1,0:T(8,128)(2,1)S(1)} %get-tuple-element.61), channel_id=1, source_target_pairs={{0,1},{1,2},{2,3},{3,0},{4,5},{5,6},{6,7},{7,4},{8,9},{9,10},{10,1... | collective-permute-start | bytes 399368 | tf_op jit(solution)/shard_map/ppermute | solution.py:65
  216.2 6.0 %collective-permute-start.32 = (f32[65]{0:T(128)S(1)}, f32[65]{0:T(128)S(1)}, u32[]{:S(2)}, u32[]{:S(2)}) collective-permute-start(f32[65]{0:T(128)S(1)} %maximum_maximum_fusion.1), channel_id=1, source_target_pairs={{0,16},{4,20},{8,24},{12,28},{16,32},{20,36},{24,40},{28,44},{32,4... | collective-permute-start | bytes 788 | tf_op jit(solution)/shard_map/ppermute | solution.py:84
  (72 other events, 661.5 us)
